TPU v7x, 512 devices: a whole 4x8x8 slice. The times are simulated.
512 devices in a mesh: pix: 128 (over y, x, z_hi, core), frm: 4 (over z_lo).
Axes of the slice: x: 4, y: 8, z: 8 (z_hi: 2, z_lo: 4; z = z_hi * 4 + z_lo), core: 2. Of those that a mesh axis runs over, the one named last changes fastest.
Arguments:
- video: bfloat16 [245760, 4096], P('pix', 'frm'), may hold values from -6 to 6
- shapes: bfloat16 [245760, 128], P('pix'), may hold values from -1.25 to 1.25
- valid: int32 [245760], P('pix'), may hold values 0 or 1
- omega: float32 [128], replicated, may hold values from 250 to 9000
- damping: float32 [128], replicated, may hold values from 0.3 to 30
- phase: float32 [128], replicated, may hold values from -3.140625 to 3.140625
Outputs:
- shape_grad: bfloat16 [245760, 128], P('pix')
- omega_grad: float32 [128], replicated
- damping_grad: float32 [128], replicated
- phase_grad: float32 [128], replicated
All inputs are finite; a program needn't handle non-finite values. No bound on the sum of `valid` on one device may be relied on, other than what follows from the above.
Results may differ from a plain program's by a relative error of at most 0.012.
Values may be sent and summed in bfloat16 or wider, within the bound.
No kernel may reach another device: no remote copies, remote signals or barrier semaphores. Data moves between devices by JAX's collectives and lax.ppermute only.
A program may use at most 64 MiB of HBM per device.

v0:
```python
import jax
import jax.numpy as jnp
from jax import lax
from jax.sharding import PartitionSpec as P

FRAMES = 4096
IMG_W = 128


def with_halo(cells, sides, width):
    for axis, dim in sides:
        count = lax.axis_size(axis)
        ends = count - 1
        head = lax.slice_in_dim(cells, 0, width, axis=dim)
        tail = lax.slice_in_dim(cells, cells.shape[dim] - width, cells.shape[dim], axis=dim)
        cells = jnp.concatenate(
            [
                lax.ppermute(tail, axis, [(i, (i + 1) % count) for i in range(ends)]),
                cells,
                lax.ppermute(head, axis, [((i + 1) % count, i) for i in range(ends)]),
            ],
            axis=dim,
        )
    return cells


def mode_terms(basis_grad, cosine, sine, times):
    omega_part = jnp.sum(basis_grad * (-times[None, :] * sine), axis=1)
    damping_part = jnp.sum(basis_grad * (-times[None, :] * cosine), axis=1)
    phase_part = jnp.sum(basis_grad * -sine, axis=1)
    return (omega_part, damping_part, phase_part)


def body(video, shapes, valid, omega, damping, phase):
    frames_local = video.shape[1]
    scale = FRAMES ** (-0.5)
    first = lax.axis_index("frm") * frames_local
    times = (first + jnp.arange(frames_local)).astype(jnp.float32) / FRAMES
    envelope = jnp.exp(-damping[:, None] * times[None, :])
    angle_all = omega[:, None] * times[None, :] + phase[:, None]
    cosine = envelope * jnp.cos(angle_all)
    sine = envelope * jnp.sin(angle_all)
    basis = cosine.astype(jnp.bfloat16)
    model = jnp.dot(shapes, basis, preferred_element_type=jnp.float32)
    resid = (valid[:, None].astype(jnp.float32) * (model - video.astype(jnp.float32))).astype(
        jnp.bfloat16
    )
    rows_local = shapes.shape[0] // IMG_W
    grid = shapes.reshape(rows_local, IMG_W, shapes.shape[1])
    padded = with_halo(grid, (("pix", 0),), 1).astype(jnp.float32)
    rows_total = rows_local * lax.axis_size("pix")
    rows_at = lax.axis_index("pix") * rows_local + jnp.arange(rows_local)
    count = ((rows_at > 0).astype(jnp.float32) + (rows_at < rows_total - 1).astype(jnp.float32))[
        :, None, None
    ]
    smooth = 4.0 * (count * grid.astype(jnp.float32) - padded[:-2] - padded[2:])
    smooth_flat = smooth.reshape(shapes.shape)
    data_part = scale * lax.dot_general(
        resid, basis, (((1,), (1,)), ((), ())), preferred_element_type=jnp.float32
    )
    data_grad = lax.psum(data_part, "frm")
    shape_grad = (data_grad + smooth_flat).astype(jnp.bfloat16)
    basis_part = scale * lax.dot_general(
        shapes, resid, (((0,), (0,)), ((), ())), preferred_element_type=jnp.float32
    )
    omega_part, damping_part, phase_part = mode_terms(basis_part, cosine, sine, times)
    omega_grad, damping_grad, phase_grad = lax.psum(
        (omega_part, damping_part, phase_part), ("pix", "frm")
    )
    return (shape_grad, omega_grad, damping_grad, phase_grad)


def solution(mesh):
    placed = (P("pix", "frm"), P("pix", None), P("pix"), P(), P(), P())
    return jax.shard_map(
        body, mesh=mesh, in_specs=placed, out_specs=(P("pix", None), P(), P(), P()), check_vma=False
    )
```

profile of v0, /device:TPU:6, one launch (start us, length us, event | category | flops | bytes accessed | tf_op | source)
XLA Modules:
  0.0 151.2 jit_solution(10240561309438790050)
XLA Ops:
  7.2 0.0 all-reduce.3.cloned.1.call-start
  7.2 0.7 neg.16
  7.9 0.0 copy-start.2
  7.9 0.0 copy-start.1
  7.9 6.4 %copy.10 = bf16[1920,1024]{0,1:T(8,128)(2,1)} copy(bf16[1920,1024]{1,0:T(8,128)(2,1)} %param.6) | data formatting | bytes 7864320 | tf_op args[0]
  14.3 0.0 copy-done.2
  14.3 0.0 copy-done.1
  14.3 0.0 copy-done.3
  14.3 0.0 copy-done.4
  14.3 4.8 %fusion.1 = bf16[1920,1024]{0,1:T(8,128)(2,1)S(1)} fusion(bf16[1920,1024]{0,1:T(8,128)(2,1)} %copy.10, bf16[1920,128]{1,0:T(8,128)(2,1)S(1)} %copy-done.1, f32[1920]{0:T(1024)S(1)} %convert_element_type.46, f32[128]{0:T(128)S(1)} %copy-done.3, f32[128]{0:T(128)S(1)} %copy-done.4, f32[1024]{0:T(1024)S(1)} %convert_multiply_fusion, f32[128]{0:T(128)S(1)} %neg.16), kind=kOutput, calls=%fused_computation.2 | convolution fusion | flops 511836160 | bytes 8369152 | tf_op jit(solution)/shard_map/dot_general | solution.py:44
  19.1 0.0 copy-start
  19.1 1.9 %copy-done = bf16[1920,1024]{0,1:T(8,128)(2,1)} copy-done((bf16[1920,1024]{0,1:T(8,128)(2,1)}, bf16[1920,1024]{0,1:T(8,128)(2,1)S(1)}, u32[]{:S(2)}) %copy-start) | copy-done | bytes 3932184
  21.0 3.6 %convolution_multiply_fusion = f32[1920,128]{1,0:T(8,128)} fusion(bf16[1920,1024]{0,1:T(8,128)(2,1)S(1)} %fusion.1, f32[128]{0:T(128)S(1)} %copy-done.3, f32[128]{0:T(128)S(1)} %copy-done.4, f32[1024]{0:T(1024)S(1)} %convert_multiply_fusion, f32[128]{0:T(128)S(1)} %neg.16), kind=kOutput, calls=%fused_computation.3 | convolution fusion | flops 504217600 | bytes 4920832 | tf_op jit(solution)/shard_map/dot_general | solution.py:58
  24.7 0.0 all-reduce.3.cloned.1.call-update
  24.7 1.9 %collective-permute-start = (bf16[1,128,128]{2,1,0:T(8,128)(2,1)S(1)}, bf16[1,128,128]{2,1,0:T(8,128)(2,1)S(1)}, u32[]{:S(2)}, u32[]{:S(2)}) collective-permute-start(bf16[1,128,128]{2,1,0:T(8,128)(2,1)S(1)} %get-tuple-element.10), channel_id=1, source_target_pairs={{0,4},{4,8},{8,12},{12,16},{16,20},{20,24},{24,28},{28,32},{32,36}... | collective-permute-start | bytes 98312 | tf_op jit(solution)/shard_map/ppermute | solution.py:18
  26.6 10.6 %collective-permute-start.1 = (bf16[1,128,128]{2,1,0:T(8,128)(2,1)S(1)}, bf16[1,128,128]{2,1,0:T(8,128)(2,1)S(1)}, u32[]{:S(2)}, u32[]{:S(2)}) collective-permute-start(bf16[1,128,128]{2,1,0:T(8,128)(2,1)S(1)} %get-tuple-element.11), channel_id=1, source_target_pairs={{4,0},{8,4},{12,8},{16,12},{20,16},{24,20},{28,24},{32,28},{36,32}... | collective-permute-start | bytes 98312 | tf_op jit(solution)/shard_map/ppermute | solution.py:20
  37.3 4.9 %multiply_reduce_fusion.1 = (f32[128]{0:T(128)S(1)}, f32[128]{0:T(128)S(1)}, f32[128]{0:T(128)S(1)}) fusion(f32[1024]{0:T(1024)S(1)} %fusion.8, f32[128]{0:T(128)S(1)} %copy-done.3, f32[128]{0:T(128)S(1)} %copy-done.4, f32[1024]{0:T(1024)S(1)} %convert_multiply_fusion, f32[128]{0:T(128)S(1)} %neg.16, bf16[1920,1024]{0,1:T(8,128)(2,1)} %copy-done, ...), kind=kOutput, calls=%fused_computation.13 | convolution fusion | flops 505282176 | bytes 4434944 | tf_op jit(solution)/shard_map/dot_general | solution.py:63
  42.1 99.8 %all-reduce = (f32[128]{0:T(128)}, f32[128]{0:T(128)}, f32[128]{0:T(128)}) all-reduce(f32[128]{0:T(128)S(1)} %get-tuple-element.5, f32[128]{0:T(128)S(1)} %get-tuple-element.4, f32[128]{0:T(128)S(1)} %get-tuple-element.6), channel_id=1, replica_groups=mesh['pix'=128,'frm'=4] {'pix','frm'}, use_global_device_ids=true, to_apply=%region_2.0 | all-reduce | flops 384 | bytes 3072 | tf_op jit(solution)/shard_map/psum | solution.py:67
  141.9 0.0 collective-permute-done
  141.9 0.0 collective-permute-done.1
  141.9 0.1 maximum_convert_fusion
  142.0 0.2 fusion.3
  142.3 0.0 all-reduce.3.cloned.1.call-done
  142.3 2.1 %fusion.4 = bf16[1920,128]{1,0:T(8,128)(2,1)} fusion(f32[1920,128]{1,0:T(8,128)} %all-reduce.3.cloned.1.call-done, f32[15,128,128]{2,1,0:T(8,128)S(1)} %fusion.3), kind=kLoop, calls=%fused_computation.10 | loop fusion | flops 491520 | bytes 2457600 | tf_op jit(solution)/shard_map/convert_element_type | solution.py:62
  (7 shorter events, 0.0 us)
Async XLA Ops:
  7.2 135.1 %all-reduce.3.cloned.1.call-start = ((), (), s32[]{:S(2)}) async-start(), calls=%async_computation | async-start | bytes 1966080 | tf_op jit(solution)/shard_map/psum | solution.py:61
  7.9 6.4 %copy-start.2 = (s32[1920]{0:T(1024)S(1)}, s32[1920]{0:T(1024)}, u32[]{:S(2)}) copy-start(s32[1920]{0:T(1024)} %param.8) | copy-start | bytes 23044
  7.9 6.4 %copy-start.1 = (bf16[1920,128]{1,0:T(8,128)(2,1)S(1)}, bf16[1920,128]{1,0:T(8,128)(2,1)}, u32[]{:S(2)}) copy-start(bf16[1920,128]{1,0:T(8,128)(2,1)} %param.7) | copy-start | bytes 1474564
  7.9 6.4 %copy-start.3 = (f32[128]{0:T(128)S(1)}, f32[128]{0:T(128)}, u32[]{:S(2)}) copy-start(f32[128]{0:T(128)} %param.11) | copy-start | bytes 1540
  7.9 6.4 %copy-start.4 = (f32[128]{0:T(128)S(1)}, f32[128]{0:T(128)}, u32[]{:S(2)}) copy-start(f32[128]{0:T(128)} %param.9) | copy-start | bytes 1540
  19.1 1.9 %copy-start = (bf16[1920,1024]{0,1:T(8,128)(2,1)}, bf16[1920,1024]{0,1:T(8,128)(2,1)S(1)}, u32[]{:S(2)}) copy-start(bf16[1920,1024]{0,1:T(8,128)(2,1)S(1)} %fusion.1) | copy-start | bytes 11796484
  24.7 117.2 %collective-permute-start = (bf16[1,128,128]{2,1,0:T(8,128)(2,1)S(1)}, bf16[1,128,128]{2,1,0:T(8,128)(2,1)S(1)}, u32[]{:S(2)}, u32[]{:S(2)}) collective-permute-start(bf16[1,128,128]{2,1,0:T(8,128)(2,1)S(1)} %get-tuple-element.10), channel_id=1, source_target_pairs={{0,4},{4,8},{8,12},{12,16},{16,20},{20,24},{24,28},{28,32},{32,36}... | collective-permute-start | bytes 98312 | tf_op jit(solution)/shard_map/ppermute | solution.py:18
  26.6 115.3 %collective-permute-start.1 = (bf16[1,128,128]{2,1,0:T(8,128)(2,1)S(1)}, bf16[1,128,128]{2,1,0:T(8,128)(2,1)S(1)}, u32[]{:S(2)}, u32[]{:S(2)}) collective-permute-start(bf16[1,128,128]{2,1,0:T(8,128)(2,1)S(1)} %get-tuple-element.11), channel_id=1, source_target_pairs={{4,0},{8,4},{12,8},{16,12},{20,16},{24,20},{28,24},{32,28},{36,32}... | collective-permute-start | bytes 98312 | tf_op jit(solution)/shard_map/ppermute | solution.py:20
Sparse Core Ops, SparseCore 0:
  24.8 73.2 all-reduce.2
where the time goes:
time: 154 us; the launch traced here: 151 us
  blocking collectives  99.8 us (65%)
  between operations  14.2 us (9%)
  matrix products  13.3 us (9%)
  starting transfers between devices  12.6 us (8%)
  local copies, waits for them, and re-layouts  8.31 us (5%)
  other arithmetic  3.09 us (2%)
    psum x1, blocking collectives, body(): lax.psum((omega_part, damping_part, phase_part), ('pix', 'frm'))  99.8 us
    ppermute x1, starting transfers between devices, with_halo(): lax.ppermute(head, axis, [((i + 1) % count, i) for i in range(ends)])  10.6 us
    unnamed x11, local copies, waits for them, and re-layouts  8.3 us
    dot_general x1, matrix products, body(): lax.dot_general(shapes, resid, (((0,), (0,)), ((), ())), preferred_elemen...  4.85 us
    dot_general x1, matrix products, body(): model = jnp.dot(shapes, basis, preferred_element_type=jnp.float32)  4.77 us
    dot_general x1, matrix products, body(): lax.dot_general(resid, basis, (((1,), (1,)), ((), ())), preferred_element...  3.64 us
  transfers between devices with their start and end apart: 3, of which 0 were waited for; matrix products, arithmetic and copies ran while one was open for 3% of the time, Pallas kernels for 0%

commit v1 on v0

v1 whole, which is shorter than its diff:
```python
import jax
import jax.numpy as jnp
from jax import lax
from jax.sharding import PartitionSpec as P

FRAMES = 4096
IMG_W = 128


def with_halo(cells, sides, width):
    for axis, dim in sides:
        count = lax.axis_size(axis)
        ends = count - 1
        head = lax.slice_in_dim(cells, 0, width, axis=dim)
        tail = lax.slice_in_dim(cells, cells.shape[dim] - width, cells.shape[dim], axis=dim)
        cells = jnp.concatenate(
            [
                lax.ppermute(tail, axis, [(i, (i + 1) % count) for i in range(ends)]),
                cells,
                lax.ppermute(head, axis, [((i + 1) % count, i) for i in range(ends)]),
            ],
            axis=dim,
        )
    return cells


def mode_terms(basis_grad, cosine, sine, times):
    omega_part = jnp.sum(basis_grad * (-times[None, :] * sine), axis=1)
    damping_part = jnp.sum(basis_grad * (-times[None, :] * cosine), axis=1)
    phase_part = jnp.sum(basis_grad * -sine, axis=1)
    return jnp.stack([omega_part, damping_part, phase_part])


def butterfly(x, axis):
    count = lax.axis_size(axis)
    bit = 1
    while bit < count:
        x = x + lax.ppermute(x, axis, [(i, i ^ bit) for i in range(count)])
        bit *= 2
    return x


def split_f32(x):
    top = lax.reduce_precision(x, exponent_bits=8, mantissa_bits=7)
    return top.astype(jnp.bfloat16), (x - top).astype(jnp.bfloat16)


def body(video, shapes, valid, omega, damping, phase):
    frames_local = video.shape[1]
    scale = FRAMES ** (-0.5)
    n_frm = lax.axis_size("frm")
    me = lax.axis_index("frm")
    first = me * frames_local
    times = (first + jnp.arange(frames_local)).astype(jnp.float32) / FRAMES
    envelope = jnp.exp(-damping[:, None] * times[None, :])
    angle_all = omega[:, None] * times[None, :] + phase[:, None]
    cosine = envelope * jnp.cos(angle_all)
    sine = envelope * jnp.sin(angle_all)
    basis = cosine.astype(jnp.bfloat16)

    rows_local = shapes.shape[0] // IMG_W
    grid = shapes.reshape(rows_local, IMG_W, shapes.shape[1])
    padded = with_halo(grid, (("pix", 0),), 1).astype(jnp.float32)

    model = jnp.dot(shapes, basis, preferred_element_type=jnp.float32)
    resid = (valid[:, None].astype(jnp.float32) * (model - video.astype(jnp.float32))).astype(
        jnp.bfloat16
    )
    basis_part = scale * lax.dot_general(
        shapes, resid, (((0,), (0,)), ((), ())), preferred_element_type=jnp.float32
    )
    terms = butterfly(mode_terms(basis_part, cosine, sine, times), "pix")

    data_part = scale * lax.dot_general(
        resid, basis, (((1,), (1,)), ((), ())), preferred_element_type=jnp.float32
    )
    n_pixels, n_modes = data_part.shape
    quarter = n_pixels // n_frm
    parts = data_part.reshape(n_frm, quarter, n_modes)
    acc = jnp.take(parts, me, axis=0)
    for s in range(1, n_frm):
        send = jnp.take(parts, (me + s) % n_frm, axis=0)
        acc = acc + lax.ppermute(send, "frm", [(i, (i + s) % n_frm) for i in range(n_frm)])

    rows_total = rows_local * lax.axis_size("pix")
    rows_at = lax.axis_index("pix") * rows_local + jnp.arange(rows_local)
    count = ((rows_at > 0).astype(jnp.float32) + (rows_at < rows_total - 1).astype(jnp.float32))[
        :, None, None
    ]
    smooth = 4.0 * (count * grid.astype(jnp.float32) - padded[:-2] - padded[2:])
    smooth_parts = smooth.reshape(n_frm, quarter, n_modes)
    own = (acc + jnp.take(smooth_parts, me, axis=0)).astype(jnp.bfloat16)

    hi, lo = split_f32(terms)
    extra = 16 - (quarter + 2 * terms.shape[0]) % 16
    packet = jnp.concatenate(
        [own, hi, lo, jnp.zeros((extra % 16, n_modes), jnp.bfloat16)], axis=0
    )
    got = [packet]
    for s in range(1, n_frm):
        got.append(lax.ppermute(packet, "frm", [(i, (i + s) % n_frm) for i in range(n_frm)]))
    stacked = jnp.stack(got)
    ordered = jnp.take(stacked, (me - jnp.arange(n_frm)) % n_frm, axis=0)
    shape_grad = ordered[:, :quarter].reshape(n_pixels, n_modes)
    k = terms.shape[0]
    hi_all = ordered[:, quarter : quarter + k].astype(jnp.float32)
    lo_all = ordered[:, quarter + k : quarter + 2 * k].astype(jnp.float32)
    pieces = hi_all + lo_all
    total = pieces[0]
    for f in range(1, n_frm):
        total = total + pieces[f]
    return (shape_grad, total[0], total[1], total[2])


def solution(mesh):
    placed = (P("pix", "frm"), P("pix", None), P("pix"), P(), P(), P())
    return jax.shard_map(
        body, mesh=mesh, in_specs=placed, out_specs=(P("pix", None), P(), P(), P()), check_vma=False
    )
```

time: 154 us -> 109 us (0.71)
  the two profiles are of different devices: /device:TPU:6 before, /device:TPU:32 now
where the time goes in v1:
time: 109 us; the launch traced here: 108 us
  starting transfers between devices  54 us (50%)
  waiting for transfers between devices  32.1 us (29%)
  matrix products  11 us (10%)
  local copies, waits for them, and re-layouts  8.31 us (8%)
  other arithmetic  1.71 us (2%)
    ppermute x7, starting transfers between devices, butterfly(): x = x + lax.ppermute(x, axis, [(i, i ^ bit) for i in range(count)])  29.8 us
    ppermute x7, waiting for transfers between devices, butterfly(): x = x + lax.ppermute(x, axis, [(i, i ^ bit) for i in range(count)])  14.4 us
    ppermute x1, waiting for transfers between devices, with_halo(): lax.ppermute(tail, axis, [(i, (i + 1) % count) for i in range(ends)])  11.5 us
    ppermute x3, starting transfers between devices, body(): lax.ppermute(send, 'frm', [(i, (i + s) % n_frm) for i in range(n_frm)])  10.1 us
    ppermute x3, starting transfers between devices, body(): lax.ppermute(packet, 'frm', [(i, (i + s) % n_frm) for i in range(n_frm)])  9.84 us
    unnamed x9, local copies, waits for them, and re-layouts  6.24 us
    ppermute x3, waiting for transfers between devices, body(): lax.ppermute(packet, 'frm', [(i, (i + s) % n_frm) for i in range(n_frm)])  6.18 us
    dot_general x1, matrix products, body(): model = jnp.dot(shapes, basis, preferred_element_type=jnp.float32)  4.77 us
  transfers between devices with their start and end apart: 15, of which 7 were waited for; matrix products, arithmetic and copies ran while one was open for 3% of the time, Pallas kernels for 0%

profile of v1, /device:TPU:32, one launch (start us, length us, event | category | flops | bytes accessed | tf_op | source)
XLA Modules:
  0.0 108.2 jit_solution(6856392724894461233)
XLA Ops:
  1.3 6.2 %copy.10 = bf16[1920,1024]{0,1:T(8,128)(2,1)} copy(bf16[1920,1024]{1,0:T(8,128)(2,1)} %param.8) | data formatting | bytes 7864320 | tf_op args[0]
  7.6 4.8 %fusion.1 = bf16[1920,1024]{0,1:T(8,128)(2,1)S(1)} fusion(bf16[1920,1024]{0,1:T(8,128)(2,1)} %copy.10, bf16[1920,128]{1,0:T(8,128)(2,1)S(1)} %copy-done, f32[1920]{0:T(1024)S(1)} %convert_element_type.58, f32[128]{0:T(128)S(1)} %copy-done.2, f32[128]{0:T(128)S(1)} %copy-done.3, f32[1024]{0:T(1024)S(1)} %get-tuple-element.29, f32[128]{0:T(128)S(1)} %neg.16), kind=kOutput, calls=%fused_computation.3 | convolution fusion | flops 511836160 | bytes 8369152 | tf_op jit(solution)/shard_map/dot_general | solution.py:65
  12.4 3.6 %multiply_reduce_fusion.2 = (f32[128]{0:T(128)S(1)}, f32[128]{0:T(128)S(1)}, f32[128]{0:T(128)S(1)}) fusion(f32[1024]{0:T(1024)S(1)} %get-tuple-element.30, f32[128]{0:T(128)S(1)} %copy-done.2, f32[128]{0:T(128)S(1)} %copy-done.3, f32[1024]{0:T(1024)S(1)} %get-tuple-element.29, f32[128]{0:T(128)S(1)} %neg.16, bf16[1920,1024]{0,1:T(8,128)(2,1)S(1)} %fusion.1, ...), kind=kOutput, calls=%fused_computation.13 | convolution fusion | flops 505282176 | bytes 4434944 | tf_op jit(solution)/shard_map/dot_general | solution.py:69
  16.0 1.9 %collective-permute-start.5 = (f32[3,128]{1,0:T(4,128)S(1)}, f32[3,128]{1,0:T(4,128)S(1)}, u32[]{:S(2)}, u32[]{:S(2)}) collective-permute-start(f32[3,128]{1,0:T(4,128)S(1)} %pad_maximum_fusion.1), channel_id=1, source_target_pairs={{0,4},{4,0},{8,12},{12,8},{16,20},{20,16},{24,28},{28,24},{32,36},... | collective-permute-start | bytes 4616 | tf_op jit(solution)/shard_map/ppermute | solution.py:38
  17.9 2.7 %convolution_multiply_fusion = f32[1920,128]{1,0:T(8,128)S(1)} fusion(bf16[1920,1024]{0,1:T(8,128)(2,1)S(1)} %fusion.1, f32[128]{0:T(128)S(1)} %copy-done.2, f32[128]{0:T(128)S(1)} %copy-done.3, f32[1024]{0:T(1024)S(1)} %get-tuple-element.29, f32[128]{0:T(128)S(1)} %neg.16), kind=kOutput, calls=%fused_computation.4 | convolution fusion | flops 504217600 | bytes 4920832 | tf_op jit(solution)/shard_map/dot_general | solution.py:74
  20.6 10.9 %collective-permute-start.6 = (f32[3,128]{1,0:T(4,128)S(1)}, f32[3,128]{1,0:T(4,128)S(1)}, u32[]{:S(2)}, u32[]{:S(2)}) collective-permute-start(f32[3,128]{1,0:T(4,128)S(1)} %fusion.16), channel_id=1, source_target_pairs={{0,8},{4,12},{8,0},{12,4},{16,24},{20,28},{24,16},{28,20},{32,40},... | collective-permute-start | bytes 4616 | tf_op jit(solution)/shard_map/ppermute | solution.py:38
  31.6 5.2 %collective-permute-start.2 = (f32[480,128]{1,0:T(8,128)S(1)}, f32[480,128]{1,0:T(8,128)S(1)}, u32[]{:S(2)}, u32[]{:S(2)}) collective-permute-start(f32[480,128]{1,0:T(8,128)S(1)} %get-tuple-element.20), channel_id=1, source_target_pairs={{0,3},{1,0},{2,1},{3,2},{4,7},{5,4},{6,5},{7,6},{8,11},{9,8},{10,9... | collective-permute-start | bytes 737288 | tf_op jit(solution)/shard_map/ppermute | solution.py:83
  36.9 1.9 %collective-permute-start.1 = (f32[480,128]{1,0:T(8,128)S(1)}, f32[480,128]{1,0:T(8,128)S(1)}, u32[]{:S(2)}, u32[]{:S(2)}) collective-permute-start(f32[480,128]{1,0:T(8,128)S(1)} %get-tuple-element.21), channel_id=1, source_target_pairs={{0,2},{1,3},{2,0},{3,1},{4,6},{5,7},{6,4},{7,5},{8,10},{9,11},{10,... | collective-permute-start | bytes 737288 | tf_op jit(solution)/shard_map/ppermute | solution.py:83
  38.8 3.0 %collective-permute-start = (f32[480,128]{1,0:T(8,128)S(1)}, f32[480,128]{1,0:T(8,128)S(1)}, u32[]{:S(2)}, u32[]{:S(2)}) collective-permute-start(f32[480,128]{1,0:T(8,128)S(1)} %get-tuple-element.19), channel_id=1, source_target_pairs={{0,1},{1,2},{2,3},{3,0},{4,5},{5,6},{6,7},{7,4},{8,9},{9,10},{10,1... | collective-permute-start | bytes 737288 | tf_op jit(solution)/shard_map/ppermute | solution.py:83
  41.8 3.4 %collective-permute-start.7 = (f32[3,128]{1,0:T(4,128)S(1)}, f32[3,128]{1,0:T(4,128)S(1)}, u32[]{:S(2)}, u32[]{:S(2)}) collective-permute-start(f32[3,128]{1,0:T(4,128)S(1)} %fusion.22), channel_id=1, source_target_pairs={{0,16},{4,20},{8,24},{12,28},{16,0},{20,4},{24,8},{28,12},{32,48},... | collective-permute-start | bytes 4616 | tf_op jit(solution)/shard_map/ppermute | solution.py:38
  45.2 2.3 %collective-permute-start.4 = (bf16[1,128,128]{2,1,0:T(8,128)(2,1)S(1)}, bf16[1,128,128]{2,1,0:T(8,128)(2,1)S(1)}, u32[]{:S(2)}, u32[]{:S(2)}) collective-permute-start(bf16[1,128,128]{2,1,0:T(8,128)(2,1)S(1)} %get-tuple-element.23), channel_id=1, source_target_pairs={{4,0},{8,4},{12,8},{16,12},{20,16},{24,20},{28,24},{32,28},{36,32}... | collective-permute-start | bytes 98312 | tf_op jit(solution)/shard_map/ppermute | solution.py:20
  47.6 4.6 %collective-permute-start.8 = (f32[3,128]{1,0:T(4,128)S(1)}, f32[3,128]{1,0:T(4,128)S(1)}, u32[]{:S(2)}, u32[]{:S(2)}) collective-permute-start(f32[3,128]{1,0:T(4,128)S(1)} %add.161), channel_id=1, source_target_pairs={{0,32},{4,36},{8,40},{12,44},{16,48},{20,52},{24,56},{28,60},{32,0... | collective-permute-start | bytes 4616 | tf_op jit(solution)/shard_map/ppermute | solution.py:38
  52.2 2.3 %collective-permute-done.8 = f32[3,128]{1,0:T(4,128)S(1)} collective-permute-done((f32[3,128]{1,0:T(4,128)S(1)}, f32[3,128]{1,0:T(4,128)S(1)}, u32[]{:S(2)}, u32[]{:S(2)}) %collective-permute-start.8) | collective-permute-done | bytes 1568 | tf_op jit(solution)/shard_map/ppermute | solution.py:38
  54.6 3.5 %collective-permute-start.9 = (f32[3,128]{1,0:T(4,128)S(1)}, f32[3,128]{1,0:T(4,128)S(1)}, u32[]{:S(2)}, u32[]{:S(2)}) collective-permute-start(f32[3,128]{1,0:T(4,128)S(1)} %add.162), channel_id=1, source_target_pairs={{0,64},{4,68},{8,72},{12,76},{16,80},{20,84},{24,88},{28,92},{32,9... | collective-permute-start | bytes 4616 | tf_op jit(solution)/shard_map/ppermute | solution.py:38
  58.1 2.0 %collective-permute-done.9 = f32[3,128]{1,0:T(4,128)S(1)} collective-permute-done((f32[3,128]{1,0:T(4,128)S(1)}, f32[3,128]{1,0:T(4,128)S(1)}, u32[]{:S(2)}, u32[]{:S(2)}) %collective-permute-start.9) | collective-permute-done | bytes 1568 | tf_op jit(solution)/shard_map/ppermute | solution.py:38
  60.1 3.6 %collective-permute-start.10 = (f32[3,128]{1,0:T(4,128)S(1)}, f32[3,128]{1,0:T(4,128)S(1)}, u32[]{:S(2)}, u32[]{:S(2)}) collective-permute-start(f32[3,128]{1,0:T(4,128)S(1)} %add.163), channel_id=1, source_target_pairs={{0,128},{4,132},{8,136},{12,140},{16,144},{20,148},{24,152},{28,15... | collective-permute-start | bytes 4616 | tf_op jit(solution)/shard_map/ppermute | solution.py:38
  63.7 2.7 %collective-permute-done.10 = f32[3,128]{1,0:T(4,128)S(1)} collective-permute-done((f32[3,128]{1,0:T(4,128)S(1)}, f32[3,128]{1,0:T(4,128)S(1)}, u32[]{:S(2)}, u32[]{:S(2)}) %collective-permute-start.10) | collective-permute-done | bytes 1568 | tf_op jit(solution)/shard_map/ppermute | solution.py:38
  68.5 7.3 %collective-permute-done.11 = f32[3,128]{1,0:T(4,128)S(1)} collective-permute-done((f32[3,128]{1,0:T(4,128)S(1)}, f32[3,128]{1,0:T(4,128)S(1)}, u32[]{:S(2)}, u32[]{:S(2)}) %collective-permute-start.11) | collective-permute-done | bytes 1568 | tf_op jit(solution)/shard_map/ppermute | solution.py:38
  77.7 11.5 %collective-permute-done.3 = bf16[1,128,128]{2,1,0:T(8,128)(2,1)S(1)} collective-permute-done((bf16[1,128,128]{2,1,0:T(8,128)(2,1)S(1)}, bf16[1,128,128]{2,1,0:T(8,128)(2,1)S(1)}, u32[]{:S(2)}, u32[]{:S(2)}) %collective-permute-start.3) | collective-permute-done | bytes 32800 | tf_op jit(solution)/shard_map/ppermute | solution.py:18
  89.8 4.8 %collective-permute-start.14 = (bf16[496,128]{1,0:T(8,128)(2,1)S(1)}, bf16[496,128]{1,0:T(8,128)(2,1)S(1)}, u32[]{:S(2)}, u32[]{:S(2)}) collective-permute-start(bf16[496,128]{1,0:T(8,128)(2,1)S(1)} %maximum_maximum_fusion), channel_id=1, source_target_pairs={{0,3},{1,0},{2,1},{3,2},{4,7},{5,4},{6,5},{7,6},{8,11},{9,8},{10,9... | collective-permute-start | bytes 380936 | tf_op jit(solution)/shard_map/ppermute | solution.py:101
  94.7 2.7 %collective-permute-start.13 = (bf16[496,128]{1,0:T(8,128)(2,1)S(1)}, bf16[496,128]{1,0:T(8,128)(2,1)S(1)}, u32[]{:S(2)}, u32[]{:S(2)}) collective-permute-start(bf16[496,128]{1,0:T(8,128)(2,1)S(1)} %maximum_maximum_fusion), channel_id=1, source_target_pairs={{0,2},{1,3},{2,0},{3,1},{4,6},{5,7},{6,4},{7,5},{8,10},{9,11},{10,... | collective-permute-start | bytes 380936 | tf_op jit(solution)/shard_map/ppermute | solution.py:101
  97.4 2.3 %collective-permute-start.12 = (bf16[496,128]{1,0:T(8,128)(2,1)S(1)}, bf16[496,128]{1,0:T(8,128)(2,1)S(1)}, u32[]{:S(2)}, u32[]{:S(2)}) collective-permute-start(bf16[496,128]{1,0:T(8,128)(2,1)S(1)} %maximum_maximum_fusion), channel_id=1, source_target_pairs={{0,1},{1,2},{2,3},{3,0},{4,5},{5,6},{6,7},{7,4},{8,9},{9,10},{10,1... | collective-permute-start | bytes 380936 | tf_op jit(solution)/shard_map/ppermute | solution.py:101
  99.9 2.7 %collective-permute-done.13 = bf16[496,128]{1,0:T(8,128)(2,1)S(1)} collective-permute-done((bf16[496,128]{1,0:T(8,128)(2,1)S(1)}, bf16[496,128]{1,0:T(8,128)(2,1)S(1)}, u32[]{:S(2)}, u32[]{:S(2)}) %collective-permute-start.13) | collective-permute-done | bytes 127008 | tf_op jit(solution)/shard_map/ppermute | solution.py:101
  102.6 3.5 %collective-permute-done.12 = bf16[496,128]{1,0:T(8,128)(2,1)S(1)} collective-permute-done((bf16[496,128]{1,0:T(8,128)(2,1)S(1)}, bf16[496,128]{1,0:T(8,128)(2,1)S(1)}, u32[]{:S(2)}, u32[]{:S(2)}) %collective-permute-start.12) | collective-permute-done | bytes 127008 | tf_op jit(solution)/shard_map/ppermute | solution.py:101
  (49 shorter events, 7.6 us)
Async XLA Ops:
  1.3 6.2 %copy-start.1 = (s32[1920]{0:T(1024)S(1)}, s32[1920]{0:T(1024)}, u32[]{:S(2)}) copy-start(s32[1920]{0:T(1024)} %param.10) | copy-start | bytes 23044
  1.3 6.2 %copy-start = (bf16[1920,128]{1,0:T(8,128)(2,1)S(1)}, bf16[1920,128]{1,0:T(8,128)(2,1)}, u32[]{:S(2)}) copy-start(bf16[1920,128]{1,0:T(8,128)(2,1)} %param.9) | copy-start | bytes 1474564
  1.3 6.2 %copy-start.2 = (f32[128]{0:T(128)S(1)}, f32[128]{0:T(128)}, u32[]{:S(2)}) copy-start(f32[128]{0:T(128)} %param.13) | copy-start | bytes 1540
  1.3 6.3 %copy-start.3 = (f32[128]{0:T(128)S(1)}, f32[128]{0:T(128)}, u32[]{:S(2)}) copy-start(f32[128]{0:T(128)} %param.11) | copy-start | bytes 1540
  16.0 4.6 %collective-permute-start.5 = (f32[3,128]{1,0:T(4,128)S(1)}, f32[3,128]{1,0:T(4,128)S(1)}, u32[]{:S(2)}, u32[]{:S(2)}) collective-permute-start(f32[3,128]{1,0:T(4,128)S(1)} %pad_maximum_fusion.1), channel_id=1, source_target_pairs={{0,4},{4,0},{8,12},{12,8},{16,20},{20,16},{24,28},{28,24},{32,36},... | collective-permute-start | bytes 4616 | tf_op jit(solution)/shard_map/ppermute | solution.py:38
  20.6 21.2 %collective-permute-start.6 = (f32[3,128]{1,0:T(4,128)S(1)}, f32[3,128]{1,0:T(4,128)S(1)}, u32[]{:S(2)}, u32[]{:S(2)}) collective-permute-start(f32[3,128]{1,0:T(4,128)S(1)} %fusion.16), channel_id=1, source_target_pairs={{0,8},{4,12},{8,0},{12,4},{16,24},{20,28},{24,16},{28,20},{32,40},... | collective-permute-start | bytes 4616 | tf_op jit(solution)/shard_map/ppermute | solution.py:38
  31.6 57.9 %collective-permute-start.2 = (f32[480,128]{1,0:T(8,128)S(1)}, f32[480,128]{1,0:T(8,128)S(1)}, u32[]{:S(2)}, u32[]{:S(2)}) collective-permute-start(f32[480,128]{1,0:T(8,128)S(1)} %get-tuple-element.20), channel_id=1, source_target_pairs={{0,3},{1,0},{2,1},{3,2},{4,7},{5,4},{6,5},{7,6},{8,11},{9,8},{10,9... | collective-permute-start | bytes 737288 | tf_op jit(solution)/shard_map/ppermute | solution.py:83
  36.9 52.7 %collective-permute-start.1 = (f32[480,128]{1,0:T(8,128)S(1)}, f32[480,128]{1,0:T(8,128)S(1)}, u32[]{:S(2)}, u32[]{:S(2)}) collective-permute-start(f32[480,128]{1,0:T(8,128)S(1)} %get-tuple-element.21), channel_id=1, source_target_pairs={{0,2},{1,3},{2,0},{3,1},{4,6},{5,7},{6,4},{7,5},{8,10},{9,11},{10,... | collective-permute-start | bytes 737288 | tf_op jit(solution)/shard_map/ppermute | solution.py:83
  38.8 50.8 %collective-permute-start = (f32[480,128]{1,0:T(8,128)S(1)}, f32[480,128]{1,0:T(8,128)S(1)}, u32[]{:S(2)}, u32[]{:S(2)}) collective-permute-start(f32[480,128]{1,0:T(8,128)S(1)} %get-tuple-element.19), channel_id=1, source_target_pairs={{0,1},{1,2},{2,3},{3,0},{4,5},{5,6},{6,7},{7,4},{8,9},{9,10},{10,1... | collective-permute-start | bytes 737288 | tf_op jit(solution)/shard_map/ppermute | solution.py:83
  41.8 5.8 %collective-permute-start.7 = (f32[3,128]{1,0:T(4,128)S(1)}, f32[3,128]{1,0:T(4,128)S(1)}, u32[]{:S(2)}, u32[]{:S(2)}) collective-permute-start(f32[3,128]{1,0:T(4,128)S(1)} %fusion.22), channel_id=1, source_target_pairs={{0,16},{4,20},{8,24},{12,28},{16,0},{20,4},{24,8},{28,12},{32,48},... | collective-permute-start | bytes 4616 | tf_op jit(solution)/shard_map/ppermute | solution.py:38
  45.2 32.5 %collective-permute-start.4 = (bf16[1,128,128]{2,1,0:T(8,128)(2,1)S(1)}, bf16[1,128,128]{2,1,0:T(8,128)(2,1)S(1)}, u32[]{:S(2)}, u32[]{:S(2)}) collective-permute-start(bf16[1,128,128]{2,1,0:T(8,128)(2,1)S(1)} %get-tuple-element.23), channel_id=1, source_target_pairs={{4,0},{8,4},{12,8},{16,12},{20,16},{24,20},{28,24},{32,28},{36,32}... | collective-permute-start | bytes 98312 | tf_op jit(solution)/shard_map/ppermute | solution.py:20
  47.6 7.0 %collective-permute-start.8 = (f32[3,128]{1,0:T(4,128)S(1)}, f32[3,128]{1,0:T(4,128)S(1)}, u32[]{:S(2)}, u32[]{:S(2)}) collective-permute-start(f32[3,128]{1,0:T(4,128)S(1)} %add.161), channel_id=1, source_target_pairs={{0,32},{4,36},{8,40},{12,44},{16,48},{20,52},{24,56},{28,60},{32,0... | collective-permute-start | bytes 4616 | tf_op jit(solution)/shard_map/ppermute | solution.py:38
  54.6 5.5 %collective-permute-start.9 = (f32[3,128]{1,0:T(4,128)S(1)}, f32[3,128]{1,0:T(4,128)S(1)}, u32[]{:S(2)}, u32[]{:S(2)}) collective-permute-start(f32[3,128]{1,0:T(4,128)S(1)} %add.162), channel_id=1, source_target_pairs={{0,64},{4,68},{8,72},{12,76},{16,80},{20,84},{24,88},{28,92},{32,9... | collective-permute-start | bytes 4616 | tf_op jit(solution)/shard_map/ppermute | solution.py:38
  60.1 6.4 %collective-permute-start.10 = (f32[3,128]{1,0:T(4,128)S(1)}, f32[3,128]{1,0:T(4,128)S(1)}, u32[]{:S(2)}, u32[]{:S(2)}) collective-permute-start(f32[3,128]{1,0:T(4,128)S(1)} %add.163), channel_id=1, source_target_pairs={{0,128},{4,132},{8,136},{12,140},{16,144},{20,148},{24,152},{28,15... | collective-permute-start | bytes 4616 | tf_op jit(solution)/shard_map/ppermute | solution.py:38
  66.4 9.4 %collective-permute-start.11 = (f32[3,128]{1,0:T(4,128)S(1)}, f32[3,128]{1,0:T(4,128)S(1)}, u32[]{:S(2)}, u32[]{:S(2)}) collective-permute-start(f32[3,128]{1,0:T(4,128)S(1)} %add.164), channel_id=1, source_target_pairs={{0,256},{4,260},{8,264},{12,268},{16,272},{20,276},{24,280},{28,28... | collective-permute-start | bytes 4616 | tf_op jit(solution)/shard_map/ppermute | solution.py:38
  75.8 13.4 %collective-permute-start.3 = (bf16[1,128,128]{2,1,0:T(8,128)(2,1)S(1)}, bf16[1,128,128]{2,1,0:T(8,128)(2,1)S(1)}, u32[]{:S(2)}, u32[]{:S(2)}) collective-permute-start(bf16[1,128,128]{2,1,0:T(8,128)(2,1)S(1)} %get-tuple-element.22), channel_id=1, source_target_pairs={{0,4},{4,8},{8,12},{12,16},{16,20},{20,24},{24,28},{28,32},{32,36}... | collective-permute-start | bytes 98312 | tf_op jit(solution)/shard_map/ppermute | solution.py:18
  89.8 10.0 %collective-permute-start.14 = (bf16[496,128]{1,0:T(8,128)(2,1)S(1)}, bf16[496,128]{1,0:T(8,128)(2,1)S(1)}, u32[]{:S(2)}, u32[]{:S(2)}) collective-permute-start(bf16[496,128]{1,0:T(8,128)(2,1)S(1)} %maximum_maximum_fusion), channel_id=1, source_target_pairs={{0,3},{1,0},{2,1},{3,2},{4,7},{5,4},{6,5},{7,6},{8,11},{9,8},{10,9... | collective-permute-start | bytes 380936 | tf_op jit(solution)/shard_map/ppermute | solution.py:101
  94.7 7.9 %collective-permute-start.13 = (bf16[496,128]{1,0:T(8,128)(2,1)S(1)}, bf16[496,128]{1,0:T(8,128)(2,1)S(1)}, u32[]{:S(2)}, u32[]{:S(2)}) collective-permute-start(bf16[496,128]{1,0:T(8,128)(2,1)S(1)} %maximum_maximum_fusion), channel_id=1, source_target_pairs={{0,2},{1,3},{2,0},{3,1},{4,6},{5,7},{6,4},{7,5},{8,10},{9,11},{10,... | collective-permute-start | bytes 380936 | tf_op jit(solution)/shard_map/ppermute | solution.py:101
  97.4 8.6 %collective-permute-start.12 = (bf16[496,128]{1,0:T(8,128)(2,1)S(1)}, bf16[496,128]{1,0:T(8,128)(2,1)S(1)}, u32[]{:S(2)}, u32[]{:S(2)}) collective-permute-start(bf16[496,128]{1,0:T(8,128)(2,1)S(1)} %maximum_maximum_fusion), channel_id=1, source_target_pairs={{0,1},{1,2},{2,3},{3,0},{4,5},{5,6},{6,7},{7,4},{8,9},{9,10},{10,1... | collective-permute-start | bytes 380936 | tf_op jit(solution)/shard_map/ppermute | solution.py:101

commit v2 on v1

--- a/solution.py
+++ b/solution.py
@@ -1,6 +1,8 @@
 import jax
 import jax.numpy as jnp
 from jax import lax
+from jax.experimental import pallas as pl
+from jax.experimental.pallas import tpu as pltpu
 from jax.sharding import PartitionSpec as P
 
 FRAMES = 4096
@@ -40,9 +42,49 @@
     return x
 
 
-def split_f32(x):
-    top = lax.reduce_precision(x, exponent_bits=8, mantissa_bits=7)
-    return top.astype(jnp.bfloat16), (x - top).astype(jnp.bfloat16)
+def fit_kernel(shapes_ref, shapes_t_ref, video_ref, valid_ref, basis_ref, basis_t_ref, data_ref, mode_ref):
+    step = pl.program_id(0)
+    model = jnp.dot(shapes_ref[...], basis_ref[...], preferred_element_type=jnp.float32)
+    resid = (valid_ref[...] * (model - video_ref[...].astype(jnp.float32))).astype(jnp.bfloat16)
+    data_ref[...] = jnp.dot(resid, basis_t_ref[...], preferred_element_type=jnp.float32)
+    part = jnp.dot(shapes_t_ref[...], resid, preferred_element_type=jnp.float32)
+
+    @pl.when(step == 0)
+    def _():
+        mode_ref[...] = part
+
+    @pl.when(step > 0)
+    def _():
+        mode_ref[...] += part
+
+
+def fit(shapes, video, valid, basis, tile=384):
+    n_pixels, n_modes = shapes.shape
+    n_frames = video.shape[1]
+    flops = 3 * 2 * n_pixels * n_modes * n_frames
+    moved = video.size * 2 + shapes.size * 4 + n_pixels * n_modes * 4 + n_modes * n_frames * 8
+    return pl.pallas_call(
+        fit_kernel,
+        grid=(n_pixels // tile,),
+        in_specs=[
+            pl.BlockSpec((tile, n_modes), lambda i: (i, 0)),
+            pl.BlockSpec((n_modes, tile), lambda i: (0, i)),
+            pl.BlockSpec((tile, n_frames), lambda i: (i, 0)),
+            pl.BlockSpec((tile, 1), lambda i: (i, 0)),
+            pl.BlockSpec((n_modes, n_frames), lambda i: (0, 0)),
+            pl.BlockSpec((n_frames, n_modes), lambda i: (0, 0)),
+        ],
+        out_specs=[
+            pl.BlockSpec((tile, n_modes), lambda i: (i, 0)),
+            pl.BlockSpec((n_modes, n_frames), lambda i: (0, 0)),
+        ],
+        out_shape=[
+            jax.ShapeDtypeStruct((n_pixels, n_modes), jnp.float32),
+            jax.ShapeDtypeStruct((n_modes, n_frames), jnp.float32),
+        ],
+        compiler_params=pltpu.CompilerParams(dimension_semantics=("arbitrary",)),
+        cost_estimate=pl.CostEstimate(flops=flops, bytes_accessed=moved, transcendentals=0),
+    )(shapes, shapes.T, video, valid.astype(jnp.float32)[:, None], basis, basis.T)
 
 
 def body(video, shapes, valid, omega, damping, phase):
@@ -62,18 +104,9 @@
     grid = shapes.reshape(rows_local, IMG_W, shapes.shape[1])
     padded = with_halo(grid, (("pix", 0),), 1).astype(jnp.float32)
 
-    model = jnp.dot(shapes, basis, preferred_element_type=jnp.float32)
-    resid = (valid[:, None].astype(jnp.float32) * (model - video.astype(jnp.float32))).astype(
-        jnp.bfloat16
-    )
-    basis_part = scale * lax.dot_general(
-        shapes, resid, (((0,), (0,)), ((), ())), preferred_element_type=jnp.float32
-    )
-    terms = butterfly(mode_terms(basis_part, cosine, sine, times), "pix")
-
-    data_part = scale * lax.dot_general(
-        resid, basis, (((1,), (1,)), ((), ())), preferred_element_type=jnp.float32
-    )
+    data_raw, mode_raw = fit(shapes, video, valid, basis)
+    terms = butterfly(butterfly(mode_terms(scale * mode_raw, cosine, sine, times), "pix"), "frm")
+    data_part = scale * data_raw
     n_pixels, n_modes = data_part.shape
     quarter = n_pixels // n_frm
     parts = data_part.reshape(n_frm, quarter, n_modes)
@@ -91,25 +124,14 @@
     smooth_parts = smooth.reshape(n_frm, quarter, n_modes)
     own = (acc + jnp.take(smooth_parts, me, axis=0)).astype(jnp.bfloat16)
 
-    hi, lo = split_f32(terms)
-    extra = 16 - (quarter + 2 * terms.shape[0]) % 16
-    packet = jnp.concatenate(
-        [own, hi, lo, jnp.zeros((extra % 16, n_modes), jnp.bfloat16)], axis=0
-    )
+    packet = own
     got = [packet]
     for s in range(1, n_frm):
         got.append(lax.ppermute(packet, "frm", [(i, (i + s) % n_frm) for i in range(n_frm)]))
     stacked = jnp.stack(got)
     ordered = jnp.take(stacked, (me - jnp.arange(n_frm)) % n_frm, axis=0)
-    shape_grad = ordered[:, :quarter].reshape(n_pixels, n_modes)
-    k = terms.shape[0]
-    hi_all = ordered[:, quarter : quarter + k].astype(jnp.float32)
-    lo_all = ordered[:, quarter + k : quarter + 2 * k].astype(jnp.float32)
-    pieces = hi_all + lo_all
-    total = pieces[0]
-    for f in range(1, n_frm):
-        total = total + pieces[f]
-    return (shape_grad, total[0], total[1], total[2])
+    shape_grad = ordered.reshape(n_pixels, n_modes)
+    return (shape_grad, terms[0], terms[1], terms[2])
 
 
 def solution(mesh):

time: 109 us -> 127 us (1.17)
  starting transfers between devices: 54 us -> 68.4 us
  other arithmetic: 1.71 us -> 14.5 us
  matrix products: 11 us -> 0 us
  Pallas kernels: 0 us -> 7.28 us
  local copies, waits for them, and re-layouts: 8.31 us -> 3.62 us
    ppermute x1, waiting for transfers between devices: 11.5 us -> 0.01 us  [with_halo(): lax.ppermute(tail, axis, [(i, (i + 1) % count) for i in range(ends)])]
    dot_general x3 -> x0, matrix products: 11 us -> none  [the longest x1 4.77 us: body(): model = jnp.dot(shapes, basis, preferred_element_type=jnp.float32)]
    ppermute x1, starting transfers between devices: 2.33 us -> 11.8 us  [with_halo(): lax.ppermute(head, axis, [((i + 1) % count, i) for i in range(ends)])]
    ppermute x7 -> x9, waiting for transfers between devices: 14.4 us -> 22 us  [butterfly(): x = x + lax.ppermute(x, axis, [(i, i ^ bit) for i in range(count)])]
    convert_element_type x2 -> x3, other arithmetic: 0.01 us -> 7.39 us  [the longest x2 6.7 us: body(): basis = cosine.astype(jnp.bfloat16)]
    pallas_call x0 -> x1, Pallas kernels: none -> 7.28 us  [fit(): pl.pallas_call(fit_kernel, grid=(n_pixels // tile,), in_specs=[pl.BlockSp...]
    ppermute x3, waiting for transfers between devices: 0.01 us -> 5.81 us  [body(): lax.ppermute(send, 'frm', [(i, (i + s) % n_frm) for i in range(n_frm)])]
    unnamed x9, local copies, waits for them, and re-layouts: 6.24 us -> 1.01 us
  transfers between devices with their start and end apart: 15 -> 17, of which waited for: 7 -> 10; matrix products, arithmetic and copies ran while one was open for 3% -> 2% of each run, Pallas kernels for 0% -> 0%
where the time goes in v2:
time: 127 us; the launch traced here: 126 us
  starting transfers between devices  68.4 us (54%)
  waiting for transfers between devices  30.9 us (24%)
  other arithmetic  14.5 us (11%)
  Pallas kernels  7.28 us (6%)
  local copies, waits for them, and re-layouts  3.62 us (3%)
    ppermute x9, starting transfers between devices, butterfly(): x = x + lax.ppermute(x, axis, [(i, i ^ bit) for i in range(count)])  32.4 us
    ppermute x9, waiting for transfers between devices, butterfly(): x = x + lax.ppermute(x, axis, [(i, i ^ bit) for i in range(count)])  22 us
    ppermute x1, starting transfers between devices, with_halo(): lax.ppermute(head, axis, [((i + 1) % count, i) for i in range(ends)])  11.8 us
    ppermute x3, starting transfers between devices, body(): lax.ppermute(send, 'frm', [(i, (i + s) % n_frm) for i in range(n_frm)])  11.2 us
    ppermute x3, starting transfers between devices, body(): lax.ppermute(packet, 'frm', [(i, (i + s) % n_frm) for i in range(n_frm)])  11.1 us
    pallas_call x1, Pallas kernels, fit(): pl.pallas_call(fit_kernel, grid=(n_pixels // tile,), in_specs=[pl.BlockSp...  7.28 us
    convert_element_type x2, other arithmetic, body(): basis = cosine.astype(jnp.bfloat16)  6.7 us
    ppermute x3, waiting for transfers between devices, body(): lax.ppermute(send, 'frm', [(i, (i + s) % n_frm) for i in range(n_frm)])  5.81 us
  transfers between devices with their start and end apart: 17, of which 10 were waited for; matrix products, arithmetic and copies ran while one was open for 2% of the time, Pallas kernels for 0%

profile of v2, /device:TPU:32, one launch (start us, length us, event | category | flops | bytes accessed | tf_op | source)
XLA Modules:
  0.0 125.7 jit_solution(8645503094045628091)
XLA Ops:
  1.4 3.3 %fusion.1.basis_ref = bf16[128,1024]{1,0:T(8,128)(2,1)} fusion(f32[128]{0:T(128)} %param.13, f32[128]{0:T(128)} %param.11, f32[1024]{0:T(1024)S(1)} %convert_multiply_fusion, f32[128]{0:T(128)S(1)} %neg.16), kind=kLoop, calls=%fused_computation.13 | loop fusion | flops 655360 | bytes 267776 | tf_op jit(solution)/shard_map/convert_element_type | solution.py:101
  4.7 3.4 %multiply_convert_fusion.basis_t_ref = bf16[1024,128]{1,0:T(8,128)(2,1)} fusion(f32[128]{0:T(128)} %param.13, f32[128]{0:T(128)} %param.11, f32[1024]{0:T(1024)S(1)} %convert_multiply_fusion, f32[128]{0:T(128)S(1)} %neg.16), kind=kLoop, calls=%fused_computation.9 | loop fusion | flops 655360 | bytes 267776 | tf_op jit(solution)/shard_map/convert_element_type | solution.py:101
  11.0 7.3 %shard_map.93 = (f32[1920,128]{1,0:T(8,128)}, f32[128,1024]{1,0:T(8,128)}) custom-call(bf16[1920,128]{1,0:T(8,128)(2,1)} %shapes_ref.1, bf16[128,1920]{1,0:T(8,128)(2,1)} %bitcast.47, bf16[1920,1024]{1,0:T(8,128)(2,1)} %video_ref.1, f32[1920,1]{1,0:T(8,128)} %broadcast_in_dim.51.valid_ref, bf16[128,1024]{1,0:T(8,128)(2,1)} %fusion.1.basis_ref, ...), custom_call_target="tpu_custom_call" | custom-call | flops 1509949440 | bytes 6946816 | tf_op jit(solution)/shard_map/pallas_call | solution.py:66
  18.3 3.3 %multiply_reduce_fusion.2 = (f32[128]{0:T(128)S(1)}, f32[128]{0:T(128)S(1)}, f32[128]{0:T(128)S(1)}) fusion(f32[128,1024]{1,0:T(8,128)} %get-tuple-element.8, f32[1024]{0:T(1024)S(1)} %fusion.5, f32[128]{0:T(128)S(1)} %copy-done.2, f32[128]{0:T(128)S(1)} %copy-done.3, f32[1024]{0:T(1024)S(1)} %convert_multiply_fusion, f32[128]{0:T(128)S(1)} %neg.16), kind=kLoop, calls=%fused_computation.7 | loop fusion | flops 1965696 | bytes 535552 | tf_op jit(solution)/shard_map/reduce_sum | solution.py:30
  24.8 10.9 %collective-permute-start.9 = (f32[3,128]{1,0:T(4,128)S(1)}, f32[3,128]{1,0:T(4,128)S(1)}, u32[]{:S(2)}, u32[]{:S(2)}) collective-permute-start(f32[3,128]{1,0:T(4,128)S(1)} %fusion.10), channel_id=1, source_target_pairs={{0,8},{4,12},{8,0},{12,4},{16,24},{20,28},{24,16},{28,20},{32,40},... | collective-permute-start | bytes 4616 | tf_op jit(solution)/shard_map/ppermute | solution.py:40
  37.2 3.4 %collective-permute-start.10 = (f32[3,128]{1,0:T(4,128)S(1)}, f32[3,128]{1,0:T(4,128)S(1)}, u32[]{:S(2)}, u32[]{:S(2)}) collective-permute-start(f32[3,128]{1,0:T(4,128)S(1)} %fusion.11), channel_id=1, source_target_pairs={{0,16},{4,20},{8,24},{12,28},{16,0},{20,4},{24,8},{28,12},{32,48},... | collective-permute-start | bytes 4616 | tf_op jit(solution)/shard_map/ppermute | solution.py:40
  40.7 2.0 %collective-permute-done.10 = f32[3,128]{1,0:T(4,128)S(1)} collective-permute-done((f32[3,128]{1,0:T(4,128)S(1)}, f32[3,128]{1,0:T(4,128)S(1)}, u32[]{:S(2)}, u32[]{:S(2)}) %collective-permute-start.10) | collective-permute-done | bytes 1568 | tf_op jit(solution)/shard_map/ppermute | solution.py:40
  42.7 4.9 %collective-permute-start.11 = (f32[3,128]{1,0:T(4,128)S(1)}, f32[3,128]{1,0:T(4,128)S(1)}, u32[]{:S(2)}, u32[]{:S(2)}) collective-permute-start(f32[3,128]{1,0:T(4,128)S(1)} %add.161), channel_id=1, source_target_pairs={{0,32},{4,36},{8,40},{12,44},{16,48},{20,52},{24,56},{28,60},{32,0... | collective-permute-start | bytes 4616 | tf_op jit(solution)/shard_map/ppermute | solution.py:40
  47.7 3.4 %collective-permute-start = (f32[480,128]{1,0:T(8,128)S(1)}, f32[480,128]{1,0:T(8,128)S(1)}, u32[]{:S(2)}, u32[]{:S(2)}) collective-permute-start(f32[480,128]{1,0:T(8,128)S(1)} %get-tuple-element.23), channel_id=1, source_target_pairs={{0,1},{1,2},{2,3},{3,0},{4,5},{5,6},{6,7},{7,4},{8,9},{9,10},{10,1... | collective-permute-start | bytes 737288 | tf_op jit(solution)/shard_map/ppermute | solution.py:116
  51.1 4.3 %collective-permute-start.1 = (f32[480,128]{1,0:T(8,128)S(1)}, f32[480,128]{1,0:T(8,128)S(1)}, u32[]{:S(2)}, u32[]{:S(2)}) collective-permute-start(f32[480,128]{1,0:T(8,128)S(1)} %get-tuple-element.25), channel_id=1, source_target_pairs={{0,2},{1,3},{2,0},{3,1},{4,6},{5,7},{6,4},{7,5},{8,10},{9,11},{10,... | collective-permute-start | bytes 737288 | tf_op jit(solution)/shard_map/ppermute | solution.py:116
  55.4 2.6 %collective-permute-start.12 = (f32[3,128]{1,0:T(4,128)S(1)}, f32[3,128]{1,0:T(4,128)S(1)}, u32[]{:S(2)}, u32[]{:S(2)}) collective-permute-start(f32[3,128]{1,0:T(4,128)S(1)} %add.162), channel_id=1, source_target_pairs={{0,64},{4,68},{8,72},{12,76},{16,80},{20,84},{24,88},{28,92},{32,9... | collective-permute-start | bytes 4616 | tf_op jit(solution)/shard_map/ppermute | solution.py:40
  60.0 11.8 %collective-permute-start.4 = (bf16[1,128,128]{2,1,0:T(8,128)(2,1)S(1)}, bf16[1,128,128]{2,1,0:T(8,128)(2,1)S(1)}, u32[]{:S(2)}, u32[]{:S(2)}) collective-permute-start(bf16[1,128,128]{2,1,0:T(8,128)(2,1)S(1)} %get-tuple-element.27), channel_id=1, source_target_pairs={{4,0},{8,4},{12,8},{16,12},{20,16},{24,20},{28,24},{32,28},{36,32}... | collective-permute-start | bytes 98312 | tf_op jit(solution)/shard_map/ppermute | solution.py:22
  71.8 1.9 %collective-permute-start.13 = (f32[3,128]{1,0:T(4,128)S(1)}, f32[3,128]{1,0:T(4,128)S(1)}, u32[]{:S(2)}, u32[]{:S(2)}) collective-permute-start(f32[3,128]{1,0:T(4,128)S(1)} %add.163), channel_id=1, source_target_pairs={{0,128},{4,132},{8,136},{12,140},{16,144},{20,148},{24,152},{28,15... | collective-permute-start | bytes 4616 | tf_op jit(solution)/shard_map/ppermute | solution.py:40
  73.7 4.4 %collective-permute-done.13 = f32[3,128]{1,0:T(4,128)S(1)} collective-permute-done((f32[3,128]{1,0:T(4,128)S(1)}, f32[3,128]{1,0:T(4,128)S(1)}, u32[]{:S(2)}, u32[]{:S(2)}) %collective-permute-start.13) | collective-permute-done | bytes 1568 | tf_op jit(solution)/shard_map/ppermute | solution.py:40
  80.1 7.4 %collective-permute-done.14 = f32[3,128]{1,0:T(4,128)S(1)} collective-permute-done((f32[3,128]{1,0:T(4,128)S(1)}, f32[3,128]{1,0:T(4,128)S(1)}, u32[]{:S(2)}, u32[]{:S(2)}) %collective-permute-start.14) | collective-permute-done | bytes 1568 | tf_op jit(solution)/shard_map/ppermute | solution.py:40
  87.5 2.4 %collective-permute-start.15 = (f32[3,128]{1,0:T(4,128)S(1)}, f32[3,128]{1,0:T(4,128)S(1)}, u32[]{:S(2)}, u32[]{:S(2)}) collective-permute-start(f32[3,128]{1,0:T(4,128)S(1)} %add.165), channel_id=1, source_target_pairs={{0,1},{1,0},{2,3},{3,2},{4,5},{5,4},{6,7},{7,6},{8,9},{9,8},{10,11... | collective-permute-start | bytes 4616 | tf_op jit(solution)/shard_map/ppermute | solution.py:40
  90.0 3.0 %collective-permute-done.15 = f32[3,128]{1,0:T(4,128)S(1)} collective-permute-done((f32[3,128]{1,0:T(4,128)S(1)}, f32[3,128]{1,0:T(4,128)S(1)}, u32[]{:S(2)}, u32[]{:S(2)}) %collective-permute-start.15) | collective-permute-done | bytes 1568 | tf_op jit(solution)/shard_map/ppermute | solution.py:40
  93.0 2.4 %collective-permute-start.16 = (f32[3,128]{1,0:T(4,128)S(1)}, f32[3,128]{1,0:T(4,128)S(1)}, u32[]{:S(2)}, u32[]{:S(2)}) collective-permute-start(f32[3,128]{1,0:T(4,128)S(1)} %add.166), channel_id=1, source_target_pairs={{0,2},{1,3},{2,0},{3,1},{4,6},{5,7},{6,4},{7,5},{8,10},{9,11},{10,... | collective-permute-start | bytes 4616 | tf_op jit(solution)/shard_map/ppermute | solution.py:40
  95.6 3.7 %collective-permute-done.16 = f32[3,128]{1,0:T(4,128)S(1)} collective-permute-done((f32[3,128]{1,0:T(4,128)S(1)}, f32[3,128]{1,0:T(4,128)S(1)}, u32[]{:S(2)}, u32[]{:S(2)}) %collective-permute-start.16) | collective-permute-done | bytes 1568 | tf_op jit(solution)/shard_map/ppermute | solution.py:40
  99.4 3.6 %collective-permute-start.2 = (f32[480,128]{1,0:T(8,128)S(1)}, f32[480,128]{1,0:T(8,128)S(1)}, u32[]{:S(2)}, u32[]{:S(2)}) collective-permute-start(f32[480,128]{1,0:T(8,128)S(1)} %get-tuple-element.24), channel_id=1, source_target_pairs={{0,3},{1,0},{2,1},{3,2},{4,7},{5,4},{6,5},{7,6},{8,11},{9,8},{10,9... | collective-permute-start | bytes 737288 | tf_op jit(solution)/shard_map/ppermute | solution.py:116
  103.4 5.8 %collective-permute-done.2 = f32[480,128]{1,0:T(8,128)S(1)} collective-permute-done((f32[480,128]{1,0:T(8,128)S(1)}, f32[480,128]{1,0:T(8,128)S(1)}, u32[]{:S(2)}, u32[]{:S(2)}) %collective-permute-start.2) | collective-permute-done | bytes 245792 | tf_op jit(solution)/shard_map/ppermute | solution.py:116
  109.2 4.9 %collective-permute-start.5 = (bf16[480,128]{1,0:T(8,128)(2,1)S(1)}, bf16[480,128]{1,0:T(8,128)(2,1)S(1)}, u32[]{:S(2)}, u32[]{:S(2)}) collective-permute-start(bf16[480,128]{1,0:T(8,128)(2,1)S(1)} %fusion.2), channel_id=1, source_target_pairs={{0,1},{1,2},{2,3},{3,0},{4,5},{5,6},{6,7},{7,4},{8,9},{9,10},{10,1... | collective-permute-start | bytes 368648 | tf_op jit(solution)/shard_map/ppermute | solution.py:130
  114.2 2.2 %collective-permute-start.6 = (bf16[480,128]{1,0:T(8,128)(2,1)S(1)}, bf16[480,128]{1,0:T(8,128)(2,1)S(1)}, u32[]{:S(2)}, u32[]{:S(2)}) collective-permute-start(bf16[480,128]{1,0:T(8,128)(2,1)S(1)} %fusion.2), channel_id=1, source_target_pairs={{0,2},{1,3},{2,0},{3,1},{4,6},{5,7},{6,4},{7,5},{8,10},{9,11},{10,... | collective-permute-start | bytes 368648 | tf_op jit(solution)/shard_map/ppermute | solution.py:130
  116.4 4.0 %collective-permute-start.7 = (bf16[480,128]{1,0:T(8,128)(2,1)S(1)}, bf16[480,128]{1,0:T(8,128)(2,1)S(1)}, u32[]{:S(2)}, u32[]{:S(2)}) collective-permute-start(bf16[480,128]{1,0:T(8,128)(2,1)S(1)} %fusion.2), channel_id=1, source_target_pairs={{0,3},{1,0},{2,1},{3,2},{4,7},{5,4},{6,5},{7,6},{8,11},{9,8},{10,9... | collective-permute-start | bytes 368648 | tf_op jit(solution)/shard_map/ppermute | solution.py:130
  (54 shorter events, 18.2 us)
Async XLA Ops:
  0.6 9.4 %copy-start = (bf16[1920,128]{1,0:T(8,128)(2,1)S(1)}, bf16[1920,128]{1,0:T(8,128)(2,1)}, u32[]{:S(2)}) copy-start(bf16[1920,128]{1,0:T(8,128)(2,1)} %shapes_ref.1) | copy-start | bytes 1474564
  11.0 7.3 %copy-start.2 = (f32[128]{0:T(128)S(1)}, f32[128]{0:T(128)}, u32[]{:S(2)}) copy-start(f32[128]{0:T(128)} %param.13) | copy-start | bytes 1540
  11.0 7.3 %copy-start.3 = (f32[128]{0:T(128)S(1)}, f32[128]{0:T(128)}, u32[]{:S(2)}) copy-start(f32[128]{0:T(128)} %param.11) | copy-start | bytes 1540
  21.7 3.1 %collective-permute-start.8 = (f32[3,128]{1,0:T(4,128)S(1)}, f32[3,128]{1,0:T(4,128)S(1)}, u32[]{:S(2)}, u32[]{:S(2)}) collective-permute-start(f32[3,128]{1,0:T(4,128)S(1)} %pad_maximum_fusion.1), channel_id=1, source_target_pairs={{0,4},{4,0},{8,12},{12,8},{16,20},{20,16},{24,28},{28,24},{32,36},... | collective-permute-start | bytes 4616 | tf_op jit(solution)/shard_map/ppermute | solution.py:40
  24.8 12.5 %collective-permute-start.9 = (f32[3,128]{1,0:T(4,128)S(1)}, f32[3,128]{1,0:T(4,128)S(1)}, u32[]{:S(2)}, u32[]{:S(2)}) collective-permute-start(f32[3,128]{1,0:T(4,128)S(1)} %fusion.10), channel_id=1, source_target_pairs={{0,8},{4,12},{8,0},{12,4},{16,24},{20,28},{24,16},{28,20},{32,40},... | collective-permute-start | bytes 4616 | tf_op jit(solution)/shard_map/ppermute | solution.py:40
  37.0 21.1 %copy-start.1 = (bf16[1920,128]{1,0:T(8,128)(2,1)S(1)}, bf16[1920,128]{1,0:T(8,128)(2,1)}, u32[]{:S(2)}) copy-start(bf16[1920,128]{1,0:T(8,128)(2,1)} %shapes_ref.1) | copy-start | bytes 1474564
  37.2 5.5 %collective-permute-start.10 = (f32[3,128]{1,0:T(4,128)S(1)}, f32[3,128]{1,0:T(4,128)S(1)}, u32[]{:S(2)}, u32[]{:S(2)}) collective-permute-start(f32[3,128]{1,0:T(4,128)S(1)} %fusion.11), channel_id=1, source_target_pairs={{0,16},{4,20},{8,24},{12,28},{16,0},{20,4},{24,8},{28,12},{32,48},... | collective-permute-start | bytes 4616 | tf_op jit(solution)/shard_map/ppermute | solution.py:40
  42.7 12.7 %collective-permute-start.11 = (f32[3,128]{1,0:T(4,128)S(1)}, f32[3,128]{1,0:T(4,128)S(1)}, u32[]{:S(2)}, u32[]{:S(2)}) collective-permute-start(f32[3,128]{1,0:T(4,128)S(1)} %add.161), channel_id=1, source_target_pairs={{0,32},{4,36},{8,40},{12,44},{16,48},{20,52},{24,56},{28,60},{32,0... | collective-permute-start | bytes 4616 | tf_op jit(solution)/shard_map/ppermute | solution.py:40
  47.7 55.6 %collective-permute-start = (f32[480,128]{1,0:T(8,128)S(1)}, f32[480,128]{1,0:T(8,128)S(1)}, u32[]{:S(2)}, u32[]{:S(2)}) collective-permute-start(f32[480,128]{1,0:T(8,128)S(1)} %get-tuple-element.23), channel_id=1, source_target_pairs={{0,1},{1,2},{2,3},{3,0},{4,5},{5,6},{6,7},{7,4},{8,9},{9,10},{10,1... | collective-permute-start | bytes 737288 | tf_op jit(solution)/shard_map/ppermute | solution.py:116
  51.1 52.2 %collective-permute-start.1 = (f32[480,128]{1,0:T(8,128)S(1)}, f32[480,128]{1,0:T(8,128)S(1)}, u32[]{:S(2)}, u32[]{:S(2)}) collective-permute-start(f32[480,128]{1,0:T(8,128)S(1)} %get-tuple-element.25), channel_id=1, source_target_pairs={{0,2},{1,3},{2,0},{3,1},{4,6},{5,7},{6,4},{7,5},{8,10},{9,11},{10,... | collective-permute-start | bytes 737288 | tf_op jit(solution)/shard_map/ppermute | solution.py:116
  55.4 16.3 %collective-permute-start.12 = (f32[3,128]{1,0:T(4,128)S(1)}, f32[3,128]{1,0:T(4,128)S(1)}, u32[]{:S(2)}, u32[]{:S(2)}) collective-permute-start(f32[3,128]{1,0:T(4,128)S(1)} %add.162), channel_id=1, source_target_pairs={{0,64},{4,68},{8,72},{12,76},{16,80},{20,84},{24,88},{28,92},{32,9... | collective-permute-start | bytes 4616 | tf_op jit(solution)/shard_map/ppermute | solution.py:40
  58.1 44.9 %collective-permute-start.3 = (bf16[1,128,128]{2,1,0:T(8,128)(2,1)S(1)}, bf16[1,128,128]{2,1,0:T(8,128)(2,1)S(1)}, u32[]{:S(2)}, u32[]{:S(2)}) collective-permute-start(bf16[1,128,128]{2,1,0:T(8,128)(2,1)S(1)} %get-tuple-element.26), channel_id=1, source_target_pairs={{0,4},{4,8},{8,12},{12,16},{16,20},{20,24},{24,28},{28,32},{32,36}... | collective-permute-start | bytes 98312 | tf_op jit(solution)/shard_map/ppermute | solution.py:20
  60.0 43.0 %collective-permute-start.4 = (bf16[1,128,128]{2,1,0:T(8,128)(2,1)S(1)}, bf16[1,128,128]{2,1,0:T(8,128)(2,1)S(1)}, u32[]{:S(2)}, u32[]{:S(2)}) collective-permute-start(bf16[1,128,128]{2,1,0:T(8,128)(2,1)S(1)} %get-tuple-element.27), channel_id=1, source_target_pairs={{4,0},{8,4},{12,8},{16,12},{20,16},{24,20},{28,24},{32,28},{36,32}... | collective-permute-start | bytes 98312 | tf_op jit(solution)/shard_map/ppermute | solution.py:22
  71.8 6.4 %collective-permute-start.13 = (f32[3,128]{1,0:T(4,128)S(1)}, f32[3,128]{1,0:T(4,128)S(1)}, u32[]{:S(2)}, u32[]{:S(2)}) collective-permute-start(f32[3,128]{1,0:T(4,128)S(1)} %add.163), channel_id=1, source_target_pairs={{0,128},{4,132},{8,136},{12,140},{16,144},{20,148},{24,152},{28,15... | collective-permute-start | bytes 4616 | tf_op jit(solution)/shard_map/ppermute | solution.py:40
  78.2 9.4 %collective-permute-start.14 = (f32[3,128]{1,0:T(4,128)S(1)}, f32[3,128]{1,0:T(4,128)S(1)}, u32[]{:S(2)}, u32[]{:S(2)}) collective-permute-start(f32[3,128]{1,0:T(4,128)S(1)} %add.164), channel_id=1, source_target_pairs={{0,256},{4,260},{8,264},{12,268},{16,272},{20,276},{24,280},{28,28... | collective-permute-start | bytes 4616 | tf_op jit(solution)/shard_map/ppermute | solution.py:40
  87.5 5.5 %collective-permute-start.15 = (f32[3,128]{1,0:T(4,128)S(1)}, f32[3,128]{1,0:T(4,128)S(1)}, u32[]{:S(2)}, u32[]{:S(2)}) collective-permute-start(f32[3,128]{1,0:T(4,128)S(1)} %add.165), channel_id=1, source_target_pairs={{0,1},{1,0},{2,3},{3,2},{4,5},{5,4},{6,7},{7,6},{8,9},{9,8},{10,11... | collective-permute-start | bytes 4616 | tf_op jit(solution)/shard_map/ppermute | solution.py:40
  93.0 6.4 %collective-permute-start.16 = (f32[3,128]{1,0:T(4,128)S(1)}, f32[3,128]{1,0:T(4,128)S(1)}, u32[]{:S(2)}, u32[]{:S(2)}) collective-permute-start(f32[3,128]{1,0:T(4,128)S(1)} %add.166), channel_id=1, source_target_pairs={{0,2},{1,3},{2,0},{3,1},{4,6},{5,7},{6,4},{7,5},{8,10},{9,11},{10,... | collective-permute-start | bytes 4616 | tf_op jit(solution)/shard_map/ppermute | solution.py:40
  99.4 9.8 %collective-permute-start.2 = (f32[480,128]{1,0:T(8,128)S(1)}, f32[480,128]{1,0:T(8,128)S(1)}, u32[]{:S(2)}, u32[]{:S(2)}) collective-permute-start(f32[480,128]{1,0:T(8,128)S(1)} %get-tuple-element.24), channel_id=1, source_target_pairs={{0,3},{1,0},{2,1},{3,2},{4,7},{5,4},{6,5},{7,6},{8,11},{9,8},{10,9... | collective-permute-start | bytes 737288 | tf_op jit(solution)/shard_map/ppermute | solution.py:116
  109.2 11.6 %collective-permute-start.5 = (bf16[480,128]{1,0:T(8,128)(2,1)S(1)}, bf16[480,128]{1,0:T(8,128)(2,1)S(1)}, u32[]{:S(2)}, u32[]{:S(2)}) collective-permute-start(bf16[480,128]{1,0:T(8,128)(2,1)S(1)} %fusion.2), channel_id=1, source_target_pairs={{0,1},{1,2},{2,3},{3,0},{4,5},{5,6},{6,7},{7,4},{8,9},{9,10},{10,1... | collective-permute-start | bytes 368648 | tf_op jit(solution)/shard_map/ppermute | solution.py:130
  114.2 8.5 %collective-permute-start.6 = (bf16[480,128]{1,0:T(8,128)(2,1)S(1)}, bf16[480,128]{1,0:T(8,128)(2,1)S(1)}, u32[]{:S(2)}, u32[]{:S(2)}) collective-permute-start(bf16[480,128]{1,0:T(8,128)(2,1)S(1)} %fusion.2), channel_id=1, source_target_pairs={{0,2},{1,3},{2,0},{3,1},{4,6},{5,7},{6,4},{7,5},{8,10},{9,11},{10,... | collective-permute-start | bytes 368648 | tf_op jit(solution)/shard_map/ppermute | solution.py:130
  116.4 7.6 %collective-permute-start.7 = (bf16[480,128]{1,0:T(8,128)(2,1)S(1)}, bf16[480,128]{1,0:T(8,128)(2,1)S(1)}, u32[]{:S(2)}, u32[]{:S(2)}) collective-permute-start(bf16[480,128]{1,0:T(8,128)(2,1)S(1)} %fusion.2), channel_id=1, source_target_pairs={{0,3},{1,0},{2,1},{3,2},{4,7},{5,4},{6,5},{7,6},{8,11},{9,8},{10,9... | collective-permute-start | bytes 368648 | tf_op jit(solution)/shard_map/ppermute | solution.py:130

commit v3 on v2

--- a/solution.py
+++ b/solution.py
@@ -33,6 +33,17 @@
     return jnp.stack([omega_part, damping_part, phase_part])
 
 
+def split_f32(x):
+    top = lax.reduce_precision(x, exponent_bits=8, mantissa_bits=7)
+    return top.astype(jnp.bfloat16), (x - top).astype(jnp.bfloat16)
+
+
+def sum_over(x, axis):
+    count = lax.axis_size(axis)
+    copies = lax.all_to_all(jnp.broadcast_to(x[None], (count,) + x.shape), axis, 0, 0, tiled=False)
+    return jnp.sum(copies, axis=0)
+
+
 def butterfly(x, axis):
     count = lax.axis_size(axis)
     bit = 1
@@ -42,11 +53,13 @@
     return x
 
 
-def fit_kernel(shapes_ref, shapes_t_ref, video_ref, valid_ref, basis_ref, basis_t_ref, data_ref, mode_ref):
+def fit_kernel(shapes_ref, shapes_t_ref, video_ref, valid_ref, basis_ref, data_ref, mode_ref):
     step = pl.program_id(0)
     model = jnp.dot(shapes_ref[...], basis_ref[...], preferred_element_type=jnp.float32)
     resid = (valid_ref[...] * (model - video_ref[...].astype(jnp.float32))).astype(jnp.bfloat16)
-    data_ref[...] = jnp.dot(resid, basis_t_ref[...], preferred_element_type=jnp.float32)
+    data_ref[...] = lax.dot_general(
+        resid, basis_ref[...], (((1,), (1,)), ((), ())), preferred_element_type=jnp.float32
+    )
     part = jnp.dot(shapes_t_ref[...], resid, preferred_element_type=jnp.float32)
 
     @pl.when(step == 0)
@@ -72,7 +85,6 @@
             pl.BlockSpec((tile, n_frames), lambda i: (i, 0)),
             pl.BlockSpec((tile, 1), lambda i: (i, 0)),
             pl.BlockSpec((n_modes, n_frames), lambda i: (0, 0)),
-            pl.BlockSpec((n_frames, n_modes), lambda i: (0, 0)),
         ],
         out_specs=[
             pl.BlockSpec((tile, n_modes), lambda i: (i, 0)),
@@ -84,7 +96,7 @@
         ],
         compiler_params=pltpu.CompilerParams(dimension_semantics=("arbitrary",)),
         cost_estimate=pl.CostEstimate(flops=flops, bytes_accessed=moved, transcendentals=0),
-    )(shapes, shapes.T, video, valid.astype(jnp.float32)[:, None], basis, basis.T)
+    )(shapes, shapes.T, video, valid.astype(jnp.float32)[:, None], basis)
 
 
 def body(video, shapes, valid, omega, damping, phase):
@@ -96,8 +108,9 @@
     times = (first + jnp.arange(frames_local)).astype(jnp.float32) / FRAMES
     envelope = jnp.exp(-damping[:, None] * times[None, :])
     angle_all = omega[:, None] * times[None, :] + phase[:, None]
-    cosine = envelope * jnp.cos(angle_all)
-    sine = envelope * jnp.sin(angle_all)
+    cosine, sine = lax.optimization_barrier(
+        (envelope * jnp.cos(angle_all), envelope * jnp.sin(angle_all))
+    )
     basis = cosine.astype(jnp.bfloat16)
 
     rows_local = shapes.shape[0] // IMG_W
@@ -105,8 +118,8 @@
     padded = with_halo(grid, (("pix", 0),), 1).astype(jnp.float32)
 
     data_raw, mode_raw = fit(shapes, video, valid, basis)
-    terms = butterfly(butterfly(mode_terms(scale * mode_raw, cosine, sine, times), "pix"), "frm")
     data_part = scale * data_raw
+    local_terms = mode_terms(scale * mode_raw, cosine, sine, times)
     n_pixels, n_modes = data_part.shape
     quarter = n_pixels // n_frm
     parts = data_part.reshape(n_frm, quarter, n_modes)
@@ -114,6 +127,7 @@
     for s in range(1, n_frm):
         send = jnp.take(parts, (me + s) % n_frm, axis=0)
         acc = acc + lax.ppermute(send, "frm", [(i, (i + s) % n_frm) for i in range(n_frm)])
+    terms = sum_over(local_terms, "pix")
 
     rows_total = rows_local * lax.axis_size("pix")
     rows_at = lax.axis_index("pix") * rows_local + jnp.arange(rows_local)
@@ -124,14 +138,23 @@
     smooth_parts = smooth.reshape(n_frm, quarter, n_modes)
     own = (acc + jnp.take(smooth_parts, me, axis=0)).astype(jnp.bfloat16)
 
-    packet = own
+    hi, lo = split_f32(terms)
+    k = terms.shape[0]
+    extra = (-(quarter + 2 * k)) % 16
+    packet = jnp.concatenate([own, hi, lo, jnp.zeros((extra, n_modes), jnp.bfloat16)], axis=0)
     got = [packet]
     for s in range(1, n_frm):
         got.append(lax.ppermute(packet, "frm", [(i, (i + s) % n_frm) for i in range(n_frm)]))
     stacked = jnp.stack(got)
     ordered = jnp.take(stacked, (me - jnp.arange(n_frm)) % n_frm, axis=0)
-    shape_grad = ordered.reshape(n_pixels, n_modes)
-    return (shape_grad, terms[0], terms[1], terms[2])
+    shape_grad = ordered[:, :quarter].reshape(n_pixels, n_modes)
+    pieces = ordered[:, quarter : quarter + k].astype(jnp.float32) + ordered[
+        :, quarter + k : quarter + 2 * k
+    ].astype(jnp.float32)
+    total = pieces[0]
+    for f in range(1, n_frm):
+        total = total + pieces[f]
+    return (shape_grad, total[0], total[1], total[2])
 
 
 def solution(mesh):

time: 127 us -> 91.7 us (0.72)
  the two profiles are of different devices: /device:TPU:32 before, /device:TPU:6 now
where the time goes in v3:
time: 91.7 us; the launch traced here: 91.1 us
  starting transfers between devices  50.8 us (55%)
  waiting for transfers between devices  20.3 us (22%)
  Pallas kernels  7.13 us (8%)
  other arithmetic  6.82 us (7%)
  local copies, waits for them, and re-layouts  5.1 us (6%)
  between operations  0.98 us (1%)
    all_to_all x1, starting transfers between devices, sum_over(): lax.all_to_all(jnp.broadcast_to(x[None], (count,) + x.shape), axis, 0, 0,...  19.8 us
    ppermute x3, starting transfers between devices, body(): lax.ppermute(packet, 'frm', [(i, (i + s) % n_frm) for i in range(n_frm)])  12.4 us
    ppermute x3, starting transfers between devices, body(): lax.ppermute(send, 'frm', [(i, (i + s) % n_frm) for i in range(n_frm)])  10.3 us
    pallas_call x1, Pallas kernels, fit(): pl.pallas_call(fit_kernel, grid=(n_pixels // tile,), in_specs=[pl.BlockSp...  7.13 us
    ppermute x1, waiting for transfers between devices, with_halo(): lax.ppermute(head, axis, [((i + 1) % count, i) for i in range(ends)])  6.95 us
    ppermute x3, waiting for transfers between devices, body(): lax.ppermute(packet, 'frm', [(i, (i + s) % n_frm) for i in range(n_frm)])  6.54 us
    ppermute x1, starting transfers between devices, with_halo(): lax.ppermute(head, axis, [((i + 1) % count, i) for i in range(ends)])  6.45 us
    ppermute x1, waiting for transfers between devices, with_halo(): lax.ppermute(tail, axis, [(i, (i + 1) % count) for i in range(ends)])  4.56 us
  transfers between devices with their start and end apart: 9, of which 5 were waited for; matrix products, arithmetic and copies ran while one was open for 1% of the time, Pallas kernels for 0%

profile of v3, /device:TPU:6, one launch (start us, length us, event | category | flops | bytes accessed | tf_op | source)
XLA Modules:
  0.0 91.1 jit_solution(6684830612246420892)
XLA Ops:
  0.7 0.7 neg.16
  1.4 2.7 %sine_multiply_fusion = (f32[128,1024]{1,0:T(8,128)S(1)}, f32[128,1024]{1,0:T(8,128)S(1)}) fusion(f32[128]{0:T(128)} %param.13, f32[128]{0:T(128)} %param.11, f32[1024]{0:T(1024)S(1)} %get-tuple-element.39, f32[128]{0:T(128)S(1)} %neg.16), kind=kLoop, calls=%fused_computation.8 | loop fusion | flops 655360 | bytes 1054208 | tf_op jit(solution)/shard_map/mul | solution.py:112
  4.1 1.0 %copy.15 = bf16[1920,128]{0,1:T(8,128)(2,1)} copy(bf16[1920,128]{1,0:T(8,128)(2,1)S(1)} %copy-done) | data formatting | bytes 983040 | tf_op args[1]
  5.1 1.3 %broadcast_in_dim.56.valid_ref = f32[1920,1]{1,0:T(8,128)} reshape(f32[1920]{0:T(1024)S(1)} %convert_element_type.51) | data formatting | bytes 15360 | tf_op jit(solution)/shard_map/broadcast_in_dim | solution.py:99
  6.4 0.7 convert_element_type.53.basis_ref
  7.1 7.1 %shard_map.93 = (f32[1920,128]{1,0:T(8,128)}, f32[128,1024]{1,0:T(8,128)}) custom-call(bf16[1920,128]{1,0:T(8,128)(2,1)} %shapes_ref.1, bf16[128,1920]{1,0:T(8,128)(2,1)} %bitcast.47, bf16[1920,1024]{1,0:T(8,128)(2,1)} %video_ref.1, f32[1920,1]{1,0:T(8,128)} %broadcast_in_dim.56.valid_ref, bf16[128,1024]{1,0:T(8,128)(2,1)} %convert_element_type.53.basis_ref), custom_call_target="tpu_custom_call" | custom-call | flops 1509949440 | bytes 6946816 | tf_op jit(solution)/shard_map/pallas_call | solution.py:79
  14.2 1.5 %multiply_reduce_fusion.2 = (f32[128]{0:T(128)S(1)}, f32[128]{0:T(128)S(1)}, f32[128]{0:T(128)S(1)}) fusion(f32[128,1024]{1,0:T(8,128)S(1)} %get-tuple-element.12, f32[128,1024]{1,0:T(8,128)} %get-tuple-element.11, f32[1024]{0:T(1024)S(1)} %get-tuple-element.40, f32[128,1024]{1,0:T(8,128)S(1)} %get-tuple-element.9), kind=kLoop, calls=%fused_computation.7 | loop fusion | flops 1310336 | bytes 1578496 | tf_op jit(solution)/shard_map/reduce_sum | solution.py:30
  15.7 0.7 broadcast_in_dim.41
  16.5 19.8 %all-to-all-start = ((f32[128,3,128]{2,1,0:T(4,128)}), f32[128,3,128]{2,1,0:T(4,128)S(1)}, u32[]{:S(2)}, u32[]{:S(2)}) async-start(f32[128,3,128]{2,1,0:T(4,128)} %broadcast_in_dim.41), calls=%async_computation | async-start | bytes 524288 | tf_op jit(solution)/shard_map/all_to_all | solution.py:43
  36.5 5.3 %collective-permute-start.2 = (f32[480,128]{1,0:T(8,128)S(1)}, f32[480,128]{1,0:T(8,128)S(1)}, u32[]{:S(2)}, u32[]{:S(2)}) collective-permute-start(f32[480,128]{1,0:T(8,128)S(1)} %get-tuple-element.28), channel_id=1, source_target_pairs={{0,3},{1,0},{2,1},{3,2},{4,7},{5,4},{6,5},{7,6},{8,11},{9,8},{10,9... | collective-permute-start | bytes 737288 | tf_op jit(solution)/shard_map/ppermute | solution.py:129
  41.9 1.9 %collective-permute-start.1 = (f32[480,128]{1,0:T(8,128)S(1)}, f32[480,128]{1,0:T(8,128)S(1)}, u32[]{:S(2)}, u32[]{:S(2)}) collective-permute-start(f32[480,128]{1,0:T(8,128)S(1)} %get-tuple-element.29), channel_id=1, source_target_pairs={{0,2},{1,3},{2,0},{3,1},{4,6},{5,7},{6,4},{7,5},{8,10},{9,11},{10,... | collective-permute-start | bytes 737288 | tf_op jit(solution)/shard_map/ppermute | solution.py:129
  43.8 3.0 %collective-permute-start = (f32[480,128]{1,0:T(8,128)S(1)}, f32[480,128]{1,0:T(8,128)S(1)}, u32[]{:S(2)}, u32[]{:S(2)}) collective-permute-start(f32[480,128]{1,0:T(8,128)S(1)} %get-tuple-element.27), channel_id=1, source_target_pairs={{0,1},{1,2},{2,3},{3,0},{4,5},{5,6},{6,7},{7,4},{8,9},{9,10},{10,1... | collective-permute-start | bytes 737288 | tf_op jit(solution)/shard_map/ppermute | solution.py:129
  46.8 6.5 %collective-permute-start.4 = (bf16[1,128,128]{2,1,0:T(8,128)(2,1)S(1)}, bf16[1,128,128]{2,1,0:T(8,128)(2,1)S(1)}, u32[]{:S(2)}, u32[]{:S(2)}) collective-permute-start(bf16[1,128,128]{2,1,0:T(8,128)(2,1)S(1)} %get-tuple-element.31), channel_id=1, source_target_pairs={{4,0},{8,4},{12,8},{16,12},{20,16},{24,20},{28,24},{32,28},{36,32}... | collective-permute-start | bytes 98312 | tf_op jit(solution)/shard_map/ppermute | solution.py:22
  53.3 1.9 %collective-permute-start.3 = (bf16[1,128,128]{2,1,0:T(8,128)(2,1)S(1)}, bf16[1,128,128]{2,1,0:T(8,128)(2,1)S(1)}, u32[]{:S(2)}, u32[]{:S(2)}) collective-permute-start(bf16[1,128,128]{2,1,0:T(8,128)(2,1)S(1)} %get-tuple-element.30), channel_id=1, source_target_pairs={{0,4},{4,8},{8,12},{12,16},{16,20},{20,24},{24,28},{28,32},{32,36}... | collective-permute-start | bytes 98312 | tf_op jit(solution)/shard_map/ppermute | solution.py:20
  55.4 7.0 %collective-permute-done.4 = bf16[1,128,128]{2,1,0:T(8,128)(2,1)S(1)} collective-permute-done((bf16[1,128,128]{2,1,0:T(8,128)(2,1)S(1)}, bf16[1,128,128]{2,1,0:T(8,128)(2,1)S(1)}, u32[]{:S(2)}, u32[]{:S(2)}) %collective-permute-start.4) | collective-permute-done | bytes 32800 | tf_op jit(solution)/shard_map/ppermute | solution.py:22
  62.3 4.6 %collective-permute-done.3 = bf16[1,128,128]{2,1,0:T(8,128)(2,1)S(1)} collective-permute-done((bf16[1,128,128]{2,1,0:T(8,128)(2,1)S(1)}, bf16[1,128,128]{2,1,0:T(8,128)(2,1)S(1)}, u32[]{:S(2)}, u32[]{:S(2)}) %collective-permute-start.3) | collective-permute-done | bytes 32800 | tf_op jit(solution)/shard_map/ppermute | solution.py:20
  67.3 2.2 %collective-permute-done.1 = f32[480,128]{1,0:T(8,128)S(1)} collective-permute-done((f32[480,128]{1,0:T(8,128)S(1)}, f32[480,128]{1,0:T(8,128)S(1)}, u32[]{:S(2)}, u32[]{:S(2)}) %collective-permute-start.1) | collective-permute-done | bytes 245792 | tf_op jit(solution)/shard_map/ppermute | solution.py:129
  69.9 1.9 %collective-permute-start.7 = (bf16[496,128]{1,0:T(8,128)(2,1)S(1)}, bf16[496,128]{1,0:T(8,128)(2,1)S(1)}, u32[]{:S(2)}, u32[]{:S(2)}) collective-permute-start(bf16[496,128]{1,0:T(8,128)(2,1)S(1)} %maximum_maximum_fusion), channel_id=1, source_target_pairs={{0,3},{1,0},{2,1},{3,2},{4,7},{5,4},{6,5},{7,6},{8,11},{9,8},{10,9... | collective-permute-start | bytes 380936 | tf_op jit(solution)/shard_map/ppermute | solution.py:147
  71.8 8.5 %collective-permute-start.6 = (bf16[496,128]{1,0:T(8,128)(2,1)S(1)}, bf16[496,128]{1,0:T(8,128)(2,1)S(1)}, u32[]{:S(2)}, u32[]{:S(2)}) collective-permute-start(bf16[496,128]{1,0:T(8,128)(2,1)S(1)} %maximum_maximum_fusion), channel_id=1, source_target_pairs={{0,2},{1,3},{2,0},{3,1},{4,6},{5,7},{6,4},{7,5},{8,10},{9,11},{10,... | collective-permute-start | bytes 380936 | tf_op jit(solution)/shard_map/ppermute | solution.py:147
  80.3 1.9 %collective-permute-start.5 = (bf16[496,128]{1,0:T(8,128)(2,1)S(1)}, bf16[496,128]{1,0:T(8,128)(2,1)S(1)}, u32[]{:S(2)}, u32[]{:S(2)}) collective-permute-start(bf16[496,128]{1,0:T(8,128)(2,1)S(1)} %maximum_maximum_fusion), channel_id=1, source_target_pairs={{0,1},{1,2},{2,3},{3,0},{4,5},{5,6},{6,7},{7,4},{8,9},{9,10},{10,1... | collective-permute-start | bytes 380936 | tf_op jit(solution)/shard_map/ppermute | solution.py:147
  82.4 3.0 %collective-permute-done.6 = bf16[496,128]{1,0:T(8,128)(2,1)S(1)} collective-permute-done((bf16[496,128]{1,0:T(8,128)(2,1)S(1)}, bf16[496,128]{1,0:T(8,128)(2,1)S(1)}, u32[]{:S(2)}, u32[]{:S(2)}) %collective-permute-start.6) | collective-permute-done | bytes 127008 | tf_op jit(solution)/shard_map/ppermute | solution.py:147
  85.4 3.6 %collective-permute-done.5 = bf16[496,128]{1,0:T(8,128)(2,1)S(1)} collective-permute-done((bf16[496,128]{1,0:T(8,128)(2,1)S(1)}, bf16[496,128]{1,0:T(8,128)(2,1)S(1)}, u32[]{:S(2)}, u32[]{:S(2)}) %collective-permute-start.5) | collective-permute-done | bytes 127008 | tf_op jit(solution)/shard_map/ppermute | solution.py:147
  89.0 0.6 gather_fusion
  89.8 0.8 slice.80
  (36 shorter events, 1.9 us)
Async XLA Ops:
  0.6 3.4 %copy-start = (bf16[1920,128]{1,0:T(8,128)(2,1)S(1)}, bf16[1920,128]{1,0:T(8,128)(2,1)}, u32[]{:S(2)}) copy-start(bf16[1920,128]{1,0:T(8,128)(2,1)} %shapes_ref.1) | copy-start | bytes 1474564
  0.6 4.4 %copy-start.3 = (s32[1920]{0:T(1024)S(1)}, s32[1920]{0:T(1024)}, u32[]{:S(2)}) copy-start(s32[1920]{0:T(1024)} %param.10) | copy-start | bytes 23044
  14.2 22.1 %copy-start.2 = (f32[1920,128]{1,0:T(8,128)S(1)}, f32[1920,128]{1,0:T(8,128)}, u32[]{:S(2)}) copy-start(f32[1920,128]{1,0:T(8,128)} %get-tuple-element.10) | copy-start | bytes 2949124
  16.5 53.1 %all-to-all-start = ((f32[128,3,128]{2,1,0:T(4,128)}), f32[128,3,128]{2,1,0:T(4,128)S(1)}, u32[]{:S(2)}, u32[]{:S(2)}) async-start(f32[128,3,128]{2,1,0:T(4,128)} %broadcast_in_dim.41), calls=%async_computation | async-start | bytes 524288 | tf_op jit(solution)/shard_map/all_to_all | solution.py:43
  36.4 10.4 %copy-start.1 = (bf16[1920,128]{1,0:T(8,128)(2,1)S(1)}, bf16[1920,128]{1,0:T(8,128)(2,1)}, u32[]{:S(2)}) copy-start(bf16[1920,128]{1,0:T(8,128)(2,1)} %shapes_ref.1) | copy-start | bytes 1474564
  36.5 30.7 %collective-permute-start.2 = (f32[480,128]{1,0:T(8,128)S(1)}, f32[480,128]{1,0:T(8,128)S(1)}, u32[]{:S(2)}, u32[]{:S(2)}) collective-permute-start(f32[480,128]{1,0:T(8,128)S(1)} %get-tuple-element.28), channel_id=1, source_target_pairs={{0,3},{1,0},{2,1},{3,2},{4,7},{5,4},{6,5},{7,6},{8,11},{9,8},{10,9... | collective-permute-start | bytes 737288 | tf_op jit(solution)/shard_map/ppermute | solution.py:129
  41.9 27.6 %collective-permute-start.1 = (f32[480,128]{1,0:T(8,128)S(1)}, f32[480,128]{1,0:T(8,128)S(1)}, u32[]{:S(2)}, u32[]{:S(2)}) collective-permute-start(f32[480,128]{1,0:T(8,128)S(1)} %get-tuple-element.29), channel_id=1, source_target_pairs={{0,2},{1,3},{2,0},{3,1},{4,6},{5,7},{6,4},{7,5},{8,10},{9,11},{10,... | collective-permute-start | bytes 737288 | tf_op jit(solution)/shard_map/ppermute | solution.py:129
  43.8 25.7 %collective-permute-start = (f32[480,128]{1,0:T(8,128)S(1)}, f32[480,128]{1,0:T(8,128)S(1)}, u32[]{:S(2)}, u32[]{:S(2)}) collective-permute-start(f32[480,128]{1,0:T(8,128)S(1)} %get-tuple-element.27), channel_id=1, source_target_pairs={{0,1},{1,2},{2,3},{3,0},{4,5},{5,6},{6,7},{7,4},{8,9},{9,10},{10,1... | collective-permute-start | bytes 737288 | tf_op jit(solution)/shard_map/ppermute | solution.py:129
  46.8 15.5 %collective-permute-start.4 = (bf16[1,128,128]{2,1,0:T(8,128)(2,1)S(1)}, bf16[1,128,128]{2,1,0:T(8,128)(2,1)S(1)}, u32[]{:S(2)}, u32[]{:S(2)}) collective-permute-start(bf16[1,128,128]{2,1,0:T(8,128)(2,1)S(1)} %get-tuple-element.31), channel_id=1, source_target_pairs={{4,0},{8,4},{12,8},{16,12},{20,16},{24,20},{28,24},{32,28},{36,32}... | collective-permute-start | bytes 98312 | tf_op jit(solution)/shard_map/ppermute | solution.py:22
  53.3 13.6 %collective-permute-start.3 = (bf16[1,128,128]{2,1,0:T(8,128)(2,1)S(1)}, bf16[1,128,128]{2,1,0:T(8,128)(2,1)S(1)}, u32[]{:S(2)}, u32[]{:S(2)}) collective-permute-start(bf16[1,128,128]{2,1,0:T(8,128)(2,1)S(1)} %get-tuple-element.30), channel_id=1, source_target_pairs={{0,4},{4,8},{8,12},{12,16},{16,20},{20,24},{24,28},{28,32},{32,36}... | collective-permute-start | bytes 98312 | tf_op jit(solution)/shard_map/ppermute | solution.py:20
  69.9 12.5 %collective-permute-start.7 = (bf16[496,128]{1,0:T(8,128)(2,1)S(1)}, bf16[496,128]{1,0:T(8,128)(2,1)S(1)}, u32[]{:S(2)}, u32[]{:S(2)}) collective-permute-start(bf16[496,128]{1,0:T(8,128)(2,1)S(1)} %maximum_maximum_fusion), channel_id=1, source_target_pairs={{0,3},{1,0},{2,1},{3,2},{4,7},{5,4},{6,5},{7,6},{8,11},{9,8},{10,9... | collective-permute-start | bytes 380936 | tf_op jit(solution)/shard_map/ppermute | solution.py:147
  71.8 13.6 %collective-permute-start.6 = (bf16[496,128]{1,0:T(8,128)(2,1)S(1)}, bf16[496,128]{1,0:T(8,128)(2,1)S(1)}, u32[]{:S(2)}, u32[]{:S(2)}) collective-permute-start(bf16[496,128]{1,0:T(8,128)(2,1)S(1)} %maximum_maximum_fusion), channel_id=1, source_target_pairs={{0,2},{1,3},{2,0},{3,1},{4,6},{5,7},{6,4},{7,5},{8,10},{9,11},{10,... | collective-permute-start | bytes 380936 | tf_op jit(solution)/shard_map/ppermute | solution.py:147
  80.3 8.6 %collective-permute-start.5 = (bf16[496,128]{1,0:T(8,128)(2,1)S(1)}, bf16[496,128]{1,0:T(8,128)(2,1)S(1)}, u32[]{:S(2)}, u32[]{:S(2)}) collective-permute-start(bf16[496,128]{1,0:T(8,128)(2,1)S(1)} %maximum_maximum_fusion), channel_id=1, source_target_pairs={{0,1},{1,2},{2,3},{3,0},{4,5},{5,6},{6,7},{7,4},{8,9},{9,10},{10,1... | collective-permute-start | bytes 380936 | tf_op jit(solution)/shard_map/ppermute | solution.py:147

commit v4 on v3

--- a/solution.py
+++ b/solution.py
@@ -4,6 +4,7 @@
 from jax.experimental import pallas as pl
 from jax.experimental.pallas import tpu as pltpu
 from jax.sharding import PartitionSpec as P
+
 
 FRAMES = 4096
 IMG_W = 128
@@ -42,15 +43,6 @@
     count = lax.axis_size(axis)
     copies = lax.all_to_all(jnp.broadcast_to(x[None], (count,) + x.shape), axis, 0, 0, tiled=False)
     return jnp.sum(copies, axis=0)
-
-
-def butterfly(x, axis):
-    count = lax.axis_size(axis)
-    bit = 1
-    while bit < count:
-        x = x + lax.ppermute(x, axis, [(i, i ^ bit) for i in range(count)])
-        bit *= 2
-    return x
 
 
 def fit_kernel(shapes_ref, shapes_t_ref, video_ref, valid_ref, basis_ref, data_ref, mode_ref):
@@ -160,5 +152,9 @@
 def solution(mesh):
     placed = (P("pix", "frm"), P("pix", None), P("pix"), P(), P(), P())
     return jax.shard_map(
-        body, mesh=mesh, in_specs=placed, out_specs=(P("pix", None), P(), P(), P()), check_vma=False
+        body,
+        mesh=mesh,
+        in_specs=placed,
+        out_specs=(P("pix", None), P(), P(), P()),
+        check_vma=False,
     )

time: 91.7 us -> 91.7 us (level)
  no operation moved by 1% of the time
where the time goes in v4:
time: 91.7 us; the launch traced here: 91.1 us
  starting transfers between devices  50.8 us (55%)
  waiting for transfers between devices  20.3 us (22%)
  Pallas kernels  7.13 us (8%)
  other arithmetic  6.82 us (7%)
  local copies, waits for them, and re-layouts  5.1 us (6%)
  between operations  0.98 us (1%)
    all_to_all x1, starting transfers between devices, sum_over(): lax.all_to_all(jnp.broadcast_to(x[None], (count,) + x.shape), axis, 0, 0,...  19.8 us
    ppermute x3, starting transfers between devices, body(): lax.ppermute(packet, 'frm', [(i, (i + s) % n_frm) for i in range(n_frm)])  12.4 us
    ppermute x3, starting transfers between devices, body(): lax.ppermute(send, 'frm', [(i, (i + s) % n_frm) for i in range(n_frm)])  10.3 us
    pallas_call x1, Pallas kernels, fit(): pl.pallas_call(fit_kernel, grid=(n_pixels // tile,), in_specs=[pl.BlockSp...  7.13 us
    ppermute x1, waiting for transfers between devices, with_halo(): lax.ppermute(head, axis, [((i + 1) % count, i) for i in range(ends)])  6.95 us
    ppermute x3, waiting for transfers between devices, body(): lax.ppermute(packet, 'frm', [(i, (i + s) % n_frm) for i in range(n_frm)])  6.54 us
    ppermute x1, starting transfers between devices, with_halo(): lax.ppermute(head, axis, [((i + 1) % count, i) for i in range(ends)])  6.45 us
    ppermute x1, waiting for transfers between devices, with_halo(): lax.ppermute(tail, axis, [(i, (i + 1) % count) for i in range(ends)])  4.56 us
  transfers between devices with their start and end apart: 9, of which 5 were waited for; matrix products, arithmetic and copies ran while one was open for 1% of the time, Pallas kernels for 0%

profile of v4, /device:TPU:6, one launch (start us, length us, event | category | flops | bytes accessed | tf_op | source)
XLA Modules:
  0.0 91.1 jit_solution(6684830612246420892)
XLA Ops:
  0.7 0.7 neg.16
  1.4 2.7 %sine_multiply_fusion = (f32[128,1024]{1,0:T(8,128)S(1)}, f32[128,1024]{1,0:T(8,128)S(1)}) fusion(f32[128]{0:T(128)} %param.13, f32[128]{0:T(128)} %param.11, f32[1024]{0:T(1024)S(1)} %get-tuple-element.39, f32[128]{0:T(128)S(1)} %neg.16), kind=kLoop, calls=%fused_computation.8 | loop fusion | flops 655360 | bytes 1054208 | tf_op jit(solution)/shard_map/mul | solution.py:104
  4.1 1.0 %copy.15 = bf16[1920,128]{0,1:T(8,128)(2,1)} copy(bf16[1920,128]{1,0:T(8,128)(2,1)S(1)} %copy-done) | data formatting | bytes 983040 | tf_op args[1]
  5.1 1.3 %broadcast_in_dim.56.valid_ref = f32[1920,1]{1,0:T(8,128)} reshape(f32[1920]{0:T(1024)S(1)} %convert_element_type.51) | data formatting | bytes 15360 | tf_op jit(solution)/shard_map/broadcast_in_dim | solution.py:91
  6.4 0.7 convert_element_type.53.basis_ref
  7.1 7.1 %shard_map.93 = (f32[1920,128]{1,0:T(8,128)}, f32[128,1024]{1,0:T(8,128)}) custom-call(bf16[1920,128]{1,0:T(8,128)(2,1)} %shapes_ref.1, bf16[128,1920]{1,0:T(8,128)(2,1)} %bitcast.47, bf16[1920,1024]{1,0:T(8,128)(2,1)} %video_ref.1, f32[1920,1]{1,0:T(8,128)} %broadcast_in_dim.56.valid_ref, bf16[128,1024]{1,0:T(8,128)(2,1)} %convert_element_type.53.basis_ref), custom_call_target="tpu_custom_call" | custom-call | flops 1509949440 | bytes 6946816 | tf_op jit(solution)/shard_map/pallas_call | solution.py:71
  14.2 1.5 %multiply_reduce_fusion.2 = (f32[128]{0:T(128)S(1)}, f32[128]{0:T(128)S(1)}, f32[128]{0:T(128)S(1)}) fusion(f32[128,1024]{1,0:T(8,128)S(1)} %get-tuple-element.12, f32[128,1024]{1,0:T(8,128)} %get-tuple-element.11, f32[1024]{0:T(1024)S(1)} %get-tuple-element.40, f32[128,1024]{1,0:T(8,128)S(1)} %get-tuple-element.9), kind=kLoop, calls=%fused_computation.7 | loop fusion | flops 1310336 | bytes 1578496 | tf_op jit(solution)/shard_map/reduce_sum | solution.py:31
  15.7 0.7 broadcast_in_dim.41
  16.5 19.8 %all-to-all-start = ((f32[128,3,128]{2,1,0:T(4,128)}), f32[128,3,128]{2,1,0:T(4,128)S(1)}, u32[]{:S(2)}, u32[]{:S(2)}) async-start(f32[128,3,128]{2,1,0:T(4,128)} %broadcast_in_dim.41), calls=%async_computation | async-start | bytes 524288 | tf_op jit(solution)/shard_map/all_to_all | solution.py:44
  36.5 5.3 %collective-permute-start.2 = (f32[480,128]{1,0:T(8,128)S(1)}, f32[480,128]{1,0:T(8,128)S(1)}, u32[]{:S(2)}, u32[]{:S(2)}) collective-permute-start(f32[480,128]{1,0:T(8,128)S(1)} %get-tuple-element.28), channel_id=1, source_target_pairs={{0,3},{1,0},{2,1},{3,2},{4,7},{5,4},{6,5},{7,6},{8,11},{9,8},{10,9... | collective-permute-start | bytes 737288 | tf_op jit(solution)/shard_map/ppermute | solution.py:121
  41.9 1.9 %collective-permute-start.1 = (f32[480,128]{1,0:T(8,128)S(1)}, f32[480,128]{1,0:T(8,128)S(1)}, u32[]{:S(2)}, u32[]{:S(2)}) collective-permute-start(f32[480,128]{1,0:T(8,128)S(1)} %get-tuple-element.29), channel_id=1, source_target_pairs={{0,2},{1,3},{2,0},{3,1},{4,6},{5,7},{6,4},{7,5},{8,10},{9,11},{10,... | collective-permute-start | bytes 737288 | tf_op jit(solution)/shard_map/ppermute | solution.py:121
  43.8 3.0 %collective-permute-start = (f32[480,128]{1,0:T(8,128)S(1)}, f32[480,128]{1,0:T(8,128)S(1)}, u32[]{:S(2)}, u32[]{:S(2)}) collective-permute-start(f32[480,128]{1,0:T(8,128)S(1)} %get-tuple-element.27), channel_id=1, source_target_pairs={{0,1},{1,2},{2,3},{3,0},{4,5},{5,6},{6,7},{7,4},{8,9},{9,10},{10,1... | collective-permute-start | bytes 737288 | tf_op jit(solution)/shard_map/ppermute | solution.py:121
  46.8 6.5 %collective-permute-start.4 = (bf16[1,128,128]{2,1,0:T(8,128)(2,1)S(1)}, bf16[1,128,128]{2,1,0:T(8,128)(2,1)S(1)}, u32[]{:S(2)}, u32[]{:S(2)}) collective-permute-start(bf16[1,128,128]{2,1,0:T(8,128)(2,1)S(1)} %get-tuple-element.31), channel_id=1, source_target_pairs={{4,0},{8,4},{12,8},{16,12},{20,16},{24,20},{28,24},{32,28},{36,32}... | collective-permute-start | bytes 98312 | tf_op jit(solution)/shard_map/ppermute | solution.py:23
  53.3 1.9 %collective-permute-start.3 = (bf16[1,128,128]{2,1,0:T(8,128)(2,1)S(1)}, bf16[1,128,128]{2,1,0:T(8,128)(2,1)S(1)}, u32[]{:S(2)}, u32[]{:S(2)}) collective-permute-start(bf16[1,128,128]{2,1,0:T(8,128)(2,1)S(1)} %get-tuple-element.30), channel_id=1, source_target_pairs={{0,4},{4,8},{8,12},{12,16},{16,20},{20,24},{24,28},{28,32},{32,36}... | collective-permute-start | bytes 98312 | tf_op jit(solution)/shard_map/ppermute | solution.py:21
  55.4 7.0 %collective-permute-done.4 = bf16[1,128,128]{2,1,0:T(8,128)(2,1)S(1)} collective-permute-done((bf16[1,128,128]{2,1,0:T(8,128)(2,1)S(1)}, bf16[1,128,128]{2,1,0:T(8,128)(2,1)S(1)}, u32[]{:S(2)}, u32[]{:S(2)}) %collective-permute-start.4) | collective-permute-done | bytes 32800 | tf_op jit(solution)/shard_map/ppermute | solution.py:23
  62.3 4.6 %collective-permute-done.3 = bf16[1,128,128]{2,1,0:T(8,128)(2,1)S(1)} collective-permute-done((bf16[1,128,128]{2,1,0:T(8,128)(2,1)S(1)}, bf16[1,128,128]{2,1,0:T(8,128)(2,1)S(1)}, u32[]{:S(2)}, u32[]{:S(2)}) %collective-permute-start.3) | collective-permute-done | bytes 32800 | tf_op jit(solution)/shard_map/ppermute | solution.py:21
  67.3 2.2 %collective-permute-done.1 = f32[480,128]{1,0:T(8,128)S(1)} collective-permute-done((f32[480,128]{1,0:T(8,128)S(1)}, f32[480,128]{1,0:T(8,128)S(1)}, u32[]{:S(2)}, u32[]{:S(2)}) %collective-permute-start.1) | collective-permute-done | bytes 245792 | tf_op jit(solution)/shard_map/ppermute | solution.py:121
  69.9 1.9 %collective-permute-start.7 = (bf16[496,128]{1,0:T(8,128)(2,1)S(1)}, bf16[496,128]{1,0:T(8,128)(2,1)S(1)}, u32[]{:S(2)}, u32[]{:S(2)}) collective-permute-start(bf16[496,128]{1,0:T(8,128)(2,1)S(1)} %maximum_maximum_fusion), channel_id=1, source_target_pairs={{0,3},{1,0},{2,1},{3,2},{4,7},{5,4},{6,5},{7,6},{8,11},{9,8},{10,9... | collective-permute-start | bytes 380936 | tf_op jit(solution)/shard_map/ppermute | solution.py:139
  71.8 8.5 %collective-permute-start.6 = (bf16[496,128]{1,0:T(8,128)(2,1)S(1)}, bf16[496,128]{1,0:T(8,128)(2,1)S(1)}, u32[]{:S(2)}, u32[]{:S(2)}) collective-permute-start(bf16[496,128]{1,0:T(8,128)(2,1)S(1)} %maximum_maximum_fusion), channel_id=1, source_target_pairs={{0,2},{1,3},{2,0},{3,1},{4,6},{5,7},{6,4},{7,5},{8,10},{9,11},{10,... | collective-permute-start | bytes 380936 | tf_op jit(solution)/shard_map/ppermute | solution.py:139
  80.3 1.9 %collective-permute-start.5 = (bf16[496,128]{1,0:T(8,128)(2,1)S(1)}, bf16[496,128]{1,0:T(8,128)(2,1)S(1)}, u32[]{:S(2)}, u32[]{:S(2)}) collective-permute-start(bf16[496,128]{1,0:T(8,128)(2,1)S(1)} %maximum_maximum_fusion), channel_id=1, source_target_pairs={{0,1},{1,2},{2,3},{3,0},{4,5},{5,6},{6,7},{7,4},{8,9},{9,10},{10,1... | collective-permute-start | bytes 380936 | tf_op jit(solution)/shard_map/ppermute | solution.py:139
  82.4 3.0 %collective-permute-done.6 = bf16[496,128]{1,0:T(8,128)(2,1)S(1)} collective-permute-done((bf16[496,128]{1,0:T(8,128)(2,1)S(1)}, bf16[496,128]{1,0:T(8,128)(2,1)S(1)}, u32[]{:S(2)}, u32[]{:S(2)}) %collective-permute-start.6) | collective-permute-done | bytes 127008 | tf_op jit(solution)/shard_map/ppermute | solution.py:139
  85.4 3.6 %collective-permute-done.5 = bf16[496,128]{1,0:T(8,128)(2,1)S(1)} collective-permute-done((bf16[496,128]{1,0:T(8,128)(2,1)S(1)}, bf16[496,128]{1,0:T(8,128)(2,1)S(1)}, u32[]{:S(2)}, u32[]{:S(2)}) %collective-permute-start.5) | collective-permute-done | bytes 127008 | tf_op jit(solution)/shard_map/ppermute | solution.py:139
  89.0 0.6 gather_fusion
  89.8 0.8 slice.80
  (36 shorter events, 1.9 us)
Async XLA Ops:
  0.6 3.4 %copy-start = (bf16[1920,128]{1,0:T(8,128)(2,1)S(1)}, bf16[1920,128]{1,0:T(8,128)(2,1)}, u32[]{:S(2)}) copy-start(bf16[1920,128]{1,0:T(8,128)(2,1)} %shapes_ref.1) | copy-start | bytes 1474564
  0.6 4.4 %copy-start.3 = (s32[1920]{0:T(1024)S(1)}, s32[1920]{0:T(1024)}, u32[]{:S(2)}) copy-start(s32[1920]{0:T(1024)} %param.10) | copy-start | bytes 23044
  14.2 22.1 %copy-start.2 = (f32[1920,128]{1,0:T(8,128)S(1)}, f32[1920,128]{1,0:T(8,128)}, u32[]{:S(2)}) copy-start(f32[1920,128]{1,0:T(8,128)} %get-tuple-element.10) | copy-start | bytes 2949124
  16.5 53.1 %all-to-all-start = ((f32[128,3,128]{2,1,0:T(4,128)}), f32[128,3,128]{2,1,0:T(4,128)S(1)}, u32[]{:S(2)}, u32[]{:S(2)}) async-start(f32[128,3,128]{2,1,0:T(4,128)} %broadcast_in_dim.41), calls=%async_computation | async-start | bytes 524288 | tf_op jit(solution)/shard_map/all_to_all | solution.py:44
  36.4 10.4 %copy-start.1 = (bf16[1920,128]{1,0:T(8,128)(2,1)S(1)}, bf16[1920,128]{1,0:T(8,128)(2,1)}, u32[]{:S(2)}) copy-start(bf16[1920,128]{1,0:T(8,128)(2,1)} %shapes_ref.1) | copy-start | bytes 1474564
  36.5 30.7 %collective-permute-start.2 = (f32[480,128]{1,0:T(8,128)S(1)}, f32[480,128]{1,0:T(8,128)S(1)}, u32[]{:S(2)}, u32[]{:S(2)}) collective-permute-start(f32[480,128]{1,0:T(8,128)S(1)} %get-tuple-element.28), channel_id=1, source_target_pairs={{0,3},{1,0},{2,1},{3,2},{4,7},{5,4},{6,5},{7,6},{8,11},{9,8},{10,9... | collective-permute-start | bytes 737288 | tf_op jit(solution)/shard_map/ppermute | solution.py:121
  41.9 27.6 %collective-permute-start.1 = (f32[480,128]{1,0:T(8,128)S(1)}, f32[480,128]{1,0:T(8,128)S(1)}, u32[]{:S(2)}, u32[]{:S(2)}) collective-permute-start(f32[480,128]{1,0:T(8,128)S(1)} %get-tuple-element.29), channel_id=1, source_target_pairs={{0,2},{1,3},{2,0},{3,1},{4,6},{5,7},{6,4},{7,5},{8,10},{9,11},{10,... | collective-permute-start | bytes 737288 | tf_op jit(solution)/shard_map/ppermute | solution.py:121
  43.8 25.7 %collective-permute-start = (f32[480,128]{1,0:T(8,128)S(1)}, f32[480,128]{1,0:T(8,128)S(1)}, u32[]{:S(2)}, u32[]{:S(2)}) collective-permute-start(f32[480,128]{1,0:T(8,128)S(1)} %get-tuple-element.27), channel_id=1, source_target_pairs={{0,1},{1,2},{2,3},{3,0},{4,5},{5,6},{6,7},{7,4},{8,9},{9,10},{10,1... | collective-permute-start | bytes 737288 | tf_op jit(solution)/shard_map/ppermute | solution.py:121
  46.8 15.5 %collective-permute-start.4 = (bf16[1,128,128]{2,1,0:T(8,128)(2,1)S(1)}, bf16[1,128,128]{2,1,0:T(8,128)(2,1)S(1)}, u32[]{:S(2)}, u32[]{:S(2)}) collective-permute-start(bf16[1,128,128]{2,1,0:T(8,128)(2,1)S(1)} %get-tuple-element.31), channel_id=1, source_target_pairs={{4,0},{8,4},{12,8},{16,12},{20,16},{24,20},{28,24},{32,28},{36,32}... | collective-permute-start | bytes 98312 | tf_op jit(solution)/shard_map/ppermute | solution.py:23
  53.3 13.6 %collective-permute-start.3 = (bf16[1,128,128]{2,1,0:T(8,128)(2,1)S(1)}, bf16[1,128,128]{2,1,0:T(8,128)(2,1)S(1)}, u32[]{:S(2)}, u32[]{:S(2)}) collective-permute-start(bf16[1,128,128]{2,1,0:T(8,128)(2,1)S(1)} %get-tuple-element.30), channel_id=1, source_target_pairs={{0,4},{4,8},{8,12},{12,16},{16,20},{20,24},{24,28},{28,32},{32,36}... | collective-permute-start | bytes 98312 | tf_op jit(solution)/shard_map/ppermute | solution.py:21
  69.9 12.5 %collective-permute-start.7 = (bf16[496,128]{1,0:T(8,128)(2,1)S(1)}, bf16[496,128]{1,0:T(8,128)(2,1)S(1)}, u32[]{:S(2)}, u32[]{:S(2)}) collective-permute-start(bf16[496,128]{1,0:T(8,128)(2,1)S(1)} %maximum_maximum_fusion), channel_id=1, source_target_pairs={{0,3},{1,0},{2,1},{3,2},{4,7},{5,4},{6,5},{7,6},{8,11},{9,8},{10,9... | collective-permute-start | bytes 380936 | tf_op jit(solution)/shard_map/ppermute | solution.py:139
  71.8 13.6 %collective-permute-start.6 = (bf16[496,128]{1,0:T(8,128)(2,1)S(1)}, bf16[496,128]{1,0:T(8,128)(2,1)S(1)}, u32[]{:S(2)}, u32[]{:S(2)}) collective-permute-start(bf16[496,128]{1,0:T(8,128)(2,1)S(1)} %maximum_maximum_fusion), channel_id=1, source_target_pairs={{0,2},{1,3},{2,0},{3,1},{4,6},{5,7},{6,4},{7,5},{8,10},{9,11},{10,... | collective-permute-start | bytes 380936 | tf_op jit(solution)/shard_map/ppermute | solution.py:139
  80.3 8.6 %collective-permute-start.5 = (bf16[496,128]{1,0:T(8,128)(2,1)S(1)}, bf16[496,128]{1,0:T(8,128)(2,1)S(1)}, u32[]{:S(2)}, u32[]{:S(2)}) collective-permute-start(bf16[496,128]{1,0:T(8,128)(2,1)S(1)} %maximum_maximum_fusion), channel_id=1, source_target_pairs={{0,1},{1,2},{2,3},{3,0},{4,5},{5,6},{6,7},{7,4},{8,9},{9,10},{10,1... | collective-permute-start | bytes 380936 | tf_op jit(solution)/shard_map/ppermute | solution.py:139

commit v5 on v3

--- a/solution.py
+++ b/solution.py
@@ -53,10 +53,10 @@
     return x
 
 
-def fit_kernel(shapes_ref, shapes_t_ref, video_ref, valid_ref, basis_ref, data_ref, mode_ref):
+def fit_kernel(shapes_ref, shapes_t_ref, video_ref, basis_ref, data_ref, mode_ref):
     step = pl.program_id(0)
     model = jnp.dot(shapes_ref[...], basis_ref[...], preferred_element_type=jnp.float32)
-    resid = (valid_ref[...] * (model - video_ref[...].astype(jnp.float32))).astype(jnp.bfloat16)
+    resid = (model - video_ref[...].astype(jnp.float32)).astype(jnp.bfloat16)
     data_ref[...] = lax.dot_general(
         resid, basis_ref[...], (((1,), (1,)), ((), ())), preferred_element_type=jnp.float32
     )
@@ -71,7 +71,7 @@
         mode_ref[...] += part
 
 
-def fit(shapes, video, valid, basis, tile=384):
+def fit(shapes, video, valid, basis, tile=640):
     n_pixels, n_modes = shapes.shape
     n_frames = video.shape[1]
     flops = 3 * 2 * n_pixels * n_modes * n_frames
@@ -83,7 +83,6 @@
             pl.BlockSpec((tile, n_modes), lambda i: (i, 0)),
             pl.BlockSpec((n_modes, tile), lambda i: (0, i)),
             pl.BlockSpec((tile, n_frames), lambda i: (i, 0)),
-            pl.BlockSpec((tile, 1), lambda i: (i, 0)),
             pl.BlockSpec((n_modes, n_frames), lambda i: (0, 0)),
         ],
         out_specs=[
@@ -96,7 +95,7 @@
         ],
         compiler_params=pltpu.CompilerParams(dimension_semantics=("arbitrary",)),
         cost_estimate=pl.CostEstimate(flops=flops, bytes_accessed=moved, transcendentals=0),
-    )(shapes, shapes.T, video, valid.astype(jnp.float32)[:, None], basis)
+    )(shapes, (shapes * valid[:, None].astype(shapes.dtype)).T, video, basis)
 
 
 def body(video, shapes, valid, omega, damping, phase):
@@ -118,7 +117,7 @@
     padded = with_halo(grid, (("pix", 0),), 1).astype(jnp.float32)
 
     data_raw, mode_raw = fit(shapes, video, valid, basis)
-    data_part = scale * data_raw
+    data_part = scale * data_raw * valid[:, None].astype(jnp.float32)
     local_terms = mode_terms(scale * mode_raw, cosine, sine, times)
     n_pixels, n_modes = data_part.shape
     quarter = n_pixels // n_frm

time: 91.7 us -> 89.6 us (0.977)
  local copies, waits for them, and re-layouts: 5.1 us -> 3.09 us
  other arithmetic: 6.82 us -> 7.89 us
  Pallas kernels: 7.13 us -> 6.21 us
    broadcast_in_dim x1 -> x0, local copies, waits for them, and re-layouts: 1.27 us -> none  [fit(): valid.astype(jnp.float32)[:, None]]
    pallas_call x1, Pallas kernels: 7.13 us -> 6.21 us  [fit(): pl.pallas_call(fit_kernel, grid=(n_pixels // tile,), in_specs=[pl.BlockSp...]
where the time goes in v5:
time: 89.6 us; the launch traced here: 89.1 us
  starting transfers between devices  50.7 us (57%)
  waiting for transfers between devices  20.2 us (23%)
  other arithmetic  7.89 us (9%)
  Pallas kernels  6.21 us (7%)
  local copies, waits for them, and re-layouts  3.09 us (3%)
  between operations  1 us (1%)
    all_to_all x1, starting transfers between devices, sum_over(): lax.all_to_all(jnp.broadcast_to(x[None], (count,) + x.shape), axis, 0, 0,...  19.8 us
    ppermute x3, starting transfers between devices, body(): lax.ppermute(packet, 'frm', [(i, (i + s) % n_frm) for i in range(n_frm)])  12.3 us
    ppermute x3, starting transfers between devices, body(): lax.ppermute(send, 'frm', [(i, (i + s) % n_frm) for i in range(n_frm)])  10.3 us
    ppermute x1, waiting for transfers between devices, with_halo(): lax.ppermute(head, axis, [((i + 1) % count, i) for i in range(ends)])  6.75 us
    ppermute x3, waiting for transfers between devices, body(): lax.ppermute(packet, 'frm', [(i, (i + s) % n_frm) for i in range(n_frm)])  6.54 us
    ppermute x1, starting transfers between devices, with_halo(): lax.ppermute(head, axis, [((i + 1) % count, i) for i in range(ends)])  6.45 us
    pallas_call x1, Pallas kernels, fit(): pl.pallas_call(fit_kernel, grid=(n_pixels // tile,), in_specs=[pl.BlockSp...  6.21 us
    ppermute x1, waiting for transfers between devices, with_halo(): lax.ppermute(tail, axis, [(i, (i + 1) % count) for i in range(ends)])  4.45 us
  transfers between devices with their start and end apart: 9, of which 5 were waited for; matrix products, arithmetic and copies ran while one was open for 1% of the time, Pallas kernels for 0%

profile of v5, /device:TPU:6, one launch (start us, length us, event | category | flops | bytes accessed | tf_op | source)
XLA Modules:
  0.0 89.1 jit_solution(4746365522619467637)
XLA Ops:
  0.7 0.7 neg.16
  1.4 2.7 %sine_multiply_fusion = (f32[128,1024]{1,0:T(8,128)S(1)}, f32[128,1024]{1,0:T(8,128)S(1)}) fusion(f32[128]{0:T(128)} %param.13, f32[128]{0:T(128)} %param.11, f32[1024]{0:T(1024)S(1)} %get-tuple-element.39, f32[128]{0:T(128)S(1)} %neg.16), kind=kLoop, calls=%fused_computation.8 | loop fusion | flops 655360 | bytes 1054208 | tf_op jit(solution)/shard_map/mul | solution.py:111
  4.4 0.7 convert_element_type.58.basis_ref
  5.1 0.8 multiply_bitcast_fusion.shapes_t_ref
  5.9 6.2 %shard_map.93 = (f32[1920,128]{1,0:T(8,128)}, f32[128,1024]{1,0:T(8,128)}) custom-call(bf16[1920,128]{1,0:T(8,128)(2,1)} %shapes_ref.1, bf16[128,1920]{1,0:T(8,128)(2,1)} %multiply_bitcast_fusion.shapes_t_ref, bf16[1920,1024]{1,0:T(8,128)(2,1)} %video_ref.1, bf16[128,1024]{1,0:T(8,128)(2,1)} %convert_element_type.58.basis_ref), custom_call_target="tpu_custom_call" | custom-call | flops 1509949440 | bytes 6946816 | tf_op jit(solution)/shard_map/pallas_call | solution.py:79
  12.1 1.5 %multiply_reduce_fusion.2 = (f32[128]{0:T(128)S(1)}, f32[128]{0:T(128)S(1)}, f32[128]{0:T(128)S(1)}) fusion(f32[128,1024]{1,0:T(8,128)S(1)} %get-tuple-element.12, f32[128,1024]{1,0:T(8,128)} %get-tuple-element.11, f32[1024]{0:T(1024)S(1)} %get-tuple-element.40, f32[128,1024]{1,0:T(8,128)S(1)} %get-tuple-element.9), kind=kLoop, calls=%fused_computation.7 | loop fusion | flops 1310336 | bytes 1578496 | tf_op jit(solution)/shard_map/reduce_sum | solution.py:30
  13.6 0.7 broadcast_in_dim.21
  14.4 19.8 %all-to-all-start = ((f32[128,3,128]{2,1,0:T(4,128)}), f32[128,3,128]{2,1,0:T(4,128)S(1)}, u32[]{:S(2)}, u32[]{:S(2)}) async-start(f32[128,3,128]{2,1,0:T(4,128)} %broadcast_in_dim.21), calls=%async_computation | async-start | bytes 524288 | tf_op jit(solution)/shard_map/all_to_all | solution.py:43
  34.7 5.3 %collective-permute-start.2 = (f32[480,128]{1,0:T(8,128)S(1)}, f32[480,128]{1,0:T(8,128)S(1)}, u32[]{:S(2)}, u32[]{:S(2)}) collective-permute-start(f32[480,128]{1,0:T(8,128)S(1)} %get-tuple-element.28), channel_id=1, source_target_pairs={{0,3},{1,0},{2,1},{3,2},{4,7},{5,4},{6,5},{7,6},{8,11},{9,8},{10,9... | collective-permute-start | bytes 737288 | tf_op jit(solution)/shard_map/ppermute | solution.py:128
  40.0 1.9 %collective-permute-start.1 = (f32[480,128]{1,0:T(8,128)S(1)}, f32[480,128]{1,0:T(8,128)S(1)}, u32[]{:S(2)}, u32[]{:S(2)}) collective-permute-start(f32[480,128]{1,0:T(8,128)S(1)} %get-tuple-element.29), channel_id=1, source_target_pairs={{0,2},{1,3},{2,0},{3,1},{4,6},{5,7},{6,4},{7,5},{8,10},{9,11},{10,... | collective-permute-start | bytes 737288 | tf_op jit(solution)/shard_map/ppermute | solution.py:128
  42.0 3.0 %collective-permute-start = (f32[480,128]{1,0:T(8,128)S(1)}, f32[480,128]{1,0:T(8,128)S(1)}, u32[]{:S(2)}, u32[]{:S(2)}) collective-permute-start(f32[480,128]{1,0:T(8,128)S(1)} %get-tuple-element.27), channel_id=1, source_target_pairs={{0,1},{1,2},{2,3},{3,0},{4,5},{5,6},{6,7},{7,4},{8,9},{9,10},{10,1... | collective-permute-start | bytes 737288 | tf_op jit(solution)/shard_map/ppermute | solution.py:128
  45.0 6.5 %collective-permute-start.4 = (bf16[1,128,128]{2,1,0:T(8,128)(2,1)S(1)}, bf16[1,128,128]{2,1,0:T(8,128)(2,1)S(1)}, u32[]{:S(2)}, u32[]{:S(2)}) collective-permute-start(bf16[1,128,128]{2,1,0:T(8,128)(2,1)S(1)} %get-tuple-element.31), channel_id=1, source_target_pairs={{4,0},{8,4},{12,8},{16,12},{20,16},{24,20},{28,24},{32,28},{36,32}... | collective-permute-start | bytes 98312 | tf_op jit(solution)/shard_map/ppermute | solution.py:22
  51.5 1.9 %collective-permute-start.3 = (bf16[1,128,128]{2,1,0:T(8,128)(2,1)S(1)}, bf16[1,128,128]{2,1,0:T(8,128)(2,1)S(1)}, u32[]{:S(2)}, u32[]{:S(2)}) collective-permute-start(bf16[1,128,128]{2,1,0:T(8,128)(2,1)S(1)} %get-tuple-element.30), channel_id=1, source_target_pairs={{0,4},{4,8},{8,12},{12,16},{16,20},{20,24},{24,28},{28,32},{32,36}... | collective-permute-start | bytes 98312 | tf_op jit(solution)/shard_map/ppermute | solution.py:20
  53.6 6.7 %collective-permute-done.4 = bf16[1,128,128]{2,1,0:T(8,128)(2,1)S(1)} collective-permute-done((bf16[1,128,128]{2,1,0:T(8,128)(2,1)S(1)}, bf16[1,128,128]{2,1,0:T(8,128)(2,1)S(1)}, u32[]{:S(2)}, u32[]{:S(2)}) %collective-permute-start.4) | collective-permute-done | bytes 32800 | tf_op jit(solution)/shard_map/ppermute | solution.py:22
  60.3 4.4 %collective-permute-done.3 = bf16[1,128,128]{2,1,0:T(8,128)(2,1)S(1)} collective-permute-done((bf16[1,128,128]{2,1,0:T(8,128)(2,1)S(1)}, bf16[1,128,128]{2,1,0:T(8,128)(2,1)S(1)}, u32[]{:S(2)}, u32[]{:S(2)}) %collective-permute-start.3) | collective-permute-done | bytes 32800 | tf_op jit(solution)/shard_map/ppermute | solution.py:20
  65.1 2.4 %collective-permute-done.1 = f32[480,128]{1,0:T(8,128)S(1)} collective-permute-done((f32[480,128]{1,0:T(8,128)S(1)}, f32[480,128]{1,0:T(8,128)S(1)}, u32[]{:S(2)}, u32[]{:S(2)}) %collective-permute-start.1) | collective-permute-done | bytes 245792 | tf_op jit(solution)/shard_map/ppermute | solution.py:128
  67.9 1.9 %collective-permute-start.7 = (bf16[496,128]{1,0:T(8,128)(2,1)S(1)}, bf16[496,128]{1,0:T(8,128)(2,1)S(1)}, u32[]{:S(2)}, u32[]{:S(2)}) collective-permute-start(bf16[496,128]{1,0:T(8,128)(2,1)S(1)} %maximum_maximum_fusion), channel_id=1, source_target_pairs={{0,3},{1,0},{2,1},{3,2},{4,7},{5,4},{6,5},{7,6},{8,11},{9,8},{10,9... | collective-permute-start | bytes 380936 | tf_op jit(solution)/shard_map/ppermute | solution.py:146
  69.9 8.4 %collective-permute-start.6 = (bf16[496,128]{1,0:T(8,128)(2,1)S(1)}, bf16[496,128]{1,0:T(8,128)(2,1)S(1)}, u32[]{:S(2)}, u32[]{:S(2)}) collective-permute-start(bf16[496,128]{1,0:T(8,128)(2,1)S(1)} %maximum_maximum_fusion), channel_id=1, source_target_pairs={{0,2},{1,3},{2,0},{3,1},{4,6},{5,7},{6,4},{7,5},{8,10},{9,11},{10,... | collective-permute-start | bytes 380936 | tf_op jit(solution)/shard_map/ppermute | solution.py:146
  78.3 1.9 %collective-permute-start.5 = (bf16[496,128]{1,0:T(8,128)(2,1)S(1)}, bf16[496,128]{1,0:T(8,128)(2,1)S(1)}, u32[]{:S(2)}, u32[]{:S(2)}) collective-permute-start(bf16[496,128]{1,0:T(8,128)(2,1)S(1)} %maximum_maximum_fusion), channel_id=1, source_target_pairs={{0,1},{1,2},{2,3},{3,0},{4,5},{5,6},{6,7},{7,4},{8,9},{9,10},{10,1... | collective-permute-start | bytes 380936 | tf_op jit(solution)/shard_map/ppermute | solution.py:146
  80.4 3.0 %collective-permute-done.6 = bf16[496,128]{1,0:T(8,128)(2,1)S(1)} collective-permute-done((bf16[496,128]{1,0:T(8,128)(2,1)S(1)}, bf16[496,128]{1,0:T(8,128)(2,1)S(1)}, u32[]{:S(2)}, u32[]{:S(2)}) %collective-permute-start.6) | collective-permute-done | bytes 127008 | tf_op jit(solution)/shard_map/ppermute | solution.py:146
  83.3 3.6 %collective-permute-done.5 = bf16[496,128]{1,0:T(8,128)(2,1)S(1)} collective-permute-done((bf16[496,128]{1,0:T(8,128)(2,1)S(1)}, bf16[496,128]{1,0:T(8,128)(2,1)S(1)}, u32[]{:S(2)}, u32[]{:S(2)}) %collective-permute-start.5) | collective-permute-done | bytes 127008 | tf_op jit(solution)/shard_map/ppermute | solution.py:146
  87.0 0.6 gather_fusion
  87.8 0.8 slice.80
  88.6 0.5 slice_bitcast_fusion.2
  (37 shorter events, 1.8 us)
Async XLA Ops:
  0.6 3.4 %copy-start = (bf16[1920,128]{1,0:T(8,128)(2,1)S(1)}, bf16[1920,128]{1,0:T(8,128)(2,1)}, u32[]{:S(2)}) copy-start(bf16[1920,128]{1,0:T(8,128)(2,1)} %shapes_ref.1) | copy-start | bytes 1474564
  0.6 3.7 %copy-start.3 = (s32[1920]{0:T(1024)S(1)}, s32[1920]{0:T(1024)}, u32[]{:S(2)}) copy-start(s32[1920]{0:T(1024)} %param.10) | copy-start | bytes 23044
  12.1 22.1 %copy-start.2 = (f32[1920,128]{1,0:T(8,128)S(1)}, f32[1920,128]{1,0:T(8,128)}, u32[]{:S(2)}) copy-start(f32[1920,128]{1,0:T(8,128)} %get-tuple-element.10) | copy-start | bytes 2949124
  14.4 53.3 %all-to-all-start = ((f32[128,3,128]{2,1,0:T(4,128)}), f32[128,3,128]{2,1,0:T(4,128)S(1)}, u32[]{:S(2)}, u32[]{:S(2)}) async-start(f32[128,3,128]{2,1,0:T(4,128)} %broadcast_in_dim.21), calls=%async_computation | async-start | bytes 524288 | tf_op jit(solution)/shard_map/all_to_all | solution.py:43
  34.6 10.4 %copy-start.1 = (bf16[1920,128]{1,0:T(8,128)(2,1)S(1)}, bf16[1920,128]{1,0:T(8,128)(2,1)}, u32[]{:S(2)}) copy-start(bf16[1920,128]{1,0:T(8,128)(2,1)} %shapes_ref.1) | copy-start | bytes 1474564
  34.7 30.4 %collective-permute-start.2 = (f32[480,128]{1,0:T(8,128)S(1)}, f32[480,128]{1,0:T(8,128)S(1)}, u32[]{:S(2)}, u32[]{:S(2)}) collective-permute-start(f32[480,128]{1,0:T(8,128)S(1)} %get-tuple-element.28), channel_id=1, source_target_pairs={{0,3},{1,0},{2,1},{3,2},{4,7},{5,4},{6,5},{7,6},{8,11},{9,8},{10,9... | collective-permute-start | bytes 737288 | tf_op jit(solution)/shard_map/ppermute | solution.py:128
  40.0 27.5 %collective-permute-start.1 = (f32[480,128]{1,0:T(8,128)S(1)}, f32[480,128]{1,0:T(8,128)S(1)}, u32[]{:S(2)}, u32[]{:S(2)}) collective-permute-start(f32[480,128]{1,0:T(8,128)S(1)} %get-tuple-element.29), channel_id=1, source_target_pairs={{0,2},{1,3},{2,0},{3,1},{4,6},{5,7},{6,4},{7,5},{8,10},{9,11},{10,... | collective-permute-start | bytes 737288 | tf_op jit(solution)/shard_map/ppermute | solution.py:128
  42.0 25.6 %collective-permute-start = (f32[480,128]{1,0:T(8,128)S(1)}, f32[480,128]{1,0:T(8,128)S(1)}, u32[]{:S(2)}, u32[]{:S(2)}) collective-permute-start(f32[480,128]{1,0:T(8,128)S(1)} %get-tuple-element.27), channel_id=1, source_target_pairs={{0,1},{1,2},{2,3},{3,0},{4,5},{5,6},{6,7},{7,4},{8,9},{9,10},{10,1... | collective-permute-start | bytes 737288 | tf_op jit(solution)/shard_map/ppermute | solution.py:128
  45.0 15.3 %collective-permute-start.4 = (bf16[1,128,128]{2,1,0:T(8,128)(2,1)S(1)}, bf16[1,128,128]{2,1,0:T(8,128)(2,1)S(1)}, u32[]{:S(2)}, u32[]{:S(2)}) collective-permute-start(bf16[1,128,128]{2,1,0:T(8,128)(2,1)S(1)} %get-tuple-element.31), channel_id=1, source_target_pairs={{4,0},{8,4},{12,8},{16,12},{20,16},{24,20},{28,24},{32,28},{36,32}... | collective-permute-start | bytes 98312 | tf_op jit(solution)/shard_map/ppermute | solution.py:22
  51.5 13.3 %collective-permute-start.3 = (bf16[1,128,128]{2,1,0:T(8,128)(2,1)S(1)}, bf16[1,128,128]{2,1,0:T(8,128)(2,1)S(1)}, u32[]{:S(2)}, u32[]{:S(2)}) collective-permute-start(bf16[1,128,128]{2,1,0:T(8,128)(2,1)S(1)} %get-tuple-element.30), channel_id=1, source_target_pairs={{0,4},{4,8},{8,12},{12,16},{16,20},{20,24},{24,28},{28,32},{32,36}... | collective-permute-start | bytes 98312 | tf_op jit(solution)/shard_map/ppermute | solution.py:20
  67.9 12.4 %collective-permute-start.7 = (bf16[496,128]{1,0:T(8,128)(2,1)S(1)}, bf16[496,128]{1,0:T(8,128)(2,1)S(1)}, u32[]{:S(2)}, u32[]{:S(2)}) collective-permute-start(bf16[496,128]{1,0:T(8,128)(2,1)S(1)} %maximum_maximum_fusion), channel_id=1, source_target_pairs={{0,3},{1,0},{2,1},{3,2},{4,7},{5,4},{6,5},{7,6},{8,11},{9,8},{10,9... | collective-permute-start | bytes 380936 | tf_op jit(solution)/shard_map/ppermute | solution.py:146
  69.9 13.5 %collective-permute-start.6 = (bf16[496,128]{1,0:T(8,128)(2,1)S(1)}, bf16[496,128]{1,0:T(8,128)(2,1)S(1)}, u32[]{:S(2)}, u32[]{:S(2)}) collective-permute-start(bf16[496,128]{1,0:T(8,128)(2,1)S(1)} %maximum_maximum_fusion), channel_id=1, source_target_pairs={{0,2},{1,3},{2,0},{3,1},{4,6},{5,7},{6,4},{7,5},{8,10},{9,11},{10,... | collective-permute-start | bytes 380936 | tf_op jit(solution)/shard_map/ppermute | solution.py:146
  78.3 8.6 %collective-permute-start.5 = (bf16[496,128]{1,0:T(8,128)(2,1)S(1)}, bf16[496,128]{1,0:T(8,128)(2,1)S(1)}, u32[]{:S(2)}, u32[]{:S(2)}) collective-permute-start(bf16[496,128]{1,0:T(8,128)(2,1)S(1)} %maximum_maximum_fusion), channel_id=1, source_target_pairs={{0,1},{1,2},{2,3},{3,0},{4,5},{5,6},{6,7},{7,4},{8,9},{9,10},{10,1... | collective-permute-start | bytes 380936 | tf_op jit(solution)/shard_map/ppermute | solution.py:146

commit v6 on v5

--- a/solution.py
+++ b/solution.py
@@ -124,8 +124,9 @@
     parts = data_part.reshape(n_frm, quarter, n_modes)
     acc = jnp.take(parts, me, axis=0)
     for s in range(1, n_frm):
-        send = jnp.take(parts, (me + s) % n_frm, axis=0)
-        acc = acc + lax.ppermute(send, "frm", [(i, (i + s) % n_frm) for i in range(n_frm)])
+        send = jnp.take(parts, (me + s) % n_frm, axis=0).astype(jnp.bfloat16)
+        got_part = lax.ppermute(send, "frm", [(i, (i + s) % n_frm) for i in range(n_frm)])
+        acc = acc + got_part.astype(jnp.float32)
     terms = sum_over(local_terms, "pix")
 
     rows_total = rows_local * lax.axis_size("pix")

time: 89.6 us -> 81 us (0.904)
  waiting for transfers between devices: 20.2 us -> 12.8 us
  starting transfers between devices: 50.7 us -> 49.3 us
    ppermute x1, waiting for transfers between devices: 6.75 us -> 0.01 us  [with_halo(): lax.ppermute(head, axis, [((i + 1) % count, i) for i in range(ends)])]
    ppermute x1, waiting for transfers between devices: 4.45 us -> 0.01 us  [with_halo(): lax.ppermute(tail, axis, [(i, (i + 1) % count) for i in range(ends)])]
    ppermute x3, waiting for transfers between devices: 2.45 us -> 6.55 us  [body(): lax.ppermute(send, 'frm', [(i, (i + s) % n_frm) for i in range(n_frm)])]
    ppermute x3, starting transfers between devices: 12.3 us -> 10.1 us  [body(): lax.ppermute(packet, 'frm', [(i, (i + s) % n_frm) for i in range(n_frm)])]
  transfers between devices with their start and end apart: 9 -> 9, of which waited for: 5 -> 2; matrix products, arithmetic and copies ran while one was open for 1% -> 1% of each run, Pallas kernels for 0% -> 0%
where the time goes in v6:
time: 81 us; the launch traced here: 80.3 us
  starting transfers between devices  49.3 us (61%)
  waiting for transfers between devices  12.8 us (16%)
  other arithmetic  7.95 us (10%)
  Pallas kernels  6.21 us (8%)
  local copies, waits for them, and re-layouts  3.08 us (4%)
  between operations  1 us (1%)
    all_to_all x1, starting transfers between devices, sum_over(): lax.all_to_all(jnp.broadcast_to(x[None], (count,) + x.shape), axis, 0, 0,...  19.8 us
    ppermute x3, starting transfers between devices, body(): lax.ppermute(packet, 'frm', [(i, (i + s) % n_frm) for i in range(n_frm)])  10.1 us
    ppermute x3, starting transfers between devices, body(): lax.ppermute(send, 'frm', [(i, (i + s) % n_frm) for i in range(n_frm)])  10.1 us
    ppermute x1, starting transfers between devices, with_halo(): lax.ppermute(head, axis, [((i + 1) % count, i) for i in range(ends)])  7.29 us
    ppermute x3, waiting for transfers between devices, body(): lax.ppermute(send, 'frm', [(i, (i + s) % n_frm) for i in range(n_frm)])  6.55 us
    pallas_call x1, Pallas kernels, fit(): pl.pallas_call(fit_kernel, grid=(n_pixels // tile,), in_specs=[pl.BlockSp...  6.21 us
    ppermute x3, waiting for transfers between devices, body(): lax.ppermute(packet, 'frm', [(i, (i + s) % n_frm) for i in range(n_frm)])  6.21 us
    mul x1, other arithmetic, body(): envelope * jnp.sin(angle_all)  2.69 us
  transfers between devices with their start and end apart: 9, of which 2 were waited for; matrix products, arithmetic and copies ran while one was open for 1% of the time, Pallas kernels for 0%

profile of v6, /device:TPU:6, one launch (start us, length us, event | category | flops | bytes accessed | tf_op | source)
XLA Modules:
  0.0 80.3 jit_solution(3136787977863408331)
XLA Ops:
  0.7 0.7 neg.16
  1.4 2.7 %sine_multiply_fusion = (f32[128,1024]{1,0:T(8,128)S(1)}, f32[128,1024]{1,0:T(8,128)S(1)}) fusion(f32[128]{0:T(128)} %param.13, f32[128]{0:T(128)} %param.11, f32[1024]{0:T(1024)S(1)} %get-tuple-element.39, f32[128]{0:T(128)S(1)} %neg.16), kind=kLoop, calls=%fused_computation.8 | loop fusion | flops 655360 | bytes 1054208 | tf_op jit(solution)/shard_map/mul | solution.py:111
  4.1 0.3 copy.12
  4.4 0.7 convert_element_type.76.basis_ref
  5.1 0.8 %multiply_bitcast_fusion.shapes_t_ref = bf16[128,1920]{1,0:T(8,128)(2,1)} fusion(bf16[1920,128]{0,1:T(8,128)(2,1)S(1)} %copy.12, bf16[1920]{0:T(1024)(128)(2,1)S(1)} %convert_element_type.74), kind=kLoop, calls=%fused_computation.15 | loop fusion | flops 245760 | bytes 986880 | tf_op jit(solution)/shard_map/transpose | solution.py:98
  5.9 6.2 %shard_map.93 = (f32[1920,128]{1,0:T(8,128)}, f32[128,1024]{1,0:T(8,128)}) custom-call(bf16[1920,128]{1,0:T(8,128)(2,1)} %shapes_ref.1, bf16[128,1920]{1,0:T(8,128)(2,1)} %multiply_bitcast_fusion.shapes_t_ref, bf16[1920,1024]{1,0:T(8,128)(2,1)} %video_ref.1, bf16[128,1024]{1,0:T(8,128)(2,1)} %convert_element_type.76.basis_ref), custom_call_target="tpu_custom_call" | custom-call | flops 1509949440 | bytes 6946816 | tf_op jit(solution)/shard_map/pallas_call | solution.py:79
  12.1 1.5 %multiply_reduce_fusion.2 = (f32[128]{0:T(128)S(1)}, f32[128]{0:T(128)S(1)}, f32[128]{0:T(128)S(1)}) fusion(f32[128,1024]{1,0:T(8,128)S(1)} %get-tuple-element.12, f32[128,1024]{1,0:T(8,128)} %get-tuple-element.11, f32[1024]{0:T(1024)S(1)} %get-tuple-element.40, f32[128,1024]{1,0:T(8,128)S(1)} %get-tuple-element.9), kind=kLoop, calls=%fused_computation.7 | loop fusion | flops 1310336 | bytes 1578496 | tf_op jit(solution)/shard_map/reduce_sum | solution.py:30
  13.6 0.7 broadcast_in_dim.21
  14.4 19.8 %all-to-all-start = ((f32[128,3,128]{2,1,0:T(4,128)}), f32[128,3,128]{2,1,0:T(4,128)S(1)}, u32[]{:S(2)}, u32[]{:S(2)}) async-start(f32[128,3,128]{2,1,0:T(4,128)} %broadcast_in_dim.21), calls=%async_computation | async-start | bytes 524288 | tf_op jit(solution)/shard_map/all_to_all | solution.py:43
  34.3 7.3 %collective-permute-start.4 = (bf16[1,128,128]{2,1,0:T(8,128)(2,1)S(1)}, bf16[1,128,128]{2,1,0:T(8,128)(2,1)S(1)}, u32[]{:S(2)}, u32[]{:S(2)}) collective-permute-start(bf16[1,128,128]{2,1,0:T(8,128)(2,1)S(1)} %get-tuple-element.31), channel_id=1, source_target_pairs={{4,0},{8,4},{12,8},{16,12},{20,16},{24,20},{28,24},{32,28},{36,32}... | collective-permute-start | bytes 98312 | tf_op jit(solution)/shard_map/ppermute | solution.py:22
  41.6 1.9 %collective-permute-start.3 = (bf16[1,128,128]{2,1,0:T(8,128)(2,1)S(1)}, bf16[1,128,128]{2,1,0:T(8,128)(2,1)S(1)}, u32[]{:S(2)}, u32[]{:S(2)}) collective-permute-start(bf16[1,128,128]{2,1,0:T(8,128)(2,1)S(1)} %get-tuple-element.30), channel_id=1, source_target_pairs={{0,4},{4,8},{8,12},{12,16},{16,20},{20,24},{24,28},{28,32},{32,36}... | collective-permute-start | bytes 98312 | tf_op jit(solution)/shard_map/ppermute | solution.py:20
  43.6 0.3 broadcast_multiply_fusion
  44.0 5.2 %collective-permute-start.2 = (bf16[480,128]{1,0:T(8,128)(2,1)S(1)}, bf16[480,128]{1,0:T(8,128)(2,1)S(1)}, u32[]{:S(2)}, u32[]{:S(2)}) collective-permute-start(bf16[480,128]{1,0:T(8,128)(2,1)S(1)} %get-tuple-element.28), channel_id=1, source_target_pairs={{0,3},{1,0},{2,1},{3,2},{4,7},{5,4},{6,5},{7,6},{8,11},{9,8},{10,9... | collective-permute-start | bytes 368648 | tf_op jit(solution)/shard_map/ppermute | solution.py:128
  49.2 1.9 %collective-permute-start.1 = (bf16[480,128]{1,0:T(8,128)(2,1)S(1)}, bf16[480,128]{1,0:T(8,128)(2,1)S(1)}, u32[]{:S(2)}, u32[]{:S(2)}) collective-permute-start(bf16[480,128]{1,0:T(8,128)(2,1)S(1)} %get-tuple-element.29), channel_id=1, source_target_pairs={{0,2},{1,3},{2,0},{3,1},{4,6},{5,7},{6,4},{7,5},{8,10},{9,11},{10,... | collective-permute-start | bytes 368648 | tf_op jit(solution)/shard_map/ppermute | solution.py:128
  51.1 3.0 %collective-permute-start = (bf16[480,128]{1,0:T(8,128)(2,1)S(1)}, bf16[480,128]{1,0:T(8,128)(2,1)S(1)}, u32[]{:S(2)}, u32[]{:S(2)}) collective-permute-start(bf16[480,128]{1,0:T(8,128)(2,1)S(1)} %get-tuple-element.27), channel_id=1, source_target_pairs={{0,1},{1,2},{2,3},{3,0},{4,5},{5,6},{6,7},{7,4},{8,9},{9,10},{10,1... | collective-permute-start | bytes 368648 | tf_op jit(solution)/shard_map/ppermute | solution.py:128
  54.4 0.2 fusion
  54.7 6.5 %collective-permute-done.1 = bf16[480,128]{1,0:T(8,128)(2,1)S(1)} collective-permute-done((bf16[480,128]{1,0:T(8,128)(2,1)S(1)}, bf16[480,128]{1,0:T(8,128)(2,1)S(1)}, u32[]{:S(2)}, u32[]{:S(2)}) %collective-permute-start.1) | collective-permute-done | bytes 122912 | tf_op jit(solution)/shard_map/ppermute | solution.py:128
  61.6 3.9 %collective-permute-start.7 = (bf16[496,128]{1,0:T(8,128)(2,1)S(1)}, bf16[496,128]{1,0:T(8,128)(2,1)S(1)}, u32[]{:S(2)}, u32[]{:S(2)}) collective-permute-start(bf16[496,128]{1,0:T(8,128)(2,1)S(1)} %maximum_maximum_fusion), channel_id=1, source_target_pairs={{0,3},{1,0},{2,1},{3,2},{4,7},{5,4},{6,5},{7,6},{8,11},{9,8},{10,9... | collective-permute-start | bytes 380936 | tf_op jit(solution)/shard_map/ppermute | solution.py:147
  65.5 2.3 %collective-permute-start.6 = (bf16[496,128]{1,0:T(8,128)(2,1)S(1)}, bf16[496,128]{1,0:T(8,128)(2,1)S(1)}, u32[]{:S(2)}, u32[]{:S(2)}) collective-permute-start(bf16[496,128]{1,0:T(8,128)(2,1)S(1)} %maximum_maximum_fusion), channel_id=1, source_target_pairs={{0,2},{1,3},{2,0},{3,1},{4,6},{5,7},{6,4},{7,5},{8,10},{9,11},{10,... | collective-permute-start | bytes 380936 | tf_op jit(solution)/shard_map/ppermute | solution.py:147
  67.9 3.9 %collective-permute-start.5 = (bf16[496,128]{1,0:T(8,128)(2,1)S(1)}, bf16[496,128]{1,0:T(8,128)(2,1)S(1)}, u32[]{:S(2)}, u32[]{:S(2)}) collective-permute-start(bf16[496,128]{1,0:T(8,128)(2,1)S(1)} %maximum_maximum_fusion), channel_id=1, source_target_pairs={{0,1},{1,2},{2,3},{3,0},{4,5},{5,6},{6,7},{7,4},{8,9},{9,10},{10,1... | collective-permute-start | bytes 380936 | tf_op jit(solution)/shard_map/ppermute | solution.py:147
  71.9 6.2 %collective-permute-done.6 = bf16[496,128]{1,0:T(8,128)(2,1)S(1)} collective-permute-done((bf16[496,128]{1,0:T(8,128)(2,1)S(1)}, bf16[496,128]{1,0:T(8,128)(2,1)S(1)}, u32[]{:S(2)}, u32[]{:S(2)}) %collective-permute-start.6) | collective-permute-done | bytes 127008 | tf_op jit(solution)/shard_map/ppermute | solution.py:147
  78.2 0.6 gather_fusion
  79.0 0.8 %slice.80 = bf16[4,480,128]{2,1,0:T(8,128)(2,1)} slice(bf16[4,496,128]{2,1,0:T(8,128)(2,1)S(1)} %broadcast_select_fusion), slice={[0:4], [0:480], [0:128]} | slice | bytes 983040 | tf_op jit(solution)/shard_map/slice | solution.py:150
  79.8 0.5 slice_bitcast_fusion.2
  (37 shorter events, 1.1 us)
Async XLA Ops:
  0.6 3.4 %copy-start = (bf16[1920,128]{1,0:T(8,128)(2,1)S(1)}, bf16[1920,128]{1,0:T(8,128)(2,1)}, u32[]{:S(2)}) copy-start(bf16[1920,128]{1,0:T(8,128)(2,1)} %shapes_ref.1) | copy-start | bytes 1474564
  0.6 3.7 %copy-start.3 = (s32[1920]{0:T(1024)S(1)}, s32[1920]{0:T(1024)}, u32[]{:S(2)}) copy-start(s32[1920]{0:T(1024)} %param.10) | copy-start | bytes 23044
  12.1 22.1 %copy-start.1 = (bf16[1920,128]{1,0:T(8,128)(2,1)S(1)}, bf16[1920,128]{1,0:T(8,128)(2,1)}, u32[]{:S(2)}) copy-start(bf16[1920,128]{1,0:T(8,128)(2,1)} %shapes_ref.1) | copy-start | bytes 1474564
  12.1 31.4 %copy-start.2 = (f32[1920,128]{1,0:T(8,128)S(1)}, f32[1920,128]{1,0:T(8,128)}, u32[]{:S(2)}) copy-start(f32[1920,128]{1,0:T(8,128)} %get-tuple-element.10) | copy-start | bytes 2949124
  14.4 46.9 %all-to-all-start = ((f32[128,3,128]{2,1,0:T(4,128)}), f32[128,3,128]{2,1,0:T(4,128)S(1)}, u32[]{:S(2)}, u32[]{:S(2)}) async-start(f32[128,3,128]{2,1,0:T(4,128)} %broadcast_in_dim.21), calls=%async_computation | async-start | bytes 524288 | tf_op jit(solution)/shard_map/all_to_all | solution.py:43
  34.3 20.0 %collective-permute-start.4 = (bf16[1,128,128]{2,1,0:T(8,128)(2,1)S(1)}, bf16[1,128,128]{2,1,0:T(8,128)(2,1)S(1)}, u32[]{:S(2)}, u32[]{:S(2)}) collective-permute-start(bf16[1,128,128]{2,1,0:T(8,128)(2,1)S(1)} %get-tuple-element.31), channel_id=1, source_target_pairs={{4,0},{8,4},{12,8},{16,12},{20,16},{24,20},{28,24},{32,28},{36,32}... | collective-permute-start | bytes 98312 | tf_op jit(solution)/shard_map/ppermute | solution.py:22
  41.6 12.8 %collective-permute-start.3 = (bf16[1,128,128]{2,1,0:T(8,128)(2,1)S(1)}, bf16[1,128,128]{2,1,0:T(8,128)(2,1)S(1)}, u32[]{:S(2)}, u32[]{:S(2)}) collective-permute-start(bf16[1,128,128]{2,1,0:T(8,128)(2,1)S(1)} %get-tuple-element.30), channel_id=1, source_target_pairs={{0,4},{4,8},{8,12},{12,16},{16,20},{20,24},{24,28},{28,32},{32,36}... | collective-permute-start | bytes 98312 | tf_op jit(solution)/shard_map/ppermute | solution.py:20
  44.0 10.7 %collective-permute-start.2 = (bf16[480,128]{1,0:T(8,128)(2,1)S(1)}, bf16[480,128]{1,0:T(8,128)(2,1)S(1)}, u32[]{:S(2)}, u32[]{:S(2)}) collective-permute-start(bf16[480,128]{1,0:T(8,128)(2,1)S(1)} %get-tuple-element.28), channel_id=1, source_target_pairs={{0,3},{1,0},{2,1},{3,2},{4,7},{5,4},{6,5},{7,6},{8,11},{9,8},{10,9... | collective-permute-start | bytes 368648 | tf_op jit(solution)/shard_map/ppermute | solution.py:128
  49.2 12.0 %collective-permute-start.1 = (bf16[480,128]{1,0:T(8,128)(2,1)S(1)}, bf16[480,128]{1,0:T(8,128)(2,1)S(1)}, u32[]{:S(2)}, u32[]{:S(2)}) collective-permute-start(bf16[480,128]{1,0:T(8,128)(2,1)S(1)} %get-tuple-element.29), channel_id=1, source_target_pairs={{0,2},{1,3},{2,0},{3,1},{4,6},{5,7},{6,4},{7,5},{8,10},{9,11},{10,... | collective-permute-start | bytes 368648 | tf_op jit(solution)/shard_map/ppermute | solution.py:128
  51.1 10.1 %collective-permute-start = (bf16[480,128]{1,0:T(8,128)(2,1)S(1)}, bf16[480,128]{1,0:T(8,128)(2,1)S(1)}, u32[]{:S(2)}, u32[]{:S(2)}) collective-permute-start(bf16[480,128]{1,0:T(8,128)(2,1)S(1)} %get-tuple-element.27), channel_id=1, source_target_pairs={{0,1},{1,2},{2,3},{3,0},{4,5},{5,6},{6,7},{7,4},{8,9},{9,10},{10,1... | collective-permute-start | bytes 368648 | tf_op jit(solution)/shard_map/ppermute | solution.py:128
  61.6 10.3 %collective-permute-start.7 = (bf16[496,128]{1,0:T(8,128)(2,1)S(1)}, bf16[496,128]{1,0:T(8,128)(2,1)S(1)}, u32[]{:S(2)}, u32[]{:S(2)}) collective-permute-start(bf16[496,128]{1,0:T(8,128)(2,1)S(1)} %maximum_maximum_fusion), channel_id=1, source_target_pairs={{0,3},{1,0},{2,1},{3,2},{4,7},{5,4},{6,5},{7,6},{8,11},{9,8},{10,9... | collective-permute-start | bytes 380936 | tf_op jit(solution)/shard_map/ppermute | solution.py:147
  65.5 12.6 %collective-permute-start.6 = (bf16[496,128]{1,0:T(8,128)(2,1)S(1)}, bf16[496,128]{1,0:T(8,128)(2,1)S(1)}, u32[]{:S(2)}, u32[]{:S(2)}) collective-permute-start(bf16[496,128]{1,0:T(8,128)(2,1)S(1)} %maximum_maximum_fusion), channel_id=1, source_target_pairs={{0,2},{1,3},{2,0},{3,1},{4,6},{5,7},{6,4},{7,5},{8,10},{9,11},{10,... | collective-permute-start | bytes 380936 | tf_op jit(solution)/shard_map/ppermute | solution.py:147
  67.9 10.3 %collective-permute-start.5 = (bf16[496,128]{1,0:T(8,128)(2,1)S(1)}, bf16[496,128]{1,0:T(8,128)(2,1)S(1)}, u32[]{:S(2)}, u32[]{:S(2)}) collective-permute-start(bf16[496,128]{1,0:T(8,128)(2,1)S(1)} %maximum_maximum_fusion), channel_id=1, source_target_pairs={{0,1},{1,2},{2,3},{3,0},{4,5},{5,6},{6,7},{7,4},{8,9},{9,10},{10,1... | collective-permute-start | bytes 380936 | tf_op jit(solution)/shard_map/ppermute | solution.py:147

commit v7 on v6

--- a/solution.py
+++ b/solution.py
@@ -4,6 +4,7 @@
 from jax.experimental import pallas as pl
 from jax.experimental.pallas import tpu as pltpu
 from jax.sharding import PartitionSpec as P
+
 
 FRAMES = 4096
 IMG_W = 128
@@ -42,15 +43,6 @@
     count = lax.axis_size(axis)
     copies = lax.all_to_all(jnp.broadcast_to(x[None], (count,) + x.shape), axis, 0, 0, tiled=False)
     return jnp.sum(copies, axis=0)
-
-
-def butterfly(x, axis):
-    count = lax.axis_size(axis)
-    bit = 1
-    while bit < count:
-        x = x + lax.ppermute(x, axis, [(i, i ^ bit) for i in range(count)])
-        bit *= 2
-    return x
 
 
 def fit_kernel(shapes_ref, shapes_t_ref, video_ref, basis_ref, data_ref, mode_ref):
@@ -160,5 +152,9 @@
 def solution(mesh):
     placed = (P("pix", "frm"), P("pix", None), P("pix"), P(), P(), P())
     return jax.shard_map(
-        body, mesh=mesh, in_specs=placed, out_specs=(P("pix", None), P(), P(), P()), check_vma=False
+        body,
+        mesh=mesh,
+        in_specs=placed,
+        out_specs=(P("pix", None), P(), P(), P()),
+        check_vma=False,
     )

time: 81 us -> 81 us (level)
  no operation moved by 1% of the time
where the time goes in v7:
time: 81 us; the launch traced here: 80.3 us
  starting transfers between devices  49.3 us (61%)
  waiting for transfers between devices  12.8 us (16%)
  other arithmetic  7.95 us (10%)
  Pallas kernels  6.21 us (8%)
  local copies, waits for them, and re-layouts  3.08 us (4%)
  between operations  1 us (1%)
    all_to_all x1, starting transfers between devices, sum_over(): lax.all_to_all(jnp.broadcast_to(x[None], (count,) + x.shape), axis, 0, 0,...  19.8 us
    ppermute x3, starting transfers between devices, body(): lax.ppermute(packet, 'frm', [(i, (i + s) % n_frm) for i in range(n_frm)])  10.1 us
    ppermute x3, starting transfers between devices, body(): lax.ppermute(send, 'frm', [(i, (i + s) % n_frm) for i in range(n_frm)])  10.1 us
    ppermute x1, starting transfers between devices, with_halo(): lax.ppermute(head, axis, [((i + 1) % count, i) for i in range(ends)])  7.29 us
    ppermute x3, waiting for transfers between devices, body(): lax.ppermute(send, 'frm', [(i, (i + s) % n_frm) for i in range(n_frm)])  6.55 us
    pallas_call x1, Pallas kernels, fit(): pl.pallas_call(fit_kernel, grid=(n_pixels // tile,), in_specs=[pl.BlockSp...  6.21 us
    ppermute x3, waiting for transfers between devices, body(): lax.ppermute(packet, 'frm', [(i, (i + s) % n_frm) for i in range(n_frm)])  6.21 us
    mul x1, other arithmetic, body(): envelope * jnp.sin(angle_all)  2.69 us
  transfers between devices with their start and end apart: 9, of which 2 were waited for; matrix products, arithmetic and copies ran while one was open for 1% of the time, Pallas kernels for 0%

profile of v7, /device:TPU:6, one launch (start us, length us, event | category | flops | bytes accessed | tf_op | source)
XLA Modules:
  0.0 80.3 jit_solution(3136787977863408331)
XLA Ops:
  0.7 0.7 neg.16
  1.4 2.7 %sine_multiply_fusion = (f32[128,1024]{1,0:T(8,128)S(1)}, f32[128,1024]{1,0:T(8,128)S(1)}) fusion(f32[128]{0:T(128)} %param.13, f32[128]{0:T(128)} %param.11, f32[1024]{0:T(1024)S(1)} %get-tuple-element.39, f32[128]{0:T(128)S(1)} %neg.16), kind=kLoop, calls=%fused_computation.8 | loop fusion | flops 655360 | bytes 1054208 | tf_op jit(solution)/shard_map/mul | solution.py:103
  4.1 0.3 copy.12
  4.4 0.7 convert_element_type.76.basis_ref
  5.1 0.8 %multiply_bitcast_fusion.shapes_t_ref = bf16[128,1920]{1,0:T(8,128)(2,1)} fusion(bf16[1920,128]{0,1:T(8,128)(2,1)S(1)} %copy.12, bf16[1920]{0:T(1024)(128)(2,1)S(1)} %convert_element_type.74), kind=kLoop, calls=%fused_computation.15 | loop fusion | flops 245760 | bytes 986880 | tf_op jit(solution)/shard_map/transpose | solution.py:90
  5.9 6.2 %shard_map.93 = (f32[1920,128]{1,0:T(8,128)}, f32[128,1024]{1,0:T(8,128)}) custom-call(bf16[1920,128]{1,0:T(8,128)(2,1)} %shapes_ref.1, bf16[128,1920]{1,0:T(8,128)(2,1)} %multiply_bitcast_fusion.shapes_t_ref, bf16[1920,1024]{1,0:T(8,128)(2,1)} %video_ref.1, bf16[128,1024]{1,0:T(8,128)(2,1)} %convert_element_type.76.basis_ref), custom_call_target="tpu_custom_call" | custom-call | flops 1509949440 | bytes 6946816 | tf_op jit(solution)/shard_map/pallas_call | solution.py:71
  12.1 1.5 %multiply_reduce_fusion.2 = (f32[128]{0:T(128)S(1)}, f32[128]{0:T(128)S(1)}, f32[128]{0:T(128)S(1)}) fusion(f32[128,1024]{1,0:T(8,128)S(1)} %get-tuple-element.12, f32[128,1024]{1,0:T(8,128)} %get-tuple-element.11, f32[1024]{0:T(1024)S(1)} %get-tuple-element.40, f32[128,1024]{1,0:T(8,128)S(1)} %get-tuple-element.9), kind=kLoop, calls=%fused_computation.7 | loop fusion | flops 1310336 | bytes 1578496 | tf_op jit(solution)/shard_map/reduce_sum | solution.py:31
  13.6 0.7 broadcast_in_dim.21
  14.4 19.8 %all-to-all-start = ((f32[128,3,128]{2,1,0:T(4,128)}), f32[128,3,128]{2,1,0:T(4,128)S(1)}, u32[]{:S(2)}, u32[]{:S(2)}) async-start(f32[128,3,128]{2,1,0:T(4,128)} %broadcast_in_dim.21), calls=%async_computation | async-start | bytes 524288 | tf_op jit(solution)/shard_map/all_to_all | solution.py:44
  34.3 7.3 %collective-permute-start.4 = (bf16[1,128,128]{2,1,0:T(8,128)(2,1)S(1)}, bf16[1,128,128]{2,1,0:T(8,128)(2,1)S(1)}, u32[]{:S(2)}, u32[]{:S(2)}) collective-permute-start(bf16[1,128,128]{2,1,0:T(8,128)(2,1)S(1)} %get-tuple-element.31), channel_id=1, source_target_pairs={{4,0},{8,4},{12,8},{16,12},{20,16},{24,20},{28,24},{32,28},{36,32}... | collective-permute-start | bytes 98312 | tf_op jit(solution)/shard_map/ppermute | solution.py:23
  41.6 1.9 %collective-permute-start.3 = (bf16[1,128,128]{2,1,0:T(8,128)(2,1)S(1)}, bf16[1,128,128]{2,1,0:T(8,128)(2,1)S(1)}, u32[]{:S(2)}, u32[]{:S(2)}) collective-permute-start(bf16[1,128,128]{2,1,0:T(8,128)(2,1)S(1)} %get-tuple-element.30), channel_id=1, source_target_pairs={{0,4},{4,8},{8,12},{12,16},{16,20},{20,24},{24,28},{28,32},{32,36}... | collective-permute-start | bytes 98312 | tf_op jit(solution)/shard_map/ppermute | solution.py:21
  43.6 0.3 broadcast_multiply_fusion
  44.0 5.2 %collective-permute-start.2 = (bf16[480,128]{1,0:T(8,128)(2,1)S(1)}, bf16[480,128]{1,0:T(8,128)(2,1)S(1)}, u32[]{:S(2)}, u32[]{:S(2)}) collective-permute-start(bf16[480,128]{1,0:T(8,128)(2,1)S(1)} %get-tuple-element.28), channel_id=1, source_target_pairs={{0,3},{1,0},{2,1},{3,2},{4,7},{5,4},{6,5},{7,6},{8,11},{9,8},{10,9... | collective-permute-start | bytes 368648 | tf_op jit(solution)/shard_map/ppermute | solution.py:120
  49.2 1.9 %collective-permute-start.1 = (bf16[480,128]{1,0:T(8,128)(2,1)S(1)}, bf16[480,128]{1,0:T(8,128)(2,1)S(1)}, u32[]{:S(2)}, u32[]{:S(2)}) collective-permute-start(bf16[480,128]{1,0:T(8,128)(2,1)S(1)} %get-tuple-element.29), channel_id=1, source_target_pairs={{0,2},{1,3},{2,0},{3,1},{4,6},{5,7},{6,4},{7,5},{8,10},{9,11},{10,... | collective-permute-start | bytes 368648 | tf_op jit(solution)/shard_map/ppermute | solution.py:120
  51.1 3.0 %collective-permute-start = (bf16[480,128]{1,0:T(8,128)(2,1)S(1)}, bf16[480,128]{1,0:T(8,128)(2,1)S(1)}, u32[]{:S(2)}, u32[]{:S(2)}) collective-permute-start(bf16[480,128]{1,0:T(8,128)(2,1)S(1)} %get-tuple-element.27), channel_id=1, source_target_pairs={{0,1},{1,2},{2,3},{3,0},{4,5},{5,6},{6,7},{7,4},{8,9},{9,10},{10,1... | collective-permute-start | bytes 368648 | tf_op jit(solution)/shard_map/ppermute | solution.py:120
  54.4 0.2 fusion
  54.7 6.5 %collective-permute-done.1 = bf16[480,128]{1,0:T(8,128)(2,1)S(1)} collective-permute-done((bf16[480,128]{1,0:T(8,128)(2,1)S(1)}, bf16[480,128]{1,0:T(8,128)(2,1)S(1)}, u32[]{:S(2)}, u32[]{:S(2)}) %collective-permute-start.1) | collective-permute-done | bytes 122912 | tf_op jit(solution)/shard_map/ppermute | solution.py:120
  61.6 3.9 %collective-permute-start.7 = (bf16[496,128]{1,0:T(8,128)(2,1)S(1)}, bf16[496,128]{1,0:T(8,128)(2,1)S(1)}, u32[]{:S(2)}, u32[]{:S(2)}) collective-permute-start(bf16[496,128]{1,0:T(8,128)(2,1)S(1)} %maximum_maximum_fusion), channel_id=1, source_target_pairs={{0,3},{1,0},{2,1},{3,2},{4,7},{5,4},{6,5},{7,6},{8,11},{9,8},{10,9... | collective-permute-start | bytes 380936 | tf_op jit(solution)/shard_map/ppermute | solution.py:139
  65.5 2.3 %collective-permute-start.6 = (bf16[496,128]{1,0:T(8,128)(2,1)S(1)}, bf16[496,128]{1,0:T(8,128)(2,1)S(1)}, u32[]{:S(2)}, u32[]{:S(2)}) collective-permute-start(bf16[496,128]{1,0:T(8,128)(2,1)S(1)} %maximum_maximum_fusion), channel_id=1, source_target_pairs={{0,2},{1,3},{2,0},{3,1},{4,6},{5,7},{6,4},{7,5},{8,10},{9,11},{10,... | collective-permute-start | bytes 380936 | tf_op jit(solution)/shard_map/ppermute | solution.py:139
  67.9 3.9 %collective-permute-start.5 = (bf16[496,128]{1,0:T(8,128)(2,1)S(1)}, bf16[496,128]{1,0:T(8,128)(2,1)S(1)}, u32[]{:S(2)}, u32[]{:S(2)}) collective-permute-start(bf16[496,128]{1,0:T(8,128)(2,1)S(1)} %maximum_maximum_fusion), channel_id=1, source_target_pairs={{0,1},{1,2},{2,3},{3,0},{4,5},{5,6},{6,7},{7,4},{8,9},{9,10},{10,1... | collective-permute-start | bytes 380936 | tf_op jit(solution)/shard_map/ppermute | solution.py:139
  71.9 6.2 %collective-permute-done.6 = bf16[496,128]{1,0:T(8,128)(2,1)S(1)} collective-permute-done((bf16[496,128]{1,0:T(8,128)(2,1)S(1)}, bf16[496,128]{1,0:T(8,128)(2,1)S(1)}, u32[]{:S(2)}, u32[]{:S(2)}) %collective-permute-start.6) | collective-permute-done | bytes 127008 | tf_op jit(solution)/shard_map/ppermute | solution.py:139
  78.2 0.6 gather_fusion
  79.0 0.8 %slice.80 = bf16[4,480,128]{2,1,0:T(8,128)(2,1)} slice(bf16[4,496,128]{2,1,0:T(8,128)(2,1)S(1)} %broadcast_select_fusion), slice={[0:4], [0:480], [0:128]} | slice | bytes 983040 | tf_op jit(solution)/shard_map/slice | solution.py:142
  79.8 0.5 slice_bitcast_fusion.2
  (37 shorter events, 1.1 us)
Async XLA Ops:
  0.6 3.4 %copy-start = (bf16[1920,128]{1,0:T(8,128)(2,1)S(1)}, bf16[1920,128]{1,0:T(8,128)(2,1)}, u32[]{:S(2)}) copy-start(bf16[1920,128]{1,0:T(8,128)(2,1)} %shapes_ref.1) | copy-start | bytes 1474564
  0.6 3.7 %copy-start.3 = (s32[1920]{0:T(1024)S(1)}, s32[1920]{0:T(1024)}, u32[]{:S(2)}) copy-start(s32[1920]{0:T(1024)} %param.10) | copy-start | bytes 23044
  12.1 22.1 %copy-start.1 = (bf16[1920,128]{1,0:T(8,128)(2,1)S(1)}, bf16[1920,128]{1,0:T(8,128)(2,1)}, u32[]{:S(2)}) copy-start(bf16[1920,128]{1,0:T(8,128)(2,1)} %shapes_ref.1) | copy-start | bytes 1474564
  12.1 31.4 %copy-start.2 = (f32[1920,128]{1,0:T(8,128)S(1)}, f32[1920,128]{1,0:T(8,128)}, u32[]{:S(2)}) copy-start(f32[1920,128]{1,0:T(8,128)} %get-tuple-element.10) | copy-start | bytes 2949124
  14.4 46.9 %all-to-all-start = ((f32[128,3,128]{2,1,0:T(4,128)}), f32[128,3,128]{2,1,0:T(4,128)S(1)}, u32[]{:S(2)}, u32[]{:S(2)}) async-start(f32[128,3,128]{2,1,0:T(4,128)} %broadcast_in_dim.21), calls=%async_computation | async-start | bytes 524288 | tf_op jit(solution)/shard_map/all_to_all | solution.py:44
  34.3 20.0 %collective-permute-start.4 = (bf16[1,128,128]{2,1,0:T(8,128)(2,1)S(1)}, bf16[1,128,128]{2,1,0:T(8,128)(2,1)S(1)}, u32[]{:S(2)}, u32[]{:S(2)}) collective-permute-start(bf16[1,128,128]{2,1,0:T(8,128)(2,1)S(1)} %get-tuple-element.31), channel_id=1, source_target_pairs={{4,0},{8,4},{12,8},{16,12},{20,16},{24,20},{28,24},{32,28},{36,32}... | collective-permute-start | bytes 98312 | tf_op jit(solution)/shard_map/ppermute | solution.py:23
  41.6 12.8 %collective-permute-start.3 = (bf16[1,128,128]{2,1,0:T(8,128)(2,1)S(1)}, bf16[1,128,128]{2,1,0:T(8,128)(2,1)S(1)}, u32[]{:S(2)}, u32[]{:S(2)}) collective-permute-start(bf16[1,128,128]{2,1,0:T(8,128)(2,1)S(1)} %get-tuple-element.30), channel_id=1, source_target_pairs={{0,4},{4,8},{8,12},{12,16},{16,20},{20,24},{24,28},{28,32},{32,36}... | collective-permute-start | bytes 98312 | tf_op jit(solution)/shard_map/ppermute | solution.py:21
  44.0 10.7 %collective-permute-start.2 = (bf16[480,128]{1,0:T(8,128)(2,1)S(1)}, bf16[480,128]{1,0:T(8,128)(2,1)S(1)}, u32[]{:S(2)}, u32[]{:S(2)}) collective-permute-start(bf16[480,128]{1,0:T(8,128)(2,1)S(1)} %get-tuple-element.28), channel_id=1, source_target_pairs={{0,3},{1,0},{2,1},{3,2},{4,7},{5,4},{6,5},{7,6},{8,11},{9,8},{10,9... | collective-permute-start | bytes 368648 | tf_op jit(solution)/shard_map/ppermute | solution.py:120
  49.2 12.0 %collective-permute-start.1 = (bf16[480,128]{1,0:T(8,128)(2,1)S(1)}, bf16[480,128]{1,0:T(8,128)(2,1)S(1)}, u32[]{:S(2)}, u32[]{:S(2)}) collective-permute-start(bf16[480,128]{1,0:T(8,128)(2,1)S(1)} %get-tuple-element.29), channel_id=1, source_target_pairs={{0,2},{1,3},{2,0},{3,1},{4,6},{5,7},{6,4},{7,5},{8,10},{9,11},{10,... | collective-permute-start | bytes 368648 | tf_op jit(solution)/shard_map/ppermute | solution.py:120
  51.1 10.1 %collective-permute-start = (bf16[480,128]{1,0:T(8,128)(2,1)S(1)}, bf16[480,128]{1,0:T(8,128)(2,1)S(1)}, u32[]{:S(2)}, u32[]{:S(2)}) collective-permute-start(bf16[480,128]{1,0:T(8,128)(2,1)S(1)} %get-tuple-element.27), channel_id=1, source_target_pairs={{0,1},{1,2},{2,3},{3,0},{4,5},{5,6},{6,7},{7,4},{8,9},{9,10},{10,1... | collective-permute-start | bytes 368648 | tf_op jit(solution)/shard_map/ppermute | solution.py:120
  61.6 10.3 %collective-permute-start.7 = (bf16[496,128]{1,0:T(8,128)(2,1)S(1)}, bf16[496,128]{1,0:T(8,128)(2,1)S(1)}, u32[]{:S(2)}, u32[]{:S(2)}) collective-permute-start(bf16[496,128]{1,0:T(8,128)(2,1)S(1)} %maximum_maximum_fusion), channel_id=1, source_target_pairs={{0,3},{1,0},{2,1},{3,2},{4,7},{5,4},{6,5},{7,6},{8,11},{9,8},{10,9... | collective-permute-start | bytes 380936 | tf_op jit(solution)/shard_map/ppermute | solution.py:139
  65.5 12.6 %collective-permute-start.6 = (bf16[496,128]{1,0:T(8,128)(2,1)S(1)}, bf16[496,128]{1,0:T(8,128)(2,1)S(1)}, u32[]{:S(2)}, u32[]{:S(2)}) collective-permute-start(bf16[496,128]{1,0:T(8,128)(2,1)S(1)} %maximum_maximum_fusion), channel_id=1, source_target_pairs={{0,2},{1,3},{2,0},{3,1},{4,6},{5,7},{6,4},{7,5},{8,10},{9,11},{10,... | collective-permute-start | bytes 380936 | tf_op jit(solution)/shard_map/ppermute | solution.py:139
  67.9 10.3 %collective-permute-start.5 = (bf16[496,128]{1,0:T(8,128)(2,1)S(1)}, bf16[496,128]{1,0:T(8,128)(2,1)S(1)}, u32[]{:S(2)}, u32[]{:S(2)}) collective-permute-start(bf16[496,128]{1,0:T(8,128)(2,1)S(1)} %maximum_maximum_fusion), channel_id=1, source_target_pairs={{0,1},{1,2},{2,3},{3,0},{4,5},{5,6},{6,7},{7,4},{8,9},{9,10},{10,1... | collective-permute-start | bytes 380936 | tf_op jit(solution)/shard_map/ppermute | solution.py:139

commit v8 on v5

--- a/solution.py
+++ b/solution.py
@@ -122,10 +122,9 @@
     n_pixels, n_modes = data_part.shape
     quarter = n_pixels // n_frm
     parts = data_part.reshape(n_frm, quarter, n_modes)
-    acc = jnp.take(parts, me, axis=0)
-    for s in range(1, n_frm):
-        send = jnp.take(parts, (me + s) % n_frm, axis=0)
-        acc = acc + lax.ppermute(send, "frm", [(i, (i + s) % n_frm) for i in range(n_frm)])
+    arrived = lax.all_to_all(parts.astype(jnp.bfloat16), "frm", 0, 0, tiled=False).astype(jnp.float32)
+    own_part = jnp.take(parts, me, axis=0)
+    acc = jnp.sum(lax.dynamic_update_index_in_dim(arrived, own_part, me, 0), axis=0)
     terms = sum_over(local_terms, "pix")
 
     rows_total = rows_local * lax.axis_size("pix")
@@ -141,11 +140,9 @@
     k = terms.shape[0]
     extra = (-(quarter + 2 * k)) % 16
     packet = jnp.concatenate([own, hi, lo, jnp.zeros((extra, n_modes), jnp.bfloat16)], axis=0)
-    got = [packet]
-    for s in range(1, n_frm):
-        got.append(lax.ppermute(packet, "frm", [(i, (i + s) % n_frm) for i in range(n_frm)]))
-    stacked = jnp.stack(got)
-    ordered = jnp.take(stacked, (me - jnp.arange(n_frm)) % n_frm, axis=0)
+    ordered = lax.all_to_all(
+        jnp.broadcast_to(packet[None], (n_frm,) + packet.shape), "frm", 0, 0, tiled=False
+    )
     shape_grad = ordered[:, :quarter].reshape(n_pixels, n_modes)
     pieces = ordered[:, quarter : quarter + k].astype(jnp.float32) + ordered[
         :, quarter + k : quarter + 2 * k

time: 89.6 us -> 88.4 us (0.987)
  starting transfers between devices: 50.7 us -> 33.6 us
  blocking collectives: 0 us -> 16.1 us
    ppermute x6 -> x0, starting transfers between devices: 22.5 us -> none  [the longest x3 12.3 us: body(): lax.ppermute(packet, 'frm', [(i, (i + s) % n_frm) for i in range(n_frm)])]
    all_to_all x0 -> x1, blocking collectives: none -> 16.1 us  [body(): lax.all_to_all(jnp.broadcast_to(packet[None], (n_frm,) + packet.shape), '...]
    all_to_all x0 -> x1, waiting for transfers between devices: none -> 13.5 us  [body(): lax.all_to_all(parts.astype(jnp.bfloat16), 'frm', 0, 0, tiled=False)]
    ppermute x6 -> x0, waiting for transfers between devices: 9 us -> none  [the longest x3 6.54 us: body(): lax.ppermute(packet, 'frm', [(i, (i + s) % n_frm) for i in range(n_frm)])]
    ppermute x1, waiting for transfers between devices: 6.75 us -> 0.01 us  [with_halo(): lax.ppermute(head, axis, [((i + 1) % count, i) for i in range(ends)])]
    all_to_all x1, waiting for transfers between devices: 0.01 us -> 6.07 us  [sum_over(): lax.all_to_all(jnp.broadcast_to(x[None], (count,) + x.shape), axis, 0, 0,...]
    all_to_all x0 -> x1, starting transfers between devices: none -> 4.55 us  [body(): lax.all_to_all(parts.astype(jnp.bfloat16), 'frm', 0, 0, tiled=False)]
    ppermute x1, waiting for transfers between devices: 4.45 us -> 0.01 us  [with_halo(): lax.ppermute(tail, axis, [(i, (i + 1) % count) for i in range(ends)])]
  transfers between devices with their start and end apart: 9 -> 4, of which waited for: 5 -> 2; matrix products, arithmetic and copies ran while one was open for 1% -> 2% of each run, Pallas kernels for 0% -> 0%
where the time goes in v8:
time: 88.4 us; the launch traced here: 87.3 us
  starting transfers between devices  33.6 us (38%)
  waiting for transfers between devices  19.5 us (22%)
  blocking collectives  16.1 us (18%)
  other arithmetic  8.49 us (10%)
  Pallas kernels  6.22 us (7%)
  local copies, waits for them, and re-layouts  2.52 us (3%)
    all_to_all x1, starting transfers between devices, sum_over(): lax.all_to_all(jnp.broadcast_to(x[None], (count,) + x.shape), axis, 0, 0,...  19.8 us
    all_to_all x1, blocking collectives, body(): lax.all_to_all(jnp.broadcast_to(packet[None], (n_frm,) + packet.shape), '...  16.1 us
    all_to_all x1, waiting for transfers between devices, body(): lax.all_to_all(parts.astype(jnp.bfloat16), 'frm', 0, 0, tiled=False)  13.5 us
    ppermute x1, starting transfers between devices, with_halo(): lax.ppermute(head, axis, [((i + 1) % count, i) for i in range(ends)])  7.29 us
    pallas_call x1, Pallas kernels, fit(): pl.pallas_call(fit_kernel, grid=(n_pixels // tile,), in_specs=[pl.BlockSp...  6.22 us
    all_to_all x1, waiting for transfers between devices, sum_over(): lax.all_to_all(jnp.broadcast_to(x[None], (count,) + x.shape), axis, 0, 0,...  6.07 us
    all_to_all x1, starting transfers between devices, body(): lax.all_to_all(parts.astype(jnp.bfloat16), 'frm', 0, 0, tiled=False)  4.55 us
    mul x1, other arithmetic, body(): envelope * jnp.sin(angle_all)  2.69 us
  transfers between devices with their start and end apart: 4, of which 2 were waited for; matrix products, arithmetic and copies ran while one was open for 2% of the time, Pallas kernels for 0%

profile of v8, /device:TPU:6, one launch (start us, length us, event | category | flops | bytes accessed | tf_op | source)
XLA Modules:
  0.0 87.3 jit_solution(8518720645336495023)
XLA Ops:
  0.7 0.7 neg.16
  1.4 2.7 %sine_multiply_fusion = (f32[128,1024]{1,0:T(8,128)S(1)}, f32[128,1024]{1,0:T(8,128)S(1)}) fusion(f32[128]{0:T(128)} %param.13, f32[128]{0:T(128)} %param.11, f32[1024]{0:T(1024)S(1)} %get-tuple-element.36, f32[128]{0:T(128)S(1)} %neg.16), kind=kLoop, calls=%fused_computation.7 | loop fusion | flops 655360 | bytes 1054208 | tf_op jit(solution)/shard_map/mul | solution.py:111
  4.1 0.3 copy.12
  4.4 0.7 convert_element_type.64.basis_ref
  5.1 0.8 multiply_bitcast_fusion.shapes_t_ref
  5.9 6.2 %shard_map.93 = (f32[1920,128]{1,0:T(8,128)}, f32[128,1024]{1,0:T(8,128)}) custom-call(bf16[1920,128]{1,0:T(8,128)(2,1)} %shapes_ref.1, bf16[128,1920]{1,0:T(8,128)(2,1)} %multiply_bitcast_fusion.shapes_t_ref, bf16[1920,1024]{1,0:T(8,128)(2,1)} %video_ref.1, bf16[128,1024]{1,0:T(8,128)(2,1)} %convert_element_type.64.basis_ref), custom_call_target="tpu_custom_call" | custom-call | flops 1509949440 | bytes 6946816 | tf_op jit(solution)/shard_map/pallas_call | solution.py:79
  12.2 1.5 %multiply_reduce_fusion.2 = (f32[128]{0:T(128)S(1)}, f32[128]{0:T(128)S(1)}, f32[128]{0:T(128)S(1)}) fusion(f32[128,1024]{1,0:T(8,128)S(1)} %get-tuple-element.12, f32[128,1024]{1,0:T(8,128)} %get-tuple-element.11, f32[1024]{0:T(1024)S(1)} %get-tuple-element.37, f32[128,1024]{1,0:T(8,128)S(1)} %get-tuple-element.9), kind=kLoop, calls=%fused_computation.6 | loop fusion | flops 1310336 | bytes 1578496 | tf_op jit(solution)/shard_map/reduce_sum | solution.py:30
  13.7 0.8 broadcast_in_dim.20
  14.4 19.8 %all-to-all-start.1 = ((f32[128,3,128]{2,1,0:T(4,128)}), f32[128,3,128]{2,1,0:T(4,128)S(1)}, u32[]{:S(2)}, u32[]{:S(2)}) async-start(f32[128,3,128]{2,1,0:T(4,128)} %broadcast_in_dim.20), calls=%async_computation.1 | async-start | bytes 524288 | tf_op jit(solution)/shard_map/all_to_all | solution.py:43
  34.3 7.3 %collective-permute-start.1 = (bf16[1,128,128]{2,1,0:T(8,128)(2,1)S(1)}, bf16[1,128,128]{2,1,0:T(8,128)(2,1)S(1)}, u32[]{:S(2)}, u32[]{:S(2)}) collective-permute-start(bf16[1,128,128]{2,1,0:T(8,128)(2,1)S(1)} %get-tuple-element.28), channel_id=1, source_target_pairs={{4,0},{8,4},{12,8},{16,12},{20,16},{24,20},{28,24},{32,28},{36,32}... | collective-permute-start | bytes 98312 | tf_op jit(solution)/shard_map/ppermute | solution.py:22
  41.6 1.9 %collective-permute-start = (bf16[1,128,128]{2,1,0:T(8,128)(2,1)S(1)}, bf16[1,128,128]{2,1,0:T(8,128)(2,1)S(1)}, u32[]{:S(2)}, u32[]{:S(2)}) collective-permute-start(bf16[1,128,128]{2,1,0:T(8,128)(2,1)S(1)} %get-tuple-element.27), channel_id=1, source_target_pairs={{0,4},{4,8},{8,12},{12,16},{16,20},{20,24},{24,28},{28,32},{32,36}... | collective-permute-start | bytes 98312 | tf_op jit(solution)/shard_map/ppermute | solution.py:20
  43.5 0.3 broadcast_multiply_fusion
  43.9 0.8 convert_element_type.66
  44.7 6.1 %all-to-all-done.1 = f32[128,3,128]{2,1,0:T(4,128)S(1)} async-done(((f32[128,3,128]{2,1,0:T(4,128)}), f32[128,3,128]{2,1,0:T(4,128)S(1)}, u32[]{:S(2)}, u32[]{:S(2)}) %all-to-all-start.1) | async-done | bytes 196640 | tf_op jit(solution)/shard_map/all_to_all | solution.py:43
  50.8 4.5 %all-to-all-start = ((bf16[4,480,128]{2,1,0:T(8,128)(2,1)}), bf16[4,480,128]{2,1,0:T(8,128)(2,1)S(1)}, u32[]{:S(2)}, u32[]{:S(2)}) async-start(bf16[4,480,128]{2,1,0:T(8,128)(2,1)} %convert_element_type.66), calls=%async_computation | async-start | bytes 983040 | tf_op jit(solution)/shard_map/all_to_all | solution.py:125
  55.3 0.1 pad.5.clone
  55.4 0.1 maximum_convert_fusion
  55.5 0.2 fusion
  55.8 0.1 reduce_sum.49
  55.9 13.5 %all-to-all-done = bf16[4,480,128]{2,1,0:T(8,128)(2,1)S(1)} async-done(((bf16[4,480,128]{2,1,0:T(8,128)(2,1)}), bf16[4,480,128]{2,1,0:T(8,128)(2,1)S(1)}, u32[]{:S(2)}, u32[]{:S(2)}) %all-to-all-start) | async-done | bytes 491552 | tf_op jit(solution)/shard_map/all_to_all | solution.py:125
  69.6 0.1 maximum_maximum_fusion
  69.8 16.1 %all_to_all.15 = bf16[4,496,128]{2,1,0:T(8,128)(2,1)S(1)} all-to-all(bf16[4,496,128]{2,1,0:T(8,128)(2,1)S(1)} %broadcast_in_dim.22), channel_id=1, replica_groups=mesh['pix'=128,'frm'=4] {'frm'}, dimensions={0} | all-to-all | bytes 1015808 | tf_op jit(solution)/shard_map/all_to_all | solution.py:143
  85.9 0.5 slice_bitcast_fusion.2
  86.5 0.8 slice.78
  (25 shorter events, 0.3 us)
Async XLA Ops:
  0.6 3.4 %copy-start = (bf16[1920,128]{1,0:T(8,128)(2,1)S(1)}, bf16[1920,128]{1,0:T(8,128)(2,1)}, u32[]{:S(2)}) copy-start(bf16[1920,128]{1,0:T(8,128)(2,1)} %shapes_ref.1) | copy-start | bytes 1474564
  0.6 3.7 %copy-start.3 = (s32[1920]{0:T(1024)S(1)}, s32[1920]{0:T(1024)}, u32[]{:S(2)}) copy-start(s32[1920]{0:T(1024)} %param.10) | copy-start | bytes 23044
  12.2 22.1 %copy-start.1 = (bf16[1920,128]{1,0:T(8,128)(2,1)S(1)}, bf16[1920,128]{1,0:T(8,128)(2,1)}, u32[]{:S(2)}) copy-start(bf16[1920,128]{1,0:T(8,128)(2,1)} %shapes_ref.1) | copy-start | bytes 1474564
  12.2 31.4 %copy-start.2 = (f32[1920,128]{1,0:T(8,128)S(1)}, f32[1920,128]{1,0:T(8,128)}, u32[]{:S(2)}) copy-start(f32[1920,128]{1,0:T(8,128)} %get-tuple-element.10) | copy-start | bytes 2949124
  14.4 36.3 %all-to-all-start.1 = ((f32[128,3,128]{2,1,0:T(4,128)}), f32[128,3,128]{2,1,0:T(4,128)S(1)}, u32[]{:S(2)}, u32[]{:S(2)}) async-start(f32[128,3,128]{2,1,0:T(4,128)} %broadcast_in_dim.20), calls=%async_computation.1 | async-start | bytes 524288 | tf_op jit(solution)/shard_map/all_to_all | solution.py:43
  34.3 21.1 %collective-permute-start.1 = (bf16[1,128,128]{2,1,0:T(8,128)(2,1)S(1)}, bf16[1,128,128]{2,1,0:T(8,128)(2,1)S(1)}, u32[]{:S(2)}, u32[]{:S(2)}) collective-permute-start(bf16[1,128,128]{2,1,0:T(8,128)(2,1)S(1)} %get-tuple-element.28), channel_id=1, source_target_pairs={{4,0},{8,4},{12,8},{16,12},{20,16},{24,20},{28,24},{32,28},{36,32}... | collective-permute-start | bytes 98312 | tf_op jit(solution)/shard_map/ppermute | solution.py:22
  41.6 13.8 %collective-permute-start = (bf16[1,128,128]{2,1,0:T(8,128)(2,1)S(1)}, bf16[1,128,128]{2,1,0:T(8,128)(2,1)S(1)}, u32[]{:S(2)}, u32[]{:S(2)}) collective-permute-start(bf16[1,128,128]{2,1,0:T(8,128)(2,1)S(1)} %get-tuple-element.27), channel_id=1, source_target_pairs={{0,4},{4,8},{8,12},{12,16},{16,20},{20,24},{24,28},{28,32},{32,36}... | collective-permute-start | bytes 98312 | tf_op jit(solution)/shard_map/ppermute | solution.py:20
  50.8 18.6 %all-to-all-start = ((bf16[4,480,128]{2,1,0:T(8,128)(2,1)}), bf16[4,480,128]{2,1,0:T(8,128)(2,1)S(1)}, u32[]{:S(2)}, u32[]{:S(2)}) async-start(bf16[4,480,128]{2,1,0:T(8,128)(2,1)} %convert_element_type.66), calls=%async_computation | async-start | bytes 983040 | tf_op jit(solution)/shard_map/all_to_all | solution.py:125

commit v9 on v6

--- a/solution.py
+++ b/solution.py
@@ -105,12 +105,12 @@
     me = lax.axis_index("frm")
     first = me * frames_local
     times = (first + jnp.arange(frames_local)).astype(jnp.float32) / FRAMES
-    envelope = jnp.exp(-damping[:, None] * times[None, :])
+    envelope = jnp.exp(-(damping[:, None] * times[None, :]))
     angle_all = omega[:, None] * times[None, :] + phase[:, None]
-    cosine, sine = lax.optimization_barrier(
-        (envelope * jnp.cos(angle_all), envelope * jnp.sin(angle_all))
+    cosine_all = envelope * jnp.cos(angle_all)
+    cosine, sine, basis = lax.optimization_barrier(
+        (cosine_all, envelope * jnp.sin(angle_all), cosine_all.astype(jnp.bfloat16))
     )
-    basis = cosine.astype(jnp.bfloat16)
 
     rows_local = shapes.shape[0] // IMG_W
     grid = shapes.reshape(rows_local, IMG_W, shapes.shape[1])

time: 81 us -> 80.4 us (level)
    convert_element_type x1, other arithmetic: 0.73 us -> 3.55 us  [body(): cosine_all.astype(jnp.bfloat16)]
    mul x1 -> x0, other arithmetic: 2.69 us -> none  [body(): envelope * jnp.sin(angle_all)]
where the time goes in v9:
time: 80.4 us; the launch traced here: 79.8 us
  starting transfers between devices  49.3 us (61%)
  waiting for transfers between devices  12.8 us (16%)
  other arithmetic  7.38 us (9%)
  Pallas kernels  6.21 us (8%)
  local copies, waits for them, and re-layouts  3.08 us (4%)
  between operations  0.99 us (1%)
    all_to_all x1, starting transfers between devices, sum_over(): lax.all_to_all(jnp.broadcast_to(x[None], (count,) + x.shape), axis, 0, 0,...  19.8 us
    ppermute x3, starting transfers between devices, body(): lax.ppermute(packet, 'frm', [(i, (i + s) % n_frm) for i in range(n_frm)])  10.1 us
    ppermute x3, starting transfers between devices, body(): lax.ppermute(send, 'frm', [(i, (i + s) % n_frm) for i in range(n_frm)])  10.1 us
    ppermute x1, starting transfers between devices, with_halo(): lax.ppermute(head, axis, [((i + 1) % count, i) for i in range(ends)])  7.29 us
    ppermute x3, waiting for transfers between devices, body(): lax.ppermute(send, 'frm', [(i, (i + s) % n_frm) for i in range(n_frm)])  6.55 us
    pallas_call x1, Pallas kernels, fit(): pl.pallas_call(fit_kernel, grid=(n_pixels // tile,), in_specs=[pl.BlockSp...  6.21 us
    ppermute x3, waiting for transfers between devices, body(): lax.ppermute(packet, 'frm', [(i, (i + s) % n_frm) for i in range(n_frm)])  6.21 us
    convert_element_type x1, other arithmetic, body(): cosine_all.astype(jnp.bfloat16)  3.55 us
  transfers between devices with their start and end apart: 9, of which 2 were waited for; matrix products, arithmetic and copies ran while one was open for 1% of the time, Pallas kernels for 0%

profile of v9, /device:TPU:6, one launch (start us, length us, event | category | flops | bytes accessed | tf_op | source)
XLA Modules:
  0.0 79.8 jit_solution(4751954510043391028)
XLA Ops:
  0.7 3.6 %fusion.4 = (bf16[128,1024]{1,0:T(8,128)(2,1)}, f32[128,1024]{1,0:T(8,128)S(1)}, f32[128,1024]{1,0:T(8,128)S(1)}) fusion(f32[128]{0:T(128)} %param.13, f32[128]{0:T(128)} %param.11, f32[1024]{0:T(1024)S(1)} %get-tuple-element.42, f32[128]{0:T(128)} %param.12), kind=kLoop, calls=%fused_computation.25 | loop fusion | flops 917504 | bytes 1316352 | tf_op jit(solution)/shard_map/convert_element_type | solution.py:112
  4.2 0.3 copy.12
  4.5 0.8 %multiply_bitcast_fusion.shapes_t_ref = bf16[128,1920]{1,0:T(8,128)(2,1)} fusion(bf16[1920,128]{0,1:T(8,128)(2,1)S(1)} %copy.12, bf16[1920]{0:T(1024)(128)(2,1)S(1)} %convert_element_type.74), kind=kLoop, calls=%fused_computation.15 | loop fusion | flops 245760 | bytes 986880 | tf_op jit(solution)/shard_map/transpose | solution.py:98
  5.3 6.2 %shard_map.93 = (f32[1920,128]{1,0:T(8,128)}, f32[128,1024]{1,0:T(8,128)}) custom-call(bf16[1920,128]{1,0:T(8,128)(2,1)} %shapes_ref.1, bf16[128,1920]{1,0:T(8,128)(2,1)} %multiply_bitcast_fusion.shapes_t_ref, bf16[1920,1024]{1,0:T(8,128)(2,1)} %video_ref.1, bf16[128,1024]{1,0:T(8,128)(2,1)} %get-tuple-element.10.basis_ref), custom_call_target="tpu_custom_call" | custom-call | flops 1509949440 | bytes 6946816 | tf_op jit(solution)/shard_map/pallas_call | solution.py:79
  11.6 1.5 %multiply_reduce_fusion.2 = (f32[128]{0:T(128)S(1)}, f32[128]{0:T(128)S(1)}, f32[128]{0:T(128)S(1)}) fusion(f32[128,1024]{1,0:T(8,128)S(1)} %get-tuple-element.13, f32[128,1024]{1,0:T(8,128)} %get-tuple-element.12, f32[1024]{0:T(1024)S(1)} %get-tuple-element.43, f32[128,1024]{1,0:T(8,128)S(1)} %get-tuple-element.14), kind=kLoop, calls=%fused_computation.7 | loop fusion | flops 1310336 | bytes 1578496 | tf_op jit(solution)/shard_map/reduce_sum | solution.py:30
  13.1 0.7 broadcast_in_dim.21
  13.8 19.8 %all-to-all-start = ((f32[128,3,128]{2,1,0:T(4,128)}), f32[128,3,128]{2,1,0:T(4,128)S(1)}, u32[]{:S(2)}, u32[]{:S(2)}) async-start(f32[128,3,128]{2,1,0:T(4,128)} %broadcast_in_dim.21), calls=%async_computation | async-start | bytes 524288 | tf_op jit(solution)/shard_map/all_to_all | solution.py:43
  33.7 7.3 %collective-permute-start.4 = (bf16[1,128,128]{2,1,0:T(8,128)(2,1)S(1)}, bf16[1,128,128]{2,1,0:T(8,128)(2,1)S(1)}, u32[]{:S(2)}, u32[]{:S(2)}) collective-permute-start(bf16[1,128,128]{2,1,0:T(8,128)(2,1)S(1)} %get-tuple-element.33), channel_id=1, source_target_pairs={{4,0},{8,4},{12,8},{16,12},{20,16},{24,20},{28,24},{32,28},{36,32}... | collective-permute-start | bytes 98312 | tf_op jit(solution)/shard_map/ppermute | solution.py:22
  41.0 1.9 %collective-permute-start.3 = (bf16[1,128,128]{2,1,0:T(8,128)(2,1)S(1)}, bf16[1,128,128]{2,1,0:T(8,128)(2,1)S(1)}, u32[]{:S(2)}, u32[]{:S(2)}) collective-permute-start(bf16[1,128,128]{2,1,0:T(8,128)(2,1)S(1)} %get-tuple-element.32), channel_id=1, source_target_pairs={{0,4},{4,8},{8,12},{12,16},{16,20},{20,24},{24,28},{28,32},{32,36}... | collective-permute-start | bytes 98312 | tf_op jit(solution)/shard_map/ppermute | solution.py:20
  43.0 0.3 broadcast_multiply_fusion
  43.4 5.2 %collective-permute-start.2 = (bf16[480,128]{1,0:T(8,128)(2,1)S(1)}, bf16[480,128]{1,0:T(8,128)(2,1)S(1)}, u32[]{:S(2)}, u32[]{:S(2)}) collective-permute-start(bf16[480,128]{1,0:T(8,128)(2,1)S(1)} %get-tuple-element.30), channel_id=1, source_target_pairs={{0,3},{1,0},{2,1},{3,2},{4,7},{5,4},{6,5},{7,6},{8,11},{9,8},{10,9... | collective-permute-start | bytes 368648 | tf_op jit(solution)/shard_map/ppermute | solution.py:128
  48.6 1.9 %collective-permute-start.1 = (bf16[480,128]{1,0:T(8,128)(2,1)S(1)}, bf16[480,128]{1,0:T(8,128)(2,1)S(1)}, u32[]{:S(2)}, u32[]{:S(2)}) collective-permute-start(bf16[480,128]{1,0:T(8,128)(2,1)S(1)} %get-tuple-element.31), channel_id=1, source_target_pairs={{0,2},{1,3},{2,0},{3,1},{4,6},{5,7},{6,4},{7,5},{8,10},{9,11},{10,... | collective-permute-start | bytes 368648 | tf_op jit(solution)/shard_map/ppermute | solution.py:128
  50.5 3.0 %collective-permute-start = (bf16[480,128]{1,0:T(8,128)(2,1)S(1)}, bf16[480,128]{1,0:T(8,128)(2,1)S(1)}, u32[]{:S(2)}, u32[]{:S(2)}) collective-permute-start(bf16[480,128]{1,0:T(8,128)(2,1)S(1)} %get-tuple-element.29), channel_id=1, source_target_pairs={{0,1},{1,2},{2,3},{3,0},{4,5},{5,6},{6,7},{7,4},{8,9},{9,10},{10,1... | collective-permute-start | bytes 368648 | tf_op jit(solution)/shard_map/ppermute | solution.py:128
  53.8 0.2 fusion
  54.1 6.5 %collective-permute-done.1 = bf16[480,128]{1,0:T(8,128)(2,1)S(1)} collective-permute-done((bf16[480,128]{1,0:T(8,128)(2,1)S(1)}, bf16[480,128]{1,0:T(8,128)(2,1)S(1)}, u32[]{:S(2)}, u32[]{:S(2)}) %collective-permute-start.1) | collective-permute-done | bytes 122912 | tf_op jit(solution)/shard_map/ppermute | solution.py:128
  60.7 0.1 reduce_sum.39
  60.9 0.1 maximum_maximum_fusion
  61.0 3.9 %collective-permute-start.7 = (bf16[496,128]{1,0:T(8,128)(2,1)S(1)}, bf16[496,128]{1,0:T(8,128)(2,1)S(1)}, u32[]{:S(2)}, u32[]{:S(2)}) collective-permute-start(bf16[496,128]{1,0:T(8,128)(2,1)S(1)} %maximum_maximum_fusion), channel_id=1, source_target_pairs={{0,3},{1,0},{2,1},{3,2},{4,7},{5,4},{6,5},{7,6},{8,11},{9,8},{10,9... | collective-permute-start | bytes 380936 | tf_op jit(solution)/shard_map/ppermute | solution.py:147
  65.0 2.3 %collective-permute-start.6 = (bf16[496,128]{1,0:T(8,128)(2,1)S(1)}, bf16[496,128]{1,0:T(8,128)(2,1)S(1)}, u32[]{:S(2)}, u32[]{:S(2)}) collective-permute-start(bf16[496,128]{1,0:T(8,128)(2,1)S(1)} %maximum_maximum_fusion), channel_id=1, source_target_pairs={{0,2},{1,3},{2,0},{3,1},{4,6},{5,7},{6,4},{7,5},{8,10},{9,11},{10,... | collective-permute-start | bytes 380936 | tf_op jit(solution)/shard_map/ppermute | solution.py:147
  67.3 3.9 %collective-permute-start.5 = (bf16[496,128]{1,0:T(8,128)(2,1)S(1)}, bf16[496,128]{1,0:T(8,128)(2,1)S(1)}, u32[]{:S(2)}, u32[]{:S(2)}) collective-permute-start(bf16[496,128]{1,0:T(8,128)(2,1)S(1)} %maximum_maximum_fusion), channel_id=1, source_target_pairs={{0,1},{1,2},{2,3},{3,0},{4,5},{5,6},{6,7},{7,4},{8,9},{9,10},{10,1... | collective-permute-start | bytes 380936 | tf_op jit(solution)/shard_map/ppermute | solution.py:147
  71.4 6.2 %collective-permute-done.6 = bf16[496,128]{1,0:T(8,128)(2,1)S(1)} collective-permute-done((bf16[496,128]{1,0:T(8,128)(2,1)S(1)}, bf16[496,128]{1,0:T(8,128)(2,1)S(1)}, u32[]{:S(2)}, u32[]{:S(2)}) %collective-permute-start.6) | collective-permute-done | bytes 127008 | tf_op jit(solution)/shard_map/ppermute | solution.py:147
  77.6 0.6 gather_fusion
  78.4 0.8 %slice.80 = bf16[4,480,128]{2,1,0:T(8,128)(2,1)} slice(bf16[4,496,128]{2,1,0:T(8,128)(2,1)S(1)} %broadcast_select_fusion), slice={[0:4], [0:480], [0:128]} | slice | bytes 983040 | tf_op jit(solution)/shard_map/slice | solution.py:150
  79.2 0.5 slice_bitcast_fusion.2
  (35 shorter events, 0.8 us)
Async XLA Ops:
  0.6 3.6 %copy-start = (bf16[1920,128]{1,0:T(8,128)(2,1)S(1)}, bf16[1920,128]{1,0:T(8,128)(2,1)}, u32[]{:S(2)}) copy-start(bf16[1920,128]{1,0:T(8,128)(2,1)} %shapes_ref.1) | copy-start | bytes 1474564
  0.7 3.8 %copy-start.3 = (s32[1920]{0:T(1024)S(1)}, s32[1920]{0:T(1024)}, u32[]{:S(2)}) copy-start(s32[1920]{0:T(1024)} %param.10) | copy-start | bytes 23044
  11.6 22.1 %copy-start.1 = (bf16[1920,128]{1,0:T(8,128)(2,1)S(1)}, bf16[1920,128]{1,0:T(8,128)(2,1)}, u32[]{:S(2)}) copy-start(bf16[1920,128]{1,0:T(8,128)(2,1)} %shapes_ref.1) | copy-start | bytes 1474564
  11.6 31.4 %copy-start.2 = (f32[1920,128]{1,0:T(8,128)S(1)}, f32[1920,128]{1,0:T(8,128)}, u32[]{:S(2)}) copy-start(f32[1920,128]{1,0:T(8,128)} %get-tuple-element.11) | copy-start | bytes 2949124
  13.8 46.9 %all-to-all-start = ((f32[128,3,128]{2,1,0:T(4,128)}), f32[128,3,128]{2,1,0:T(4,128)S(1)}, u32[]{:S(2)}, u32[]{:S(2)}) async-start(f32[128,3,128]{2,1,0:T(4,128)} %broadcast_in_dim.21), calls=%async_computation | async-start | bytes 524288 | tf_op jit(solution)/shard_map/all_to_all | solution.py:43
  33.7 20.0 %collective-permute-start.4 = (bf16[1,128,128]{2,1,0:T(8,128)(2,1)S(1)}, bf16[1,128,128]{2,1,0:T(8,128)(2,1)S(1)}, u32[]{:S(2)}, u32[]{:S(2)}) collective-permute-start(bf16[1,128,128]{2,1,0:T(8,128)(2,1)S(1)} %get-tuple-element.33), channel_id=1, source_target_pairs={{4,0},{8,4},{12,8},{16,12},{20,16},{24,20},{28,24},{32,28},{36,32}... | collective-permute-start | bytes 98312 | tf_op jit(solution)/shard_map/ppermute | solution.py:22
  41.0 12.8 %collective-permute-start.3 = (bf16[1,128,128]{2,1,0:T(8,128)(2,1)S(1)}, bf16[1,128,128]{2,1,0:T(8,128)(2,1)S(1)}, u32[]{:S(2)}, u32[]{:S(2)}) collective-permute-start(bf16[1,128,128]{2,1,0:T(8,128)(2,1)S(1)} %get-tuple-element.32), channel_id=1, source_target_pairs={{0,4},{4,8},{8,12},{12,16},{16,20},{20,24},{24,28},{28,32},{32,36}... | collective-permute-start | bytes 98312 | tf_op jit(solution)/shard_map/ppermute | solution.py:20
  43.4 10.7 %collective-permute-start.2 = (bf16[480,128]{1,0:T(8,128)(2,1)S(1)}, bf16[480,128]{1,0:T(8,128)(2,1)S(1)}, u32[]{:S(2)}, u32[]{:S(2)}) collective-permute-start(bf16[480,128]{1,0:T(8,128)(2,1)S(1)} %get-tuple-element.30), channel_id=1, source_target_pairs={{0,3},{1,0},{2,1},{3,2},{4,7},{5,4},{6,5},{7,6},{8,11},{9,8},{10,9... | collective-permute-start | bytes 368648 | tf_op jit(solution)/shard_map/ppermute | solution.py:128
  48.6 12.0 %collective-permute-start.1 = (bf16[480,128]{1,0:T(8,128)(2,1)S(1)}, bf16[480,128]{1,0:T(8,128)(2,1)S(1)}, u32[]{:S(2)}, u32[]{:S(2)}) collective-permute-start(bf16[480,128]{1,0:T(8,128)(2,1)S(1)} %get-tuple-element.31), channel_id=1, source_target_pairs={{0,2},{1,3},{2,0},{3,1},{4,6},{5,7},{6,4},{7,5},{8,10},{9,11},{10,... | collective-permute-start | bytes 368648 | tf_op jit(solution)/shard_map/ppermute | solution.py:128
  50.5 10.1 %collective-permute-start = (bf16[480,128]{1,0:T(8,128)(2,1)S(1)}, bf16[480,128]{1,0:T(8,128)(2,1)S(1)}, u32[]{:S(2)}, u32[]{:S(2)}) collective-permute-start(bf16[480,128]{1,0:T(8,128)(2,1)S(1)} %get-tuple-element.29), channel_id=1, source_target_pairs={{0,1},{1,2},{2,3},{3,0},{4,5},{5,6},{6,7},{7,4},{8,9},{9,10},{10,1... | collective-permute-start | bytes 368648 | tf_op jit(solution)/shard_map/ppermute | solution.py:128
  61.0 10.3 %collective-permute-start.7 = (bf16[496,128]{1,0:T(8,128)(2,1)S(1)}, bf16[496,128]{1,0:T(8,128)(2,1)S(1)}, u32[]{:S(2)}, u32[]{:S(2)}) collective-permute-start(bf16[496,128]{1,0:T(8,128)(2,1)S(1)} %maximum_maximum_fusion), channel_id=1, source_target_pairs={{0,3},{1,0},{2,1},{3,2},{4,7},{5,4},{6,5},{7,6},{8,11},{9,8},{10,9... | collective-permute-start | bytes 380936 | tf_op jit(solution)/shard_map/ppermute | solution.py:147
  65.0 12.6 %collective-permute-start.6 = (bf16[496,128]{1,0:T(8,128)(2,1)S(1)}, bf16[496,128]{1,0:T(8,128)(2,1)S(1)}, u32[]{:S(2)}, u32[]{:S(2)}) collective-permute-start(bf16[496,128]{1,0:T(8,128)(2,1)S(1)} %maximum_maximum_fusion), channel_id=1, source_target_pairs={{0,2},{1,3},{2,0},{3,1},{4,6},{5,7},{6,4},{7,5},{8,10},{9,11},{10,... | collective-permute-start | bytes 380936 | tf_op jit(solution)/shard_map/ppermute | solution.py:147
  67.3 10.3 %collective-permute-start.5 = (bf16[496,128]{1,0:T(8,128)(2,1)S(1)}, bf16[496,128]{1,0:T(8,128)(2,1)S(1)}, u32[]{:S(2)}, u32[]{:S(2)}) collective-permute-start(bf16[496,128]{1,0:T(8,128)(2,1)S(1)} %maximum_maximum_fusion), channel_id=1, source_target_pairs={{0,1},{1,2},{2,3},{3,0},{4,5},{5,6},{6,7},{7,4},{8,9},{9,10},{10,1... | collective-permute-start | bytes 380936 | tf_op jit(solution)/shard_map/ppermute | solution.py:147
